TPU v7x, 32 devices: a whole 2x2x4 slice. The times are simulated.
32 devices in a mesh: leaf: 16 (over z, x, core), site: 2 (over y).
Axes of the slice: x: 2, y: 2, z: 4, core: 2. Of those that a mesh axis runs over, the one named last changes fastest.
Arguments:
- tips: float32 [128, 64, 256], P('leaf', None, 'site'), as said below
- parents: int32 [224], P('leaf'), may hold values from 8 to 14, as said below
- branch_lengths: float32 [224], P('leaf'), may hold values from 0.02 to 0.6
- top_parents: int32 [30], replicated, may hold values from 16 to 30, as said below
- top_lengths: float32 [30], replicated, may hold values from 0.02 to 0.6
- weights: int32 [256], P('site'), may hold values from 1 to 16
- eig_vectors: float32 [64, 64], replicated, as said below
- eig_inverse: float32 [64, 64], replicated, as said below
- eig_values: float32 [64], replicated, as said below
- labeled_rates: float32 [64, 64], replicated, as said below
- root_freq: float32 [64], replicated, as said below
Outputs:
- local_counts: float32 [224], P('leaf')
- top_counts: float32 [30], replicated
- site_loglik: float32 [256], P('site')
Inputs may be any that keep to these rules, and one draw needn't show every extreme that they name: `parents`: within each block of 14 entries (one subtree) the entries form a binary tree: every entry is larger than its own position in the block, every internal node 8 to 14 is named by exactly two entries. `top_parents`: A binary tree over the subtrees: every entry is larger than its own position, every node 16 to 2 * 16 - 2 is named by exactly two entries. `tips`: Positive. eig_vectors diag(eig_values) eig_inverse is a reversible rate matrix Q on the first 61 states with stationary frequencies root_freq and mean rate 1, and eig_inverse eig_vectors is the identity; rows, columns and eigenvalues past 61 are those of the identity and 0. `eig_inverse`: the inverse of eig_vectors, as above. `eig_values`: eigenvalues of Q, at most 0. `labeled_rates`: Off-diagonal rates of Q for a symmetric set of counted state pairs, 0 elsewhere. `root_freq`: positive on the first 61 states, 0 past them, summing to 1.
All inputs are finite; a program needn't handle non-finite values.
Results may differ from a plain program's by a relative error of at most 0.0003.
Values sent between devices are 32-bit elements; how exact they have to be, the bound alone decides.
No kernel may reach another device: no remote copies, remote signals or barrier semaphores. Data moves between devices by JAX's collectives and lax.ppermute only.
A program may use at most 64 MiB of HBM per device.

v0:
```python
import jax
import jax.numpy as jnp
from jax import lax
from jax.sharding import PartitionSpec as P

CODONS = 61


PRECISE = lax.Precision.HIGHEST


def propagate(eig_vectors, eig_inverse, eig_values, branch, partial_value):
    projected = jnp.dot(eig_inverse, partial_value, precision=PRECISE)
    damping = jnp.exp(eig_values * branch)
    return jnp.dot(eig_vectors, damping[:, None] * projected, precision=PRECISE)


def integrals(eig_values, branch):
    spread = (eig_values[:, None] - eig_values[None, :]) * branch
    near_zero = jnp.abs(spread) < 0.0001
    divisor = jnp.where(near_zero, jnp.ones_like(spread), spread)
    growth = jnp.where(
        near_zero, 1.0 + spread / 2.0 + spread * spread / 6.0, jnp.expm1(spread) / divisor
    )
    return branch * jnp.exp(eig_values[None, :] * branch) * growth


def climb_tree(leaf_rows, tree_links, lengths, eig_vectors, eig_inverse, eig_values):
    leaf_count = leaf_rows.shape[0]
    edge_count = tree_links.shape[0]
    inside = jnp.concatenate(
        [
            leaf_rows,
            jnp.ones((leaf_count - 1, leaf_rows.shape[1], leaf_rows.shape[2]), jnp.float32),
        ],
        axis=0,
    )

    def finish(inside, log_scale, position):
        node_row = lax.dynamic_index_in_dim(inside, position, 0, keepdims=False)
        biggest = jnp.max(node_row, axis=0)
        internal = position >= leaf_count
        node_row = jnp.where(internal, node_row / biggest, node_row)
        log_scale = log_scale + jnp.where(internal, jnp.log(biggest), jnp.zeros_like(biggest))
        return (lax.dynamic_update_index_in_dim(inside, node_row, position, 0), log_scale, node_row)

    def climb_visit(position, state_pair):
        inside, log_scale = state_pair
        inside, log_scale, node_row = finish(inside, log_scale, position)
        message = propagate(eig_vectors, eig_inverse, eig_values, lengths[position], node_row)
        parent_node = tree_links[position]
        target = lax.dynamic_index_in_dim(inside, parent_node, 0, keepdims=False) * message
        return (lax.dynamic_update_index_in_dim(inside, target, parent_node, 0), log_scale)

    log_scale = jnp.zeros((leaf_rows.shape[2],), jnp.float32)
    inside, log_scale = lax.fori_loop(0, edge_count, climb_visit, (inside, log_scale))
    inside, log_scale, _ = finish(inside, log_scale, edge_count)
    return (inside, log_scale)


def descend(
    inside, tree_links, lengths, root_out, weight, eig_vectors, eig_inverse, eig_values, count_basis
):
    node_count = inside.shape[0]
    edge_count = node_count - 1
    labels = jnp.arange(node_count, dtype=jnp.int32)
    edges = jnp.arange(edge_count, dtype=jnp.int32)
    member = tree_links[None, :] == labels[:, None]
    child_sum = jnp.sum(jnp.where(member, edges[None, :], 0), axis=1)
    sibling = child_sum[tree_links] - edges
    outside = jnp.zeros_like(inside).at[node_count - 1].set(root_out)

    def descend_visit(counter, state_pair):
        outside, totals = state_pair
        position = edge_count - 1 - counter
        parent_node = tree_links[position]
        beside = sibling[position]
        branch = lengths[position]
        partner = propagate(
            eig_vectors,
            eig_inverse,
            eig_values,
            lengths[beside],
            lax.dynamic_index_in_dim(inside, beside, 0, keepdims=False),
        )
        arriving = lax.dynamic_index_in_dim(outside, parent_node, 0, keepdims=False) * partner
        weighted = jnp.dot(eig_vectors.T, arriving, precision=PRECISE)
        projected = jnp.dot(
            eig_inverse,
            lax.dynamic_index_in_dim(inside, position, 0, keepdims=False),
            precision=PRECISE,
        )
        damping = jnp.exp(eig_values * branch)
        denominator = jnp.sum(weighted * damping[:, None] * projected, axis=0)
        mixed_rows = jnp.dot(
            count_basis * integrals(eig_values, branch), projected, precision=PRECISE
        )
        numerator = jnp.sum(weighted * mixed_rows, axis=0)
        pattern_total = jnp.sum(weight * numerator / denominator)
        outward = jnp.dot(eig_inverse.T, damping[:, None] * weighted, precision=PRECISE)
        outward = outward / jnp.max(outward, axis=0)
        outside = lax.dynamic_update_index_in_dim(outside, outward, position, 0)
        return (outside, totals.at[position].set(pattern_total))

    totals = jnp.zeros((edge_count,), jnp.float32)
    return lax.fori_loop(0, edge_count, descend_visit, (outside, totals))


def batch_propagate(eig_vectors, eig_inverse, eig_values, lengths, partials):
    projected = jnp.einsum("ks,esc->ekc", eig_inverse, partials, precision=PRECISE)
    damping = jnp.exp(eig_values[None, :] * lengths[:, None])
    return jnp.einsum(
        "sk,ekc->esc", eig_vectors, damping[:, :, None] * projected, precision=PRECISE
    )


def level_tree(
    leaf_rows,
    tree_links,
    lengths,
    root_out,
    weight,
    eig_vectors,
    eig_inverse,
    eig_values,
    count_basis,
):
    leaf_count = leaf_rows.shape[0]
    edge_count = tree_links.shape[0]
    node_count = edge_count + 1
    labels = jnp.arange(node_count, dtype=jnp.int32)
    edges = jnp.arange(edge_count, dtype=jnp.int32)
    member = tree_links[None, :] == labels[:, None]
    left_child = jnp.min(jnp.where(member, edges[None, :], edge_count), axis=1)[leaf_count:]
    right_child = jnp.max(jnp.where(member, edges[None, :], -1), axis=1)[leaf_count:]
    child_sum = jnp.sum(jnp.where(member, edges[None, :], 0), axis=1)
    sibling = child_sum[tree_links] - edges

    def raise_height(position, heights):
        parent_node = tree_links[position]
        return heights.at[parent_node].set(jnp.maximum(heights[parent_node], heights[position] + 1))

    heights = lax.fori_loop(0, edge_count, raise_height, jnp.zeros((node_count,), jnp.int32))

    def deepen(counter, depths):
        position = edge_count - 1 - counter
        return depths.at[position].set(depths[tree_links[position]] + 1)

    depths = lax.fori_loop(0, edge_count, deepen, jnp.zeros((node_count,), jnp.int32))
    inner_heights = heights[leaf_count:]
    edge_depths = depths[:edge_count]
    inside = jnp.concatenate(
        [
            leaf_rows,
            jnp.ones((leaf_count - 1, leaf_rows.shape[1], leaf_rows.shape[2]), jnp.float32),
        ],
        axis=0,
    )
    log_scale = jnp.zeros((leaf_rows.shape[2],), jnp.float32)

    def climb_level(level, state_pair):
        inside, log_scale = state_pair
        message = batch_propagate(
            eig_vectors, eig_inverse, eig_values, lengths, inside[:edge_count]
        )
        product = message[left_child] * message[right_child]
        biggest = jnp.max(product, axis=1)
        chosen = inner_heights == level
        normed = product / biggest[:, None, :]
        inner = jnp.where(chosen[:, None, None], normed, inside[leaf_count:])
        log_scale = log_scale + jnp.sum(jnp.where(chosen[:, None], jnp.log(biggest), 0.0), axis=0)
        return (jnp.concatenate([inside[:leaf_count], inner], axis=0), log_scale)

    inside, log_scale = lax.fori_loop(
        1, heights[node_count - 1] + 1, climb_level, (inside, log_scale)
    )
    message = batch_propagate(eig_vectors, eig_inverse, eig_values, lengths, inside[:edge_count])
    partner = message[sibling]
    damping = jnp.exp(eig_values[None, :] * lengths[:, None])
    outside = jnp.zeros_like(inside).at[node_count - 1].set(root_out)

    def arrive(outside):
        arriving = outside[tree_links] * partner
        return jnp.einsum("sk,esc->ekc", eig_vectors, arriving, precision=PRECISE)

    def descend_level(level, outside):
        weighted = arrive(outside)
        outward = jnp.einsum(
            "ks,ekc->esc", eig_inverse, damping[:, :, None] * weighted, precision=PRECISE
        )
        outward = outward / jnp.max(outward, axis=1)[:, None, :]
        chosen = edge_depths == level
        edge_rows = jnp.where(chosen[:, None, None], outward, outside[:edge_count])
        return jnp.concatenate([edge_rows, outside[edge_count:]], axis=0)

    outside = lax.fori_loop(1, jnp.max(depths) + 1, descend_level, outside)
    weighted = arrive(outside)
    projected = jnp.einsum("ks,esc->ekc", eig_inverse, inside[:edge_count], precision=PRECISE)
    denominator = jnp.sum(weighted * damping[:, :, None] * projected, axis=1)
    basis_rows = count_basis[None] * jax.vmap(lambda branch: integrals(eig_values, branch))(lengths)
    mixed_rows = jnp.einsum("ekl,elc->ekc", basis_rows, projected, precision=PRECISE)
    numerator = jnp.sum(weighted * mixed_rows, axis=1)
    totals = jnp.sum(weight[None, :] * numerator / denominator, axis=1)
    return (inside[node_count - 1], log_scale, outside, totals)


def joining_tree(
    root_rows,
    top_parents,
    top_lengths,
    root_start,
    weight,
    eig_vectors,
    eig_inverse,
    eig_values,
    count_basis,
):
    return level_tree(
        root_rows,
        top_parents,
        top_lengths,
        root_start,
        weight,
        eig_vectors,
        eig_inverse,
        eig_values,
        count_basis,
    )


def on_device(
    tips,
    parents,
    branch_lengths,
    top_parents,
    top_lengths,
    weights,
    eig_vectors,
    eig_inverse,
    eig_values,
    labeled_rates,
    root_freq,
):
    states = tips.shape[1]
    columns = tips.shape[2]
    codon_mask = (jnp.arange(states) < CODONS).astype(jnp.float32)
    count_basis = jnp.dot(
        jnp.dot(eig_inverse, labeled_rates, precision=PRECISE), eig_vectors, precision=PRECISE
    )
    inside, local_logs = climb_tree(
        tips * codon_mask[None, :, None],
        parents,
        branch_lengths,
        eig_vectors,
        eig_inverse,
        eig_values,
    )
    subtree_root = inside[-1]
    groups = lax.axis_size("leaf")
    member_index = lax.axis_index("leaf")
    taxon_count = tips.shape[0] * groups
    weight = weights.astype(jnp.float32)
    share_width = columns // groups
    root_rows, root_logs = (
        lax.all_to_all(subtree_root[None], "leaf", split_axis=2, concat_axis=0, tiled=True),
        lax.all_to_all(local_logs[None, None], "leaf", split_axis=2, concat_axis=0, tiled=True),
    )
    weight_share = lax.dynamic_slice_in_dim(weight, member_index * share_width, share_width)
    root_start = jnp.broadcast_to(root_freq[:, None], (states, share_width))
    top_root, top_logs, top_outside, top_totals = joining_tree(
        root_rows,
        top_parents,
        top_lengths,
        root_start,
        weight_share,
        eig_vectors,
        eig_inverse,
        eig_values,
        count_basis,
    )
    likelihood = jnp.sum(root_freq[:, None] * top_root, axis=0)
    part_loglik = (jnp.log(likelihood) + top_logs + jnp.sum(root_logs[:, 0], axis=0)) / taxon_count
    loglik_rows = jnp.broadcast_to(part_loglik[None, None, :], (groups, 1, share_width))
    returned, returned_loglik = (
        lax.all_to_all(top_outside[:groups], "leaf", split_axis=0, concat_axis=2, tiled=True),
        lax.all_to_all(loglik_rows, "leaf", split_axis=0, concat_axis=2, tiled=True),
    )
    site_loglik = returned_loglik[0, 0]
    _, local_totals = descend(
        inside,
        parents,
        branch_lengths,
        returned[0],
        weight,
        eig_vectors,
        eig_inverse,
        eig_values,
        count_basis,
    )
    local_sum, weight_total = lax.psum((local_totals, jnp.sum(weight)), "site")
    top_sum = lax.psum(top_totals, ("leaf", "site"))
    return (local_sum / weight_total, top_sum / weight_total, site_loglik)


def solution(mesh):
    placed = (
        P("leaf", None, "site"),
        P("leaf"),
        P("leaf"),
        P(),
        P(),
        P("site"),
        P(),
        P(),
        P(),
        P(),
        P(),
    )
    return jax.shard_map(
        on_device,
        mesh=mesh,
        in_specs=placed,
        out_specs=(P("leaf"), P(), P("site")),
        check_vma=False,
    )
```

profile of v0, /device:TPU:0, one launch (start us, length us, event | category | flops | bytes accessed | tf_op | source)
XLA Modules:
  0.0 491.0 jit_solution(9191342012481013764)
XLA Ops:
  0.7 1.0 broadcast_multiply_fusion.1
  2.5 59.4 %while.94 = (s32[]{:T(128)}, f32[15,64,128]{2,1,0:T(8,128)S(1)}, f32[128]{0:T(128)S(1)}, s32[14]{0:T(128)S(1)}, f32[14]{0:T(128)S(1)}, /*index=5*/f32[64]{0:T(12...) while((s32[]{:T(128)}, f32[15,64,128]{2,1,0:T(8,128)S(1)}, ...), condition=%wide.region_5.6_spmd.clone, body=%wide.region_3.5_spmd.clone.sunk | while | flops 12640583 | bytes 397541 | solution.py:56
  62.6 7.4 %all-to-all-start.2 = ((f32[1,1,128]{1,0,2:T(1,128)}), f32[1,1,128]{1,0,2:T(1,128)S(1)}, u32[]{:S(2)}, u32[]{:S(2)}) async-start(f32[1,1,128]{1,0,2:T(1,128)} %copy.81), calls=%async_computation.2 | async-start | bytes 131072 | tf_op jit(solution)/shard_map/all_to_all | solution.py:266
  70.8 78.7 %while.90 = (s32[]{:T(128)}, s32[31]{0:T(128)S(1)}, s32[30]{0:T(128)S(1)}, s32[]{:T(128)}, s32[]{:T(128)}, /*index=5*/s32[]{:T(128)}, s32[]{:T(128)}) while((s32[]{:T(128)}, s32[31]{0:T(128)S(1)}, s32[30]{0:T(128)S(1)}, s32[]{:T(128)}, s32[]{:T(128)}, /*index=5*/s32[]{:T(128)}, s32[]{:T(128)}) %tuple.247), condition=%wide.region_8.9_spmd, body=%wide.region_7.8_spmd.sunk | while | flops 11 | bytes 1309 | solution.py:143
  151.0 78.5 %while.89 = (s32[]{:T(128)}, s32[31]{0:T(128)S(1)}, s32[30]{0:T(128)S(1)}, s32[]{:T(128)}, s32[]{:T(128)}, /*index=5*/s32[]{:T(128)}, s32[]{:T(128)}, s32[]{:T(128)}, s32[]{:T(128)}, s32[]{:T(128)}) while((s32[]{:T(128)}, s32[31]{0:T(128)S(1)}, s32[30]{0:T(128)S(1)}, s32[]{:T(128)}, s32[]{:T(128)}, /*index=5*/s32[]{:T(128)}, s32[]{:T(128)}, ...), condition=%wide.region_1.0_spmd, body=%wide.region_0.1_spmd.sunk | while | flops 16 | bytes 1404 | solution.py:149
  236.3 6.0 %all-to-all-start = ((f32[16,1,512]{2,1,0:T(1,128)}), f32[16,1,512]{2,1,0:T(1,128)S(1)}, u32[]{:S(2)}, u32[]{:S(2)}) async-start(f32[16,1,512]{2,1,0:T(1,128)} %reshape.602), calls=%async_computation | async-start | bytes 65536 | tf_op jit(solution)/shard_map/all_to_all | solution.py:265
  244.2 4.8 all-to-all-done
  249.9 14.1 %while.91 = (s32[]{:T(128)}, f32[31,64,8]{1,0,2:T(8,128)S(1)}, f32[8]{0:T(128)S(1)}, s32[]{:T(128)}, s32[15]{0:T(128)S(1)}, /*index=5*/f32[64]{0:T(128)S(1)}, f3...) while((s32[]{:T(128)}, f32[31,64,8]{1,0,2:T(8,128)S(1)}, ...), condition=%wide.region_14.15_spmd, body=%wide.region_11.14_spmd.sunk | while | flops 23659104 | bytes 1117794 | solution.py:174
  265.3 9.2 %while.93 = (s32[]{:T(128)}, f32[31,64,8]{1,0,2:T(8,128)S(1)}, s32[]{:T(128)}, s32[30]{0:T(128)S(1)}, s32[30]{0:T(128)S(1)}, /*index=5*/f32[30,64,8]{1,2,0:T(8,1...) while((s32[]{:T(128)}, f32[31,64,8]{1,0,2:T(8,128)S(1)}, ...), condition=%wide.region_18.19_spmd.clone, body=%wide.region_16.18_spmd.clone.sunk | while | flops 23673640 | bytes 1319527 | solution.py:196
  276.0 3.4 all-to-all-start.3
  279.5 2.4 fusion.70
  282.9 2.9 all-to-all-done.3
  285.8 3.5 all-to-all-start.1
  289.4 40.6 %psum.23 = f32[30]{0:T(128)S(1)} all-reduce(f32[30]{0:T(128)S(1)} %divide_reduce_fusion), channel_id=1, replica_groups=mesh['leaf'=16,'site'=2] {'leaf','site'}, use_global_device_ids=true, to_apply=%region_32.33 | all-reduce | flops 30 | bytes 240 | tf_op jit(solution)/shard_map/psum | solution.py:301
  332.8 150.1 %while.92 = (s32[]{:T(128)}, f32[15,64,128]{2,1,0:T(8,128)S(1)}, f32[14]{0:T(128)S(1)}, f32[14]{0:T(128)S(1)}, f32[64]{0:T(128)S(1)}, /*index=5*/s32[14]{0:T(128...) while((s32[]{:T(128)}, f32[15,64,128]{2,1,0:T(8,128)S(1)}, ...), condition=%wide.region_25.26_spmd, body=%wide.region_20.25_spmd.sunk | while | flops 37888208 | bytes 662327 | solution.py:106
  339.1 1.2 broadcast_multiply_fusion.4
  349.8 1.2 broadcast_multiply_fusion.4
  360.5 1.2 broadcast_multiply_fusion.4
  371.2 1.2 broadcast_multiply_fusion.4
  382.0 1.2 broadcast_multiply_fusion.4
  392.7 1.2 broadcast_multiply_fusion.4
  403.4 1.2 broadcast_multiply_fusion.4
  414.1 1.2 broadcast_multiply_fusion.4
  424.9 1.2 broadcast_multiply_fusion.4
  435.6 1.2 broadcast_multiply_fusion.4
  446.3 1.2 broadcast_multiply_fusion.4
  457.0 1.2 broadcast_multiply_fusion.4
  467.8 1.2 broadcast_multiply_fusion.4
  478.5 1.2 broadcast_multiply_fusion.4
  482.9 5.7 %all-reduce.4 = (f32[14]{0:T(128)S(1)}, f32[]{:T(128)}) all-reduce(f32[14]{0:T(128)S(1)} %get-tuple-element.785, f32[]{:T(128)} %convert_reduce_fusion), channel_id=1, replica_groups=mesh['leaf'=16,'site'=2] {'site'}, use_global_device_ids=true, to_apply=%region_26.27 | all-reduce | flops 15 | bytes 120 | tf_op jit(solution)/shard_map/psum | solution.py:300
  488.7 1.1 broadcast_divide_fusion.1
  489.8 1.1 broadcast_divide_fusion
  (686 shorter events, 188.8 us)
Async XLA Ops:
  0.6 231.6 %copy-start = (f32[64,64]{1,0:T(8,128)S(1)}, f32[64,64]{1,0:T(8,128)}, u32[]{:S(2)}) copy-start(f32[64,64]{1,0:T(8,128)} %param.42) | copy-start | bytes 49156
  1.7 0.8 copy-start.1
  1.7 0.8 copy-start.2
  1.7 0.8 copy-start.3
  1.7 0.7 copy-start.5
  1.8 0.7 copy-start.9
  62.6 173.7 %all-to-all-start.2 = ((f32[1,1,128]{1,0,2:T(1,128)}), f32[1,1,128]{1,0,2:T(1,128)S(1)}, u32[]{:S(2)}, u32[]{:S(2)}) async-start(f32[1,1,128]{1,0,2:T(1,128)} %copy.81), calls=%async_computation.2 | async-start | bytes 131072 | tf_op jit(solution)/shard_map/all_to_all | solution.py:266
  70.2 0.7 copy-start.7
  150.4 0.7 copy-start.8
  232.5 0.7 copy-start.4
  235.7 0.7 copy-start.6
  236.3 12.7 %all-to-all-start = ((f32[16,1,512]{2,1,0:T(1,128)}), f32[16,1,512]{2,1,0:T(1,128)S(1)}, u32[]{:S(2)}, u32[]{:S(2)}) async-start(f32[16,1,512]{2,1,0:T(1,128)} %reshape.602), calls=%async_computation | async-start | bytes 65536 | tf_op jit(solution)/shard_map/all_to_all | solution.py:265
  276.0 9.8 %all-to-all-start.3 = ((f32[16,1,8]{2,1,0:T(1,128)}), f32[16,1,8]{2,1,0:T(1,128)S(1)}, u32[]{:S(2)}, u32[]{:S(2)}) async-start(f32[16,1,8]{2,1,0:T(1,128)} %broadcast_in_dim.203), calls=%async_computation.3 | async-start | bytes 16384 | tf_op jit(solution)/shard_map/all_to_all | solution.py:286
  285.8 45.9 %all-to-all-start.1 = ((f32[16,1,512]{2,1,0:T(1,128)}), f32[16,1,512]{2,1,0:T(1,128)S(1)}, u32[]{:S(2)}, u32[]{:S(2)}) async-start(f32[16,1,512]{2,1,0:T(1,128)} %reshape.604), calls=%async_computation.1 | async-start | bytes 65536 | tf_op jit(solution)/shard_map/all_to_all | solution.py:285
where the time goes:
time: 497 us; the launch traced here: 491 us
  loops' own time  203 us (41%)
  local copies, waits for them, and re-layouts  101 us (20%)
  other arithmetic  69.6 us (14%)
  blocking collectives  46.3 us (9%)
  matrix products  40.3 us (8%)
  starting transfers between devices  20.3 us (4%)
  waiting for transfers between devices  7.75 us (2%)
    another operation x1, loops' own time, descend(): return lax.fori_loop(0, edge_count, descend_visit, (outside, totals))  63.8 us
    another operation x1, loops' own time, level_tree(): lax.fori_loop(0, edge_count, raise_height, jnp.zeros((node_count,), jnp.i...  55 us
    another operation x1, loops' own time, level_tree(): lax.fori_loop(0, edge_count, deepen, jnp.zeros((node_count,), jnp.int32))  54.9 us
    psum x1, blocking collectives, on_device(): top_sum = lax.psum(top_totals, ('leaf', 'site'))  40.6 us
    another operation x1, loops' own time, climb_tree(): lax.fori_loop(0, edge_count, climb_visit, (inside, log_scale))  28 us
    dynamic_slice x30, local copies, waits for them, and re-layouts, deepen(): return depths.at[position].set(depths[tree_links[position]] + 1)  18.4 us
    dynamic_slice x30, local copies, waits for them, and re-layouts, raise_height(): parent_node = tree_links[position]  18.4 us
    mul x15, other arithmetic, integrals(): return branch * jnp.exp(eig_values[None, :] * branch) * growth  16.8 us
  transfers between devices with their start and end apart: 4, of which 2 were waited for; matrix products, arithmetic and copies ran while one was open for 12% of the time, Pallas kernels for 0%

commit v1 on v0

v1 whole, which is shorter than its diff:
```python
import functools

import jax
import jax.numpy as jnp
from jax import lax
from jax.experimental import pallas as pl
from jax.experimental.pallas import tpu as pltpu
from jax.sharding import PartitionSpec as P

CODONS = 61

PRECISE = lax.Precision.HIGHEST
F32 = jnp.float32
VMEM_LIMIT = 48 * 1024 * 1024


def _dot(a, b):
    return jnp.dot(a, b, precision=PRECISE, preferred_element_type=F32)


def integrals(eig_values, branch):
    spread = (eig_values[:, None] - eig_values[None, :]) * branch
    near_zero = jnp.abs(spread) < 0.0001
    divisor = jnp.where(near_zero, jnp.ones_like(spread), spread)
    growth = jnp.where(
        near_zero, 1.0 + spread / 2.0 + spread * spread / 6.0, jnp.expm1(spread) / divisor
    )
    return branch * jnp.exp(eig_values[None, :] * branch) * growth


def branch_matrices(eig_vectors, eig_inverse, eig_values, count_basis, lengths):
    damping = jnp.exp(eig_values[None, :] * lengths[:, None])
    trans = jnp.einsum(
        "sk,ekt->est", eig_vectors, damping[:, :, None] * eig_inverse[None], precision=PRECISE
    )
    basis = count_basis[None] * jax.vmap(lambda t: integrals(eig_values, t))(lengths)
    mixed = jnp.einsum("sk,ekl->esl", eig_vectors, basis, precision=PRECISE)
    mixed = jnp.einsum("esl,lt->est", mixed, eig_inverse, precision=PRECISE)
    return trans, jnp.swapaxes(trans, 1, 2), mixed


def _climb_kernel(par_ref, leaf_ref, p_ref, m_ref, root_ref, msg_ref, num_ref, inner_ref, *,
                  mask):
    leaf_count = leaf_ref.shape[0]
    edge_count, states, columns = msg_ref.shape
    inner_ref[...] = jnp.ones(inner_ref.shape, F32)
    if mask:
        keep = (lax.broadcasted_iota(jnp.int32, (states, columns), 0) < CODONS).astype(F32)
    unroll = edge_count <= 32

    def push(c, x):
        msg = _dot(p_ref[c], x)
        msg_ref[c] = msg
        num_ref[c] = _dot(m_ref[c], x)
        p = par_ref[c] - leaf_count
        inner_ref[p] = inner_ref[p] * msg

    def leaf_step(c, carry):
        x = leaf_ref[c, 0:states, :]
        if mask:
            x = x * keep
        push(c, x)
        return carry

    lax.fori_loop(0, leaf_count, leaf_step, 0, unroll=unroll)

    def inner_step(c, logs):
        x = inner_ref[c - leaf_count]
        big = jnp.max(x, axis=0, keepdims=True)
        push(c, x / big)
        return logs + jnp.log(big)

    logs = lax.fori_loop(
        leaf_count, edge_count, inner_step, jnp.zeros((1, columns), F32), unroll=unroll
    )
    x = inner_ref[leaf_count - 2]
    big = jnp.max(x, axis=0, keepdims=True)
    root_ref[0:states, :] = x / big
    root_ref[states:states + 1, :] = logs + jnp.log(big)


def climb(parents, leaves, trans, mixed, mask):
    leaf_count, _, columns = leaves.shape
    edge_count, states, _ = trans.shape
    vmem = pl.BlockSpec(memory_space=pltpu.VMEM)
    return pl.pallas_call(
        functools.partial(_climb_kernel, mask=mask),
        out_shape=(
            jax.ShapeDtypeStruct((states + 1, columns), F32),
            jax.ShapeDtypeStruct((edge_count, states, columns), F32),
            jax.ShapeDtypeStruct((edge_count, states, columns), F32),
        ),
        in_specs=[pl.BlockSpec(memory_space=pltpu.SMEM), vmem, vmem, vmem],
        out_specs=(vmem, vmem, vmem),
        scratch_shapes=[pltpu.VMEM((leaf_count - 1, states, columns), F32)],
        compiler_params=pltpu.CompilerParams(vmem_limit_bytes=VMEM_LIMIT),
    )(parents, leaves, trans, mixed)


def _descend_kernel(par_ref, pick_ref, out_root_ref, msg_ref, num_ref, pt_ref, w_ref,
                    tot_ref, leaf_out_ref, outside_ref, kids_ref, *, want_leaf):
    edge_count, states, columns = msg_ref.shape
    leaf_count = (edge_count + 2) // 2
    node_count = edge_count + 1
    unroll = edge_count <= 32

    def clear(n, carry):
        kids_ref[n] = 0
        return carry

    lax.fori_loop(0, node_count, clear, 0)

    def add_kid(e, carry):
        p = par_ref[e]
        kids_ref[p] = kids_ref[p] + e
        return carry

    lax.fori_loop(0, edge_count, add_kid, 0)
    outside_ref[leaf_count - 2] = out_root_ref[...]
    w = w_ref[...]

    def arrive(c):
        p = par_ref[c]
        s = kids_ref[p] - c
        arriving = outside_ref[p - leaf_count] * msg_ref[s]
        den = jnp.sum(arriving * msg_ref[c], axis=0, keepdims=True)
        num = jnp.sum(arriving * num_ref[c], axis=0, keepdims=True)
        tot_ref[c] = w * num / den
        return arriving

    def outward(c, arriving):
        out = _dot(pt_ref[c], arriving)
        return out / jnp.max(out, axis=0, keepdims=True)

    def inner_step(i, carry):
        c = edge_count - 1 - i
        outside_ref[c - leaf_count] = outward(c, arrive(c))
        return carry

    lax.fori_loop(0, edge_count - leaf_count, inner_step, 0, unroll=unroll)

    def leaf_step(i, carry):
        arrive(leaf_count - 1 - i)
        return carry

    lax.fori_loop(0, leaf_count, leaf_step, 0, unroll=unroll)
    if want_leaf:
        g = pick_ref[0]
        p = par_ref[g]
        s = kids_ref[p] - g
        leaf_out_ref[...] = outward(g, outside_ref[p - leaf_count] * msg_ref[s])
    else:
        leaf_out_ref[...] = jnp.zeros(leaf_out_ref.shape, F32)


def descend(parents, pick, root_out, msgs, nums, trans_t, weight_row, want_leaf):
    edge_count, states, columns = msgs.shape
    leaf_count = (edge_count + 2) // 2
    vmem = pl.BlockSpec(memory_space=pltpu.VMEM)
    smem = pl.BlockSpec(memory_space=pltpu.SMEM)
    return pl.pallas_call(
        functools.partial(_descend_kernel, want_leaf=want_leaf),
        out_shape=(
            jax.ShapeDtypeStruct((edge_count, 1, columns), F32),
            jax.ShapeDtypeStruct((states, columns), F32),
        ),
        in_specs=[smem, smem, vmem, vmem, vmem, vmem, vmem],
        out_specs=(vmem, vmem),
        scratch_shapes=[
            pltpu.VMEM((leaf_count - 1, states, columns), F32),
            pltpu.SMEM((edge_count + 1,), jnp.int32),
        ],
        compiler_params=pltpu.CompilerParams(vmem_limit_bytes=VMEM_LIMIT),
    )(parents, pick, root_out, msgs, nums, trans_t, weight_row)


def on_device(
    tips,
    parents,
    branch_lengths,
    top_parents,
    top_lengths,
    weights,
    eig_vectors,
    eig_inverse,
    eig_values,
    labeled_rates,
    root_freq,
):
    states = tips.shape[1]
    columns = tips.shape[2]
    local_edges = parents.shape[0]
    groups = lax.axis_size("leaf")
    member_index = lax.axis_index("leaf")
    taxon_count = tips.shape[0] * groups
    count_basis = jnp.dot(
        jnp.dot(eig_inverse, labeled_rates, precision=PRECISE), eig_vectors, precision=PRECISE
    )
    lengths = jnp.concatenate([branch_lengths, top_lengths])
    trans, trans_t, mixed = branch_matrices(
        eig_vectors, eig_inverse, eig_values, count_basis, lengths
    )
    weight = weights.astype(F32)
    weight_row = weight[None, :]

    root_block, msgs, nums = climb(
        parents, tips, trans[:local_edges], mixed[:local_edges], True
    )
    gathered = lax.all_gather(root_block, "leaf", axis=0, tiled=False)
    top_block, top_msgs, top_nums = climb(
        top_parents, gathered, trans[local_edges:], mixed[local_edges:], False
    )
    top_root = top_block[:states]
    top_logs = top_block[states]
    likelihood = jnp.sum(root_freq[:, None] * top_root, axis=0)
    site_loglik = (
        jnp.log(likelihood) + top_logs + jnp.sum(gathered[:, states], axis=0)
    ) / taxon_count
    root_start = jnp.broadcast_to(root_freq[:, None], (states, columns))
    pick = jnp.reshape(member_index, (1,)).astype(jnp.int32)
    top_rows, subtree_out = descend(
        top_parents, pick, root_start, top_msgs, top_nums, trans_t[local_edges:], weight_row,
        True,
    )
    local_rows, _ = descend(
        parents, pick, subtree_out, msgs, nums, trans_t[:local_edges], weight_row, False
    )
    sums = jnp.concatenate(
        [jnp.sum(local_rows[:, 0], axis=1), jnp.sum(top_rows[:, 0], axis=1),
         jnp.sum(weight)[None]]
    )
    sums = lax.psum(sums, "site")
    weight_total = sums[-1]
    local_sum = sums[:local_edges]
    top_sum = sums[local_edges:-1]
    return (local_sum / weight_total, top_sum / weight_total, site_loglik)


def solution(mesh):
    placed = (
        P("leaf", None, "site"),
        P("leaf"),
        P("leaf"),
        P(),
        P(),
        P("site"),
        P(),
        P(),
        P(),
        P(),
        P(),
    )
    return jax.shard_map(
        on_device,
        mesh=mesh,
        in_specs=placed,
        out_specs=(P("leaf"), P(), P("site")),
        check_vma=False,
    )
```

time: 497 us -> 64.7 us (0.13); the launches traced: 491 us -> 64.2 us
  loops' own time: 203 us -> 0 us
  local copies, waits for them, and re-layouts: 101 us -> 6.73 us
  other arithmetic: 69.6 us -> 7.78 us
  matrix products: 40.3 us -> 5.35 us
  starting transfers between devices: 20.3 us -> 0 us
  blocking collectives: 46.3 us -> 29.8 us
  Pallas kernels: 0 us -> 13.7 us
  waiting for transfers between devices: 7.75 us -> 0 us
    another operation x6 -> x0, loops' own time: 203 us -> none  [the longest x1 63.8 us: descend(): return lax.fori_loop(0, edge_count, descend_visit, (outside, totals))]
    dynamic_slice x145 -> x0, local copies, waits for them, and re-layouts: 78.5 us -> none  [the longest x30 18.4 us: deepen(): return depths.at[position].set(depths[tree_links[position]] + 1)]
    psum x2 -> x1, blocking collectives: 46.3 us -> 4.91 us  [on_device(): sums = lax.psum(sums, 'site')]
    dot_general x140 -> x3, matrix products: 40 us -> 5.03 us  [the longest x1 2.44 us: branch_matrices(): mixed = jnp.einsum('sk,ekl->esl', eig_vectors, basis, precision=PRECISE)]
    all_gather x0 -> x1, blocking collectives: none -> 24.9 us  [on_device(): gathered = lax.all_gather(root_block, 'leaf', axis=0, tiled=False)]
    scatter x74 -> x0, other arithmetic: 20.6 us -> none  [the longest x14 10.2 us: descend_visit(): return (outside, totals.at[position].set(pattern_total))]
    all_to_all x4 -> x0, starting transfers between devices: 20.3 us -> none  [the longest x1 7.39 us: on_device(): lax.all_to_all(local_logs[None, None], 'leaf', split_axis=2, concat_axis=...]
    mul x15 -> x1, other arithmetic: 16.8 us -> 0.73 us  [integrals(): return branch * jnp.exp(eig_values[None, :] * branch) * growth]
  transfers between devices with their start and end apart: 4 -> 0, of which waited for: 2 -> 0; matrix products, arithmetic and copies ran while one was open for 12% -> 0% of each run, Pallas kernels for 0% -> 0%
where the time goes in v1:
time: 64.7 us; the launch traced here: 64.2 us
  blocking collectives  29.8 us (46%)
  Pallas kernels  13.7 us (21%)
  other arithmetic  7.78 us (12%)
  local copies, waits for them, and re-layouts  6.73 us (10%)
  matrix products  5.35 us (8%)
  between operations  0.91 us (1%)
    all_gather x1, blocking collectives, on_device(): gathered = lax.all_gather(root_block, 'leaf', axis=0, tiled=False)  24.9 us
    pallas_call x2, Pallas kernels, climb(): pl.pallas_call(functools.partial(_climb_kernel, mask=mask), out_shape=(ja...  6.88 us
    pallas_call x2, Pallas kernels, descend(): pl.pallas_call(functools.partial(_descend_kernel, want_leaf=want_leaf), o...  6.79 us
    psum x1, blocking collectives, on_device(): sums = lax.psum(sums, 'site')  4.91 us
    unnamed x33, local copies, waits for them, and re-layouts  4.25 us
    dot_general x1, matrix products, branch_matrices(): mixed = jnp.einsum('sk,ekl->esl', eig_vectors, basis, precision=PRECISE)  2.44 us
    div x2, other arithmetic, on_device(): return (local_sum / weight_total, top_sum / weight_total, site_loglik)  2.39 us
    dot_general x1, matrix products, branch_matrices(): jnp.einsum('sk,ekt->est', eig_vectors, damping[:, :, None] * eig_inverse[...  1.32 us

profile of v1, /device:TPU:0, one launch (start us, length us, event | category | flops | bytes accessed | tf_op | source)
XLA Modules:
  0.0 64.2 jit_solution(477547106178351970)
XLA Ops:
  0.6 0.8 %pad_maximum_fusion = f32[44]{0:T(128)S(1)} fusion(f32[30]{0:T(128)} %param.15, f32[14]{0:T(128)} %param.13), kind=kLoop, calls=%fused_computation.35 | loop fusion | flops 44 | bytes 352 | tf_op jit(solution)/shard_map/concatenate | solution.py:199
  1.4 0.7 %broadcast_multiply_fusion = (f32[44,64]{1,0:T(8,128)S(1)}, f32[44,64]{1,0:T(8,128)S(1)}) fusion(f32[44]{0:T(128)S(1)} %pad_maximum_fusion, f32[64]{0:T(128)} %param.19), kind=kLoop, calls=%fused_computation.33 | loop fusion | flops 5632 | bytes 22960 | tf_op jit(solution)/shard_map/vmap()/mul | solution.py:28
  2.1 0.8 %copy.16 = f32[64,64]{0,1:T(8,128)S(1)} copy(f32[64,64]{1,0:T(8,128)} %param.18) | data formatting | bytes 32768 | tf_op args[7]
  3.0 1.3 %fusion.11 = f32[44,64,64]{2,1,0:T(8,128)S(1)} fusion(f32[64,64]{0,1:T(8,128)S(1)} %copy.16, f32[44,64]{1,0:T(8,128)S(1)} %get-tuple-element.22, f32[64,64]{1,0:T(8,128)S(1)} %copy-done), kind=kOutput, calls=%fused_computation.14 | convolution fusion | flops 138592256 | bytes 764928 | tf_op jit(solution)/shard_map/sk,ekt->est/dot_general | solution.py:33
  4.4 0.4 copy.17
  4.8 0.6 %copy-done.7 = f32[44,64,64]{2,1,0:T(8,128)} copy-done((f32[44,64,64]{2,1,0:T(8,128)}, f32[44,64,64]{2,1,0:T(8,128)S(1)}, u32[]{:S(2)}) %copy-start.7) | copy-done | bytes 720920
  5.5 0.2 fusion.34
  5.7 0.2 fusion.35
  5.9 2.4 %convolution_bitcast_fusion = f32[44,64,64]{2,1,0:T(8,128)S(1)} fusion(f32[44]{0:T(128)S(1)} %pad_maximum_fusion, f32[64,64]{1,0:T(8,128)S(1)} %broadcast_subtract_fusion, f32[44,64]{1,0:T(8,128)S(1)} %get-tuple-element.21, f32[64,64]{1,0:T(8,128)S(1)} %fusion.35, f32[64,64]{1,0:T(8,128)S(1)} %copy-done), kind=kOutput, calls=%fused_computation.5 | convolution fusion | flops 140754944 | bytes 781488 | tf_op jit(solution)/shard_map/sk,ekl->esl/dot_general | solution.py:37
  8.4 1.3 %fusion.24 = f32[44,64,64]{2,1,0:T(8,128)S(1)} fusion(f32[44,64,64]{2,1,0:T(8,128)S(1)} %convolution_bitcast_fusion, f32[64,64]{1,0:T(8,128)S(1)} %copy-done.11), kind=kOutput, calls=%fused_computation.26 | convolution fusion | flops 138412032 | bytes 1458176 | tf_op jit(solution)/shard_map/esl,lt->est/dot_general | solution.py:38
  9.7 2.4 %shard_map.130 = (f32[65,128]{1,0:T(8,128)S(1)}, f32[14,64,128]{2,1,0:T(8,128)S(1)}, f32[14,64,128]{2,1,0:T(8,128)S(1)}) custom-call(s32[14]{0:T(128)S(1)} %copy-done.5, f32[8,64,128]{2,1,0:T(8,128)S(1)} %copy-done.3, f32[14,64,64]{2,1,0:T(8,128)S(1)} %slice.48.p_ref, f32[14,64,64]{2,1,0:T(8,128)S(1)} %slice.49.m_ref), custom_call_target="tpu_custom_call" | custom-call | tf_op jit(solution)/shard_map/pallas_call | solution.py:86
  12.1 24.9 %all-gather.1.leaf_ref = f32[16,65,128]{2,1,0:T(8,128)S(1)} all-gather(f32[1,65,128]{2,1,0:T(8,128)S(1)} %bitcast.28), channel_id=2, replica_groups=mesh['leaf'=16,'site'=2] {'leaf'}, dimensions={0}, use_global_device_ids=true | all-gather | bytes 565760 | tf_op jit(solution)/shard_map/all_gather | solution.py:209
  37.1 0.1 slice.51.m_ref
  37.2 0.6 copy-done.6
  37.8 4.5 %shard_map.131 = (f32[65,128]{1,0:T(8,128)S(1)}, f32[30,64,128]{2,1,0:T(8,128)S(1)}, f32[30,64,128]{2,1,0:T(8,128)S(1)}) custom-call(s32[30]{0:T(128)S(1)} %copy-done.6, f32[16,65,128]{2,1,0:T(8,128)S(1)} %all-gather.1.leaf_ref, f32[30,64,64]{2,1,0:T(8,128)S(1)} %slice.50.p_ref, f32[30,64,64]{2,1,0:T(8,128)S(1)} %slice.51.m_ref), custom_call_target="tpu_custom_call" | custom-call | tf_op jit(solution)/shard_map/pallas_call | solution.py:86
  42.3 0.9 %copy-done.1 = f32[30,64,128]{2,1,0:T(8,128)} copy-done((f32[30,64,128]{2,1,0:T(8,128)}, f32[30,64,128]{2,1,0:T(8,128)S(1)}, u32[]{:S(2)}) %copy-start.1) | copy-done | bytes 983064
  43.2 0.1 slice.52.pt_ref
  43.3 0.7 %convert_bitcast_fusion.w_ref = f32[1,128]{1,0:T(1,128)S(1)} fusion(s32[128]{0:T(128)} %param.16), kind=kLoop, calls=%fused_computation.43 | loop fusion | flops 128 | bytes 1024 | tf_op jit(solution)/shard_map/broadcast_in_dim | solution.py:204
  44.1 1.2 %copy-done.2 = f32[30,64,128]{2,1,0:T(8,128)S(1)} copy-done((f32[30,64,128]{2,1,0:T(8,128)S(1)}, f32[30,64,128]{2,1,0:T(8,128)}, u32[]{:S(2)}) %copy-start.2) | copy-done | bytes 983064
  45.3 4.1 %shard_map.132 = (f32[30,1,128]{2,1,0:T(1,128)S(1)}, f32[64,128]{1,0:T(8,128)S(1)}) custom-call(s32[30]{0:T(128)S(1)} %copy-done.6, s32[1]{0:T(128)} %bitcast.pick_ref, f32[64,128]{1,0:T(8,128)S(1)} %broadcast_in_dim.7.out_root_ref, f32[30,64,128]{2,1,0:T(8,128)S(1)} %get-tuple-element.13.msg_ref, f32[30,64,128]{2,1,0:T(8,128)S(1)} %copy-done.2, ...), custom_call_target="tpu_custom_call" | custom-call | tf_op jit(solution)/shard_map/pallas_call | solution.py:161
  49.5 1.1 %slice.53.pt_ref = f32[14,64,64]{2,1,0:T(8,128)S(1)} slice(f32[44,64,64]{2,1,0:T(8,128)} %copy-done.7), slice={[0:14], [0:64], [0:64]} | slice | bytes 458752 | tf_op jit(solution)/shard_map/slice | solution.py:226
  50.5 2.7 %shard_map.133 = (f32[14,1,128]{2,1,0:T(1,128)S(1)}, f32[64,128]{1,0:T(8,128)}) custom-call(s32[14]{0:T(128)S(1)} %copy-done.5, s32[1]{0:T(128)} %bitcast.pick_ref, f32[64,128]{1,0:T(8,128)S(1)} %get-tuple-element.15.out_root_ref, f32[14,64,128]{2,1,0:T(8,128)S(1)} %get-tuple-element.16.msg_ref, f32[14,64,128]{2,1,0:T(8,128)S(1)} %get-tuple-element.17.num_ref, ...), custom_call_target="tpu_custom_call" | custom-call | tf_op jit(solution)/shard_map/pallas_call | solution.py:161
  53.2 0.2 reduce_sum.45
  53.4 1.0 %reduce_sum.46 = f32[30]{0:T(128)S(1)} reduce(f32[30,1,128]{2,1,0:T(1,128)} %copy-done.4, f32[]{:T(128)} %constant.20.clone.1), dimensions={1,2}, to_apply=%region_1.2 | reduce | flops 3810 | bytes 15484 | tf_op jit(solution)/shard_map/reduce_sum | solution.py:229
  54.4 0.6 convert_reduce_fusion
  55.0 0.7 %pad_maximum_fusion.1 = f32[45]{0:T(128)S(1)} fusion(f32[1]{0:T(128)} %bitcast.7, f32[30]{0:T(128)S(1)} %reduce_sum.46, f32[14]{0:T(128)S(1)} %reduce_sum.45), kind=kLoop, calls=%fused_computation.36 | loop fusion | flops 90 | bytes 360 | tf_op jit(solution)/shard_map/concatenate | solution.py:228
  55.7 4.9 %psum.7 = f32[45]{0:T(128)S(1)} all-reduce(f32[45]{0:T(128)S(1)} %pad_maximum_fusion.1), channel_id=1, replica_groups=mesh['leaf'=16,'site'=2] {'site'}, use_global_device_ids=true, to_apply=%region_3.4 | all-reduce | flops 45 | bytes 360 | tf_op jit(solution)/shard_map/psum | solution.py:232
  60.6 0.6 slice.43
  61.2 1.2 %slice_divide_fusion = f32[30]{0:T(128)} fusion(f32[45]{0:T(128)S(1)} %psum.7, f32[]{:T(128)} %bitcast.8), kind=kLoop, calls=%fused_computation.40 | loop fusion | flops 30 | bytes 244 | tf_op jit(solution)/shard_map/div | solution.py:236
  62.4 1.2 %slice_divide_fusion.1 = f32[14]{0:T(128)} fusion(f32[45]{0:T(128)S(1)} %psum.7, f32[]{:T(128)} %bitcast.8), kind=kLoop, calls=%fused_computation.41 | loop fusion | flops 14 | bytes 116 | tf_op jit(solution)/shard_map/div | solution.py:236
  63.6 0.1 multiply_reduce_fusion
  63.7 0.5 fusion.29
  (34 shorter events, 0.4 us)
Async XLA Ops:
  0.6 2.3 %copy-start = (f32[64,64]{1,0:T(8,128)S(1)}, f32[64,64]{1,0:T(8,128)}, u32[]{:S(2)}) copy-start(f32[64,64]{1,0:T(8,128)} %param.17) | copy-start | bytes 49156
  4.3 1.1 %copy-start.7 = (f32[44,64,64]{2,1,0:T(8,128)}, f32[44,64,64]{2,1,0:T(8,128)S(1)}, u32[]{:S(2)}) copy-start(f32[44,64,64]{2,1,0:T(8,128)S(1)} %fusion.11) | copy-start | bytes 2162692
  4.3 1.2 %copy-start.11 = (f32[64,64]{1,0:T(8,128)S(1)}, f32[64,64]{1,0:T(8,128)}, u32[]{:S(2)}) copy-start(f32[64,64]{1,0:T(8,128)} %param.18) | copy-start | bytes 49156
  4.3 1.2 %copy-start.12 = (f32[64,64]{1,0:T(8,128)S(1)}, f32[64,64]{1,0:T(8,128)}, u32[]{:S(2)}) copy-start(f32[64,64]{1,0:T(8,128)} %param.20) | copy-start | bytes 49156
  4.3 1.5 %copy-start.13 = (f32[64]{0:T(128)S(1)}, f32[64]{0:T(128)}, u32[]{:S(2)}) copy-start(f32[64]{0:T(128)} %param.19) | copy-start | bytes 772
  5.4 2.9 %copy-start.9 = (f32[44,64,64]{1,2,0:T(8,128)}, f32[44,64,64]{1,2,0:T(8,128)S(1)}, u32[]{:S(2)}) copy-start(f32[44,64,64]{1,2,0:T(8,128)S(1)} %copy.17) | copy-start | bytes 2162692
  8.4 1.4 %copy-start.3 = (f32[8,64,128]{2,1,0:T(8,128)S(1)}, f32[8,64,128]{2,1,0:T(8,128)}, u32[]{:S(2)}) copy-start(f32[8,64,128]{2,1,0:T(8,128)} %leaf_ref.1) | copy-start | bytes 786436
  8.4 1.3 %copy-start.5 = (s32[14]{0:T(128)S(1)}, s32[14]{0:T(128)}, u32[]{:S(2)}) copy-start(s32[14]{0:T(128)} %par_ref.7) | copy-start | bytes 172
  9.7 27.3 %copy-start.10 = (f32[44,64,64]{1,2,0:T(8,128)S(1)}, f32[44,64,64]{1,2,0:T(8,128)}, u32[]{:S(2)}) copy-start(f32[44,64,64]{1,2,0:T(8,128)} %copy-done.9) | copy-start | bytes 2162692
  37.1 0.7 %copy-start.6 = (s32[30]{0:T(128)S(1)}, s32[30]{0:T(128)}, u32[]{:S(2)}) copy-start(s32[30]{0:T(128)} %par_ref.6) | copy-start | bytes 364
  37.8 5.5 %copy-start.8 = (f32[44,64,64]{2,1,0:T(8,128)S(1)}, f32[44,64,64]{2,1,0:T(8,128)}, u32[]{:S(2)}) copy-start(f32[44,64,64]{2,1,0:T(8,128)} %copy-done.7) | copy-start | bytes 2162692
  42.3 1.0 %copy-start.1 = (f32[30,64,128]{2,1,0:T(8,128)}, f32[30,64,128]{2,1,0:T(8,128)S(1)}, u32[]{:S(2)}) copy-start(f32[30,64,128]{2,1,0:T(8,128)S(1)} %get-tuple-element.14.num_ref) | copy-start | bytes 2949124
  43.2 0.8 %copy-start.14 = (f32[64]{0:T(128)S(1)}, f32[64]{0:T(128)}, u32[]{:S(2)}) copy-start(f32[64]{0:T(128)} %param.21) | copy-start | bytes 772
  44.1 1.2 %copy-start.2 = (f32[30,64,128]{2,1,0:T(8,128)S(1)}, f32[30,64,128]{2,1,0:T(8,128)}, u32[]{:S(2)}) copy-start(f32[30,64,128]{2,1,0:T(8,128)} %copy-done.1) | copy-start | bytes 2949124
  49.4 3.7 %copy-start.4 = (f32[30,1,128]{2,1,0:T(1,128)}, f32[30,1,128]{2,1,0:T(1,128)S(1)}, u32[]{:S(2)}) copy-start(f32[30,1,128]{2,1,0:T(1,128)S(1)} %get-tuple-element.19) | copy-start | bytes 46084
  49.4 4.9 %copy-start.15 = (s32[128]{0:T(128)S(1)}, s32[128]{0:T(128)}, u32[]{:S(2)}) copy-start(s32[128]{0:T(128)} %param.16) | copy-start | bytes 1540

commit v2 on v1

v2 whole, which is shorter than its diff:
```python
import functools

import jax
import jax.numpy as jnp
from jax import lax
from jax.experimental import pallas as pl
from jax.experimental.pallas import tpu as pltpu
from jax.sharding import PartitionSpec as P

CODONS = 61

PRECISE = lax.Precision.HIGHEST
F32 = jnp.float32
VMEM_LIMIT = 56 * 1024 * 1024
VMEM = pl.BlockSpec(memory_space=pltpu.VMEM)
SMEM = pl.BlockSpec(memory_space=pltpu.SMEM)


def _dot(a, b):
    return jnp.dot(a, b, precision=PRECISE, preferred_element_type=F32)


def integrals(eig_values, branch):
    spread = (eig_values[:, None] - eig_values[None, :]) * branch
    near_zero = jnp.abs(spread) < 0.0001
    divisor = jnp.where(near_zero, jnp.ones_like(spread), spread)
    growth = jnp.where(
        near_zero, 1.0 + spread / 2.0 + spread * spread / 6.0, jnp.expm1(spread) / divisor
    )
    return branch * jnp.exp(eig_values[None, :] * branch) * growth


def _params(edge_count):
    return pltpu.CompilerParams(vmem_limit_bytes=VMEM_LIMIT)


def _unroll(edge_count):
    return edge_count <= 32


def _climb_kernel(par_ref, len_ref, leaf_ref, v_ref, vi_ref, lam_ref,
                  root_ref, msg_ref, x_ref, inner_ref):
    leaf_count = leaf_ref.shape[0]
    edge_count, states, columns = msg_ref.shape
    vecs = v_ref[...]
    inv = vi_ref[...]
    lam = lam_ref[...]
    inner_ref[...] = jnp.ones(inner_ref.shape, F32)
    keep = (lax.broadcasted_iota(jnp.int32, (states, columns), 0) < CODONS).astype(F32)
    unroll = _unroll(edge_count)

    def push(c, x):
        trans = _dot(vecs, jnp.exp(lam * len_ref[c]) * inv)
        msg = _dot(trans, x)
        msg_ref[c] = msg
        x_ref[c] = x
        p = par_ref[c] - leaf_count
        inner_ref[p] = inner_ref[p] * msg

    def leaf_step(c, carry):
        push(c, leaf_ref[c] * keep)
        return carry

    lax.fori_loop(0, leaf_count, leaf_step, 0, unroll=unroll)

    def inner_step(c, logs):
        x = inner_ref[c - leaf_count]
        big = jnp.max(x, axis=0, keepdims=True)
        push(c, x / big)
        return logs + jnp.log(big)

    logs = lax.fori_loop(
        leaf_count, edge_count, inner_step, jnp.zeros((1, columns), F32), unroll=unroll
    )
    x = inner_ref[leaf_count - 2]
    big = jnp.max(x, axis=0, keepdims=True)
    root_ref[0:states, :] = x / big
    root_ref[states:states + 1, :] = logs + jnp.log(big)


def climb(parents, lengths, tips, vecs, inv, lam_col):
    leaf_count, states, columns = tips.shape
    edge_count = parents.shape[0]
    return pl.pallas_call(
        _climb_kernel,
        out_shape=(
            jax.ShapeDtypeStruct((states + 1, columns), F32),
            jax.ShapeDtypeStruct((edge_count, states, columns), F32),
            jax.ShapeDtypeStruct((edge_count, states, columns), F32),
        ),
        in_specs=[SMEM, SMEM, VMEM, VMEM, VMEM, VMEM],
        out_specs=(VMEM, VMEM, VMEM),
        scratch_shapes=[pltpu.VMEM((leaf_count - 1, states, columns), F32)],
        compiler_params=_params(edge_count),
    )(parents, lengths, tips, vecs, inv, lam_col)


def _matrix_kernel(len_ref, top_len_ref, v_ref, vi_ref, lab_ref, lam_ref, lam_row_ref,
                   jl_ref, jt_ref, xs_ref,
                   num_ref, ptl_ref, pt_ref, ptt_ref, mt_ref):
    local_edges = jl_ref.shape[0]
    top_edges = jt_ref.shape[0]
    vecs = v_ref[...]
    inv = vi_ref[...]
    lam = lam_ref[...]
    lam_row = lam_row_ref[...]
    basis = _dot(_dot(inv, lab_ref[...]), vecs)
    vecs_t = vecs.T
    inv_t = inv.T

    def local_step(c, carry):
        t = len_ref[c]
        mixed = _dot(_dot(vecs, basis * jl_ref[c]), inv)
        num_ref[c] = _dot(mixed, xs_ref[c])
        ptl_ref[c] = _dot(inv_t * jnp.exp(lam_row * t), vecs_t)
        return carry

    lax.fori_loop(0, local_edges, local_step, 0, unroll=_unroll(local_edges))

    def top_step(c, carry):
        t = top_len_ref[c]
        pt_ref[c] = _dot(vecs, jnp.exp(lam * t) * inv)
        ptt_ref[c] = _dot(inv_t * jnp.exp(lam_row * t), vecs_t)
        mt_ref[c] = _dot(_dot(vecs, basis * jt_ref[c]), inv)
        return carry

    lax.fori_loop(0, top_edges, top_step, 0, unroll=_unroll(top_edges))


def matrices(lengths, top_lengths, vecs, inv, labeled, lam_col, lam_row, j_local, j_top, xs):
    local_edges, states, columns = xs.shape
    top_edges = top_lengths.shape[0]
    sq = (states, states)
    return pl.pallas_call(
        _matrix_kernel,
        out_shape=(
            jax.ShapeDtypeStruct((local_edges, states, columns), F32),
            jax.ShapeDtypeStruct((local_edges,) + sq, F32),
            jax.ShapeDtypeStruct((top_edges,) + sq, F32),
            jax.ShapeDtypeStruct((top_edges,) + sq, F32),
            jax.ShapeDtypeStruct((top_edges,) + sq, F32),
        ),
        in_specs=[SMEM, SMEM] + [VMEM] * 8,
        out_specs=(VMEM,) * 5,
        compiler_params=_params(top_edges),
    )(lengths, top_lengths, vecs, inv, labeled, lam_col, lam_row, j_local, j_top, xs)


def _lane_put(row, lane, value):
    lanes = lax.broadcasted_iota(jnp.int32, row.shape, 1)
    return jnp.where(lanes == lane, value, row)


def _descend(par_ref, kids_ref, outside_ref, msg_ref, num_ref, pt_ref, w, root_out,
             lane_offset, row, want_leaf=None):
    edge_count = par_ref.shape[0]
    leaf_count = (edge_count + 2) // 2
    node_count = edge_count + 1
    unroll = _unroll(edge_count)

    def clear(n, carry):
        kids_ref[n] = 0
        return carry

    lax.fori_loop(0, node_count, clear, 0)

    def add_kid(e, carry):
        p = par_ref[e]
        kids_ref[p] = kids_ref[p] + e
        return carry

    lax.fori_loop(0, edge_count, add_kid, 0)
    outside_ref[leaf_count - 2] = root_out

    def arriving_of(c):
        p = par_ref[c]
        s = kids_ref[p] - c
        return outside_ref[p - leaf_count] * msg_ref[s]

    def count(c, arriving, row):
        den = jnp.sum(arriving * msg_ref[c], axis=0, keepdims=True)
        num = jnp.sum(arriving * num_ref[c], axis=0, keepdims=True)
        total = jnp.sum(w * num / den, axis=1, keepdims=True)
        return _lane_put(row, lane_offset + c, total)

    def outward(c, arriving):
        out = _dot(pt_ref[c], arriving)
        return out / jnp.max(out, axis=0, keepdims=True)

    def inner_step(i, row):
        c = edge_count - 1 - i
        arriving = arriving_of(c)
        outside_ref[c - leaf_count] = outward(c, arriving)
        return count(c, arriving, row)

    row = lax.fori_loop(0, edge_count - leaf_count, inner_step, row, unroll=unroll)

    def leaf_step(i, row):
        c = leaf_count - 1 - i
        return count(c, arriving_of(c), row)

    row = lax.fori_loop(0, leaf_count, leaf_step, row, unroll=unroll)
    leaf_out = None
    if want_leaf is not None:
        leaf_out = outward(want_leaf, arriving_of(want_leaf))
    return row, leaf_out


def _join_kernel(tpar_ref, tlen_ref, pick_ref, lpar_ref,
                 gat_ref, tp_ref, tpt_ref, tm_ref, rf_ref, w_ref,
                 lmsg_ref, lnum_ref, lpt_ref,
                 row_ref, loglik_ref,
                 tinner_ref, tmsg_ref, tnum_ref, toutside_ref, loutside_ref,
                 tkids_ref, lkids_ref, *, taxon_count):
    top_edges = tpar_ref.shape[0]
    leaf_count = gat_ref.shape[0]
    local_edges = lpar_ref.shape[0]
    states, columns = tmsg_ref.shape[1], tmsg_ref.shape[2]
    unroll = _unroll(top_edges)
    g = pick_ref[0]
    tinner_ref[...] = jnp.ones(tinner_ref.shape, F32)

    def push(c, x):
        msg = _dot(tp_ref[c], x)
        tmsg_ref[c] = msg
        tnum_ref[c] = _dot(tm_ref[c], x)
        p = tpar_ref[c] - leaf_count
        tinner_ref[p] = tinner_ref[p] * msg

    def leaf_step(c, logs):
        block = gat_ref[jnp.bitwise_xor(c, g)]
        push(c, block[0:states, :])
        return logs + block[states:states + 1, :]

    leaf_logs = lax.fori_loop(
        0, leaf_count, leaf_step, jnp.zeros((1, columns), F32), unroll=unroll
    )

    def inner_step(c, logs):
        x = tinner_ref[c - leaf_count]
        big = jnp.max(x, axis=0, keepdims=True)
        push(c, x / big)
        return logs + jnp.log(big)

    logs = lax.fori_loop(
        leaf_count, top_edges, inner_step, jnp.zeros((1, columns), F32), unroll=unroll
    )
    x = tinner_ref[leaf_count - 2]
    big = jnp.max(x, axis=0, keepdims=True)
    logs = logs + jnp.log(big)
    rf = rf_ref[...]
    likelihood = jnp.sum(rf * (x / big), axis=0, keepdims=True)
    loglik_ref[...] = (jnp.log(likelihood) + logs + leaf_logs) / taxon_count

    w = w_ref[...]
    row = jnp.zeros((1, row_ref.shape[1]), F32)
    row, subtree_out = _descend(
        tpar_ref, tkids_ref, toutside_ref, tmsg_ref, tnum_ref, tpt_ref, w,
        jnp.broadcast_to(rf, (states, columns)), local_edges, row, want_leaf=g,
    )
    row, _ = _descend(
        lpar_ref, lkids_ref, loutside_ref, lmsg_ref, lnum_ref, lpt_ref, w,
        subtree_out, 0, row,
    )
    row_ref[...] = _lane_put(row, local_edges + top_edges, jnp.sum(w, axis=1, keepdims=True))


def join(top_parents, top_lengths, pick, parents, gathered, tp, tpt, tm, rf_col, w_row,
         lmsgs, lnums, lpt, taxon_count):
    leaf_count, _, columns = gathered.shape
    top_edges = top_parents.shape[0]
    local_edges, states, _ = lmsgs.shape
    lanes = max(128, -(-(local_edges + top_edges + 1) // 128) * 128)
    return pl.pallas_call(
        functools.partial(_join_kernel, taxon_count=taxon_count),
        out_shape=(
            jax.ShapeDtypeStruct((1, lanes), F32),
            jax.ShapeDtypeStruct((1, columns), F32),
        ),
        in_specs=[SMEM] * 4 + [VMEM] * 9,
        out_specs=(VMEM, VMEM),
        scratch_shapes=[
            pltpu.VMEM((leaf_count - 1, states, columns), F32),
            pltpu.VMEM((top_edges, states, columns), F32),
            pltpu.VMEM((top_edges, states, columns), F32),
            pltpu.VMEM((leaf_count - 1, states, columns), F32),
            pltpu.VMEM(((local_edges + 2) // 2 - 1, states, columns), F32),
            pltpu.SMEM((top_edges + 1,), jnp.int32),
            pltpu.SMEM((local_edges + 1,), jnp.int32),
        ],
        compiler_params=_params(top_edges),
    )(top_parents, top_lengths, pick, parents, gathered, tp, tpt, tm, rf_col, w_row,
      lmsgs, lnums, lpt)


def gather_roots(block, groups):
    buf = block[None]
    step = groups // 2
    while step >= 1:
        other = lax.ppermute(buf, "leaf", [(i, i ^ step) for i in range(groups)])
        buf = jnp.stack([buf, other], axis=1).reshape((-1,) + block.shape)
        step //= 2
    return buf


def on_device(
    tips,
    parents,
    branch_lengths,
    top_parents,
    top_lengths,
    weights,
    eig_vectors,
    eig_inverse,
    eig_values,
    labeled_rates,
    root_freq,
):
    states = tips.shape[1]
    local_edges = parents.shape[0]
    groups = lax.axis_size("leaf")
    member_index = lax.axis_index("leaf")
    taxon_count = tips.shape[0] * groups
    lam_col = eig_values[:, None]
    lam_row = eig_values[None, :]

    root_block, msgs, xs = climb(parents, branch_lengths, tips, eig_vectors, eig_inverse, lam_col)
    if groups & (groups - 1) == 0:
        gathered = gather_roots(root_block, groups)
        pick = jnp.reshape(member_index, (1,)).astype(jnp.int32)
    else:
        gathered = lax.all_gather(root_block, "leaf", axis=0, tiled=False)
        pick = jnp.zeros((1,), jnp.int32)
    j_local = jax.vmap(lambda t: integrals(eig_values, t))(branch_lengths)
    j_top = jax.vmap(lambda t: integrals(eig_values, t))(top_lengths)
    nums, lpt, tp, tpt, tm = matrices(
        branch_lengths, top_lengths, eig_vectors, eig_inverse, labeled_rates, lam_col, lam_row,
        j_local, j_top, xs,
    )
    w_row = weights.astype(F32)[None, :]
    row, loglik = join(
        top_parents, top_lengths, pick, parents, gathered, tp, tpt, tm, root_freq[:, None],
        w_row, msgs, nums, lpt, taxon_count,
    )
    sums = lax.psum(row[0], "site")
    top_edges = top_parents.shape[0]
    weight_total = sums[local_edges + top_edges]
    return (
        sums[:local_edges] / weight_total,
        sums[local_edges:local_edges + top_edges] / weight_total,
        loglik[0],
    )


def solution(mesh):
    placed = (
        P("leaf", None, "site"),
        P("leaf"),
        P("leaf"),
        P(),
        P(),
        P("site"),
        P(),
        P(),
        P(),
        P(),
        P(),
    )
    return jax.shard_map(
        on_device,
        mesh=mesh,
        in_specs=placed,
        out_specs=(P("leaf"), P(), P("site")),
        check_vma=False,
    )
```

time: 64.7 us -> 61.9 us (0.957)
  blocking collectives: 29.8 us -> 4.91 us
  Pallas kernels: 13.7 us -> 30.5 us
  starting transfers between devices: 0 us -> 7.53 us
  waiting for transfers between devices: 0 us -> 6.79 us
  matrix products: 5.35 us -> 0 us
  other arithmetic: 7.78 us -> 6.05 us
  local copies, waits for them, and re-layouts: 6.73 us -> 5.14 us
    all_gather x1 -> x0, blocking collectives: 24.9 us -> none  [on_device(): gathered = lax.all_gather(root_block, 'leaf', axis=0, tiled=False)]
    pallas_call x4 -> x3, Pallas kernels: 13.7 us -> 30.5 us  [the longest x1 14.3 us: matrices(): pl.pallas_call(_matrix_kernel, out_shape=(jax.ShapeDtypeStruct((local_edg...]
    ppermute x0 -> x4, starting transfers between devices: none -> 7.53 us  [gather_roots(): other = lax.ppermute(buf, 'leaf', [(i, i ^ step) for i in range(groups)])]
    ppermute x0 -> x4, waiting for transfers between devices: none -> 6.79 us  [gather_roots(): other = lax.ppermute(buf, 'leaf', [(i, i ^ step) for i in range(groups)])]
    dot_general x5 -> x0, matrix products: 5.35 us -> none  [the longest x1 2.44 us: branch_matrices(): mixed = jnp.einsum('sk,ekl->esl', eig_vectors, basis, precision=PRECISE)]
    unnamed x33 -> x14, local copies, waits for them, and re-layouts: 4.25 us -> 2 us
    mul x1 -> x4, other arithmetic: 0.73 us -> 2.95 us  [integrals(): return branch * jnp.exp(eig_values[None, :] * branch) * growth]
    reduce_sum x5 -> x0, other arithmetic: 1.93 us -> none  [the longest x1 1.02 us: on_device(): jnp.sum(top_rows[:, 0], axis=1)]
  transfers between devices with their start and end apart: 0 -> 4, of which waited for: 0 -> 3; matrix products, arithmetic and copies ran while one was open for 0% -> 7% of each run, Pallas kernels for 0% -> 23%
where the time goes in v2:
time: 61.9 us; the launch traced here: 61.7 us
  Pallas kernels  30.5 us (49%)
  starting transfers between devices  7.53 us (12%)
  waiting for transfers between devices  6.79 us (11%)
  other arithmetic  6.05 us (10%)
  local copies, waits for them, and re-layouts  5.14 us (8%)
  blocking collectives  4.91 us (8%)
  between operations  0.7 us (1%)
    pallas_call x1, Pallas kernels, matrices(): pl.pallas_call(_matrix_kernel, out_shape=(jax.ShapeDtypeStruct((local_edg...  14.3 us
    pallas_call x1, Pallas kernels, join(): pl.pallas_call(functools.partial(_join_kernel, taxon_count=taxon_count),...  12.3 us
    ppermute x4, starting transfers between devices, gather_roots(): other = lax.ppermute(buf, 'leaf', [(i, i ^ step) for i in range(groups)])  7.53 us
    ppermute x4, waiting for transfers between devices, gather_roots(): other = lax.ppermute(buf, 'leaf', [(i, i ^ step) for i in range(groups)])  6.79 us
    psum x1, blocking collectives, on_device(): sums = lax.psum(row[0], 'site')  4.91 us
    pallas_call x1, Pallas kernels, climb(): pl.pallas_call(_climb_kernel, out_shape=(jax.ShapeDtypeStruct((states + 1...  3.96 us
    mul x4, other arithmetic, integrals(): return branch * jnp.exp(eig_values[None, :] * branch) * growth  2.95 us
    unnamed x14, local copies, waits for them, and re-layouts  2 us
  transfers between devices with their start and end apart: 4, of which 3 were waited for; matrix products, arithmetic and copies ran while one was open for 7% of the time, Pallas kernels for 23%

profile of v2, /device:TPU:0, one launch (start us, length us, event | category | flops | bytes accessed | tf_op | source)
XLA Modules:
  0.0 61.7 jit_solution(5898613492195399725)
XLA Ops:
  0.6 0.0 copy-start.1
  0.6 0.6 %copy-done.1 = f32[64]{0:T(128)S(1)} copy-done((f32[64]{0:T(128)S(1)}, f32[64]{0:T(128)}, u32[]{:S(2)}) %copy-start.1) | copy-done | bytes 280
  1.3 0.7 %copy.22.lam_ref = f32[64,1]{1,0:T(8,128)} copy(f32[64,1]{0,1:T(1,128)S(1)} %bitcast.36) | data formatting | bytes 512 | tf_op jit(solution)/shard_map/broadcast_in_dim | solution.py:324
  2.0 4.0 %shard_map.130 = (f32[65,128]{1,0:T(8,128)}, f32[14,64,128]{2,1,0:T(8,128)}, f32[14,64,128]{2,1,0:T(8,128)}) custom-call(s32[14]{0:T(128)} %lpar_ref.1, f32[14]{0:T(128)} %len_ref.3, f32[8,64,128]{2,1,0:T(8,128)} %leaf_ref.1, f32[64,64]{1,0:T(8,128)} %v_ref.3, f32[64,64]{1,0:T(8,128)} %vi_ref.3, f32[64,1]{1,0:T(8,128)} %copy.22.lam_ref), custom_call_target="tpu_custom_call" | custom-call | tf_op jit(solution)/shard_map/pallas_call | solution.py:84
  6.0 4.1 %collective-permute-start = (f32[1,65,128]{2,1,0:T(8,128)}, f32[1,65,128]{2,1,0:T(8,128)S(1)}, u32[]{:S(2)}, u32[]{:S(2)}) collective-permute-start(f32[1,65,128]{2,1,0:T(8,128)} %bitcast.32), channel_id=1, source_target_pairs={{0,16},{2,18},{4,20},{6,22},{8,24},{10,26},{12,28},{14,30},{16,0},... | collective-permute-start | bytes 99848 | tf_op jit(solution)/shard_map/ppermute | solution.py:300
  10.1 0.1 broadcast_subtract_fusion
  10.2 0.1 exponential_multiply_fusion
  10.3 2.4 %collective-permute-done = f32[1,65,128]{2,1,0:T(8,128)S(1)} collective-permute-done((f32[1,65,128]{2,1,0:T(8,128)}, f32[1,65,128]{2,1,0:T(8,128)S(1)}, u32[]{:S(2)}, u32[]{:S(2)}) %collective-permute-start) | collective-permute-done | bytes 33312 | tf_op jit(solution)/shard_map/ppermute | solution.py:300
  12.7 1.6 %collective-permute-start.1 = (f32[2,65,128]{2,1,0:T(8,128)S(1)}, f32[2,65,128]{2,1,0:T(8,128)S(1)}, u32[]{:S(2)}, u32[]{:S(2)}) collective-permute-start(f32[2,65,128]{2,1,0:T(8,128)S(1)} %get-tuple-element.24), channel_id=1, source_target_pairs={{0,8},{2,10},{4,12},{6,14},{8,0},{10,2},{12,4},{14,6},{16,24},{18,... | collective-permute-start | bytes 199688 | tf_op jit(solution)/shard_map/ppermute | solution.py:300
  14.2 1.7 %fusion.4.jt_ref = f32[30,64,64]{2,1,0:T(8,128)} fusion(f32[30]{0:T(128)S(1)} %copy-done.2, f32[64,64]{1,0:T(8,128)S(1)} %broadcast_subtract_fusion, f32[30,64]{1,0:T(8,128)S(1)} %exponential_multiply_fusion), kind=kLoop, calls=%fused_computation.14 | loop fusion | flops 1474560 | bytes 515704 | tf_op jit(solution)/shard_map/vmap()/mul | solution.py:30
  15.9 1.2 %collective-permute-done.1 = f32[2,65,128]{2,1,0:T(8,128)S(1)} collective-permute-done((f32[2,65,128]{2,1,0:T(8,128)S(1)}, f32[2,65,128]{2,1,0:T(8,128)S(1)}, u32[]{:S(2)}, u32[]{:S(2)}) %collective-permute-start.1) | collective-permute-done | bytes 66592 | tf_op jit(solution)/shard_map/ppermute | solution.py:300
  17.1 0.1 copy.23
  17.2 0.0 copy-start.3
  17.2 1.8 %collective-permute-start.2 = (f32[4,65,128]{2,0,1:T(4,128)S(1)}, f32[4,65,128]{2,0,1:T(4,128)S(1)}, u32[]{:S(2)}, u32[]{:S(2)}) collective-permute-start(f32[4,65,128]{2,0,1:T(4,128)S(1)} %bitcast.27), channel_id=1, source_target_pairs={{0,4},{2,6},{4,0},{6,2},{8,12},{10,14},{12,8},{14,10},{16,20},{18,... | collective-permute-start | bytes 399368 | tf_op jit(solution)/shard_map/ppermute | solution.py:300
  18.9 0.1 exponential_multiply_fusion.1
  19.0 3.2 %collective-permute-done.2 = f32[4,65,128]{2,0,1:T(4,128)S(1)} collective-permute-done((f32[4,65,128]{2,0,1:T(4,128)S(1)}, f32[4,65,128]{2,0,1:T(4,128)S(1)}, u32[]{:S(2)}, u32[]{:S(2)}) %collective-permute-start.2) | collective-permute-done | bytes 133152 | tf_op jit(solution)/shard_map/ppermute | solution.py:300
  22.2 0.1 pad_maximum_fusion.1
  22.3 0.1 copy.25
  22.5 0.1 collective-permute-start.3
  22.5 1.1 %fusion.11.jl_ref = f32[14,64,64]{2,1,0:T(8,128)} fusion(f32[14]{0:T(128)S(1)} %copy-done.3, f32[64,64]{1,0:T(8,128)S(1)} %broadcast_subtract_fusion, f32[14,64]{1,0:T(8,128)S(1)} %exponential_multiply_fusion.1), kind=kLoop, calls=%fused_computation.22 | loop fusion | flops 688128 | bytes 249400 | tf_op jit(solution)/shard_map/vmap()/mul | solution.py:30
  23.7 0.7 %copy-done.4 = f32[64]{0:T(128)S(1)} copy-done((f32[64]{0:T(128)S(1)}, f32[64]{0:T(128)}, u32[]{:S(2)}) %copy-start.4) | copy-done | bytes 280
  24.3 0.7 %copy.29.rf_ref = f32[64,1]{1,0:T(8,128)} copy(f32[64,1]{0,1:T(1,128)S(1)} %bitcast.37) | data formatting | bytes 512 | tf_op jit(solution)/shard_map/broadcast_in_dim | solution.py:342
  25.0 14.3 %shard_map.131 = (f32[14,64,128]{2,1,0:T(8,128)}, f32[14,64,64]{2,1,0:T(8,128)}, f32[30,64,64]{2,1,0:T(8,128)}, f32[30,64,64]{2,1,0:T(8,128)}, f32[30,64,64]{2,1,0:T(8,128)}) custom-call(f32[14]{0:T(128)} %len_ref.3, f32[30]{0:T(128)} %tlen_ref.1, f32[64,64]{1,0:T(8,128)} %v_ref.3, f32[64,64]{1,0:T(8,128)} %vi_ref.3, f32[64,64]{1,0:T(8,128)} %lab_ref.1, ...), custom_call_target="tpu_custom_call" | custom-call | tf_op jit(solution)/shard_map/pallas_call | solution.py:134
  39.3 0.5 convert_bitcast_fusion.w_ref
  39.8 0.1 pad_maximum_fusion
  39.9 0.9 %copy.27 = f32[8,2,65,128]{3,2,1,0:T(8,128)} copy(f32[8,2,65,128]{3,0,2,1:T(8,128)S(1)} %pad_maximum_fusion) | data formatting | bytes 1064960 | tf_op jit(solution)/shard_map/stack | solution.py:301
  40.8 12.3 %shard_map.132 = (f32[1,128]{1,0:T(1,128)}, f32[1,128]{1,0:T(1,128)}) custom-call(s32[30]{0:T(128)} %tpar_ref.1, f32[30]{0:T(128)} %tlen_ref.1, s32[1]{0:T(128)} %bitcast.pick_ref, s32[14]{0:T(128)} %lpar_ref.1, f32[16,65,128]{2,1,0:T(8,128)} %bitcast.24, f32[30,64,64]{2,1,0:T(8,128)} %get-tuple-element.15.tp_ref, f32[30,64,64]{2,1,0:T(8,128)} %get-tuple-element.16.tpt_ref, ...), custom_call_target="tpu_custom_call" | custom-call | tf_op jit(solution)/shard_map/pallas_call | solution.py:274
  53.1 0.7 %copy-done.6 = f32[1,128]{1,0:T(1,128)S(1)} copy-done((f32[1,128]{1,0:T(1,128)S(1)}, f32[1,128]{1,0:T(1,128)}, u32[]{:S(2)}) %copy-start.6) | copy-done | bytes 536
  53.8 4.9 %psum.7 = f32[128]{0:T(128)S(1)} all-reduce(f32[128]{0:T(128)S(1)} %bitcast.39), channel_id=1, replica_groups=mesh['leaf'=16,'site'=2] {'site'}, use_global_device_ids=true, to_apply=%region_0.1 | all-reduce | flops 128 | bytes 1024 | tf_op jit(solution)/shard_map/psum | solution.py:345
  58.7 0.6 slice.10
  59.3 1.2 %slice_divide_fusion = f32[30]{0:T(128)} fusion(f32[128]{0:T(128)S(1)} %psum.7, f32[]{:T(128)} %bitcast.19), kind=kLoop, calls=%fused_computation.33 | loop fusion | flops 30 | bytes 244 | tf_op jit(solution)/shard_map/div | solution.py:350
  60.5 1.2 %slice_divide_fusion.1 = f32[14]{0:T(128)} fusion(f32[128]{0:T(128)S(1)} %psum.7, f32[]{:T(128)} %bitcast.19), kind=kLoop, calls=%fused_computation.34 | loop fusion | flops 14 | bytes 116 | tf_op jit(solution)/shard_map/div | solution.py:349
  (12 shorter events, 0.0 us)
Async XLA Ops:
  0.6 0.7 %copy-start.1 = (f32[64]{0:T(128)S(1)}, f32[64]{0:T(128)}, u32[]{:S(2)}) copy-start(f32[64]{0:T(128)} %param.19) | copy-start | bytes 772
  6.0 6.7 %copy-start = (f32[65,128]{1,0:T(8,128)S(1)}, f32[65,128]{1,0:T(8,128)}, u32[]{:S(2)}) copy-start(f32[65,128]{1,0:T(8,128)} %get-tuple-element.13) | copy-start | bytes 99844
  6.0 4.2 %copy-start.2 = (f32[30]{0:T(128)S(1)}, f32[30]{0:T(128)}, u32[]{:S(2)}) copy-start(f32[30]{0:T(128)} %tlen_ref.1) | copy-start | bytes 364
  6.0 6.7 %collective-permute-start = (f32[1,65,128]{2,1,0:T(8,128)}, f32[1,65,128]{2,1,0:T(8,128)S(1)}, u32[]{:S(2)}, u32[]{:S(2)}) collective-permute-start(f32[1,65,128]{2,1,0:T(8,128)} %bitcast.32), channel_id=1, source_target_pairs={{0,16},{2,18},{4,20},{6,22},{8,24},{10,26},{12,28},{14,30},{16,0},... | collective-permute-start | bytes 99848 | tf_op jit(solution)/shard_map/ppermute | solution.py:300
  12.7 4.4 %collective-permute-start.1 = (f32[2,65,128]{2,1,0:T(8,128)S(1)}, f32[2,65,128]{2,1,0:T(8,128)S(1)}, u32[]{:S(2)}, u32[]{:S(2)}) collective-permute-start(f32[2,65,128]{2,1,0:T(8,128)S(1)} %get-tuple-element.24), channel_id=1, source_target_pairs={{0,8},{2,10},{4,12},{6,14},{8,0},{10,2},{12,4},{14,6},{16,24},{18,... | collective-permute-start | bytes 199688 | tf_op jit(solution)/shard_map/ppermute | solution.py:300
  17.2 1.8 %copy-start.3 = (f32[14]{0:T(128)S(1)}, f32[14]{0:T(128)}, u32[]{:S(2)}) copy-start(f32[14]{0:T(128)} %len_ref.3) | copy-start | bytes 172
  17.2 5.1 %collective-permute-start.2 = (f32[4,65,128]{2,0,1:T(4,128)S(1)}, f32[4,65,128]{2,0,1:T(4,128)S(1)}, u32[]{:S(2)}, u32[]{:S(2)}) collective-permute-start(f32[4,65,128]{2,0,1:T(4,128)S(1)} %bitcast.27), channel_id=1, source_target_pairs={{0,4},{2,6},{4,0},{6,2},{8,12},{10,14},{12,8},{14,10},{16,20},{18,... | collective-permute-start | bytes 399368 | tf_op jit(solution)/shard_map/ppermute | solution.py:300
  22.5 17.4 %collective-permute-start.3 = (f32[8,65,128]{2,0,1:T(8,128)S(1)}, f32[8,65,128]{2,0,1:T(8,128)S(1)}, u32[]{:S(2)}, u32[]{:S(2)}) collective-permute-start(f32[8,65,128]{2,0,1:T(8,128)S(1)} %bitcast.25), channel_id=1, source_target_pairs={{0,2},{2,0},{4,6},{6,4},{8,10},{10,8},{12,14},{14,12},{16,18},{18,... | collective-permute-start | bytes 798728 | tf_op jit(solution)/shard_map/ppermute | solution.py:300
  23.7 0.7 %copy-start.4 = (f32[64]{0:T(128)S(1)}, f32[64]{0:T(128)}, u32[]{:S(2)}) copy-start(f32[64]{0:T(128)} %param.21) | copy-start | bytes 772
  25.0 14.3 %copy-start.5 = (s32[128]{0:T(128)S(1)}, s32[128]{0:T(128)}, u32[]{:S(2)}) copy-start(s32[128]{0:T(128)} %param.16) | copy-start | bytes 1540
  53.1 0.7 %copy-start.6 = (f32[1,128]{1,0:T(1,128)S(1)}, f32[1,128]{1,0:T(1,128)}, u32[]{:S(2)}) copy-start(f32[1,128]{1,0:T(1,128)} %get-tuple-element.21) | copy-start | bytes 1540

commit v3 on v2

v3 whole, which is shorter than its diff:
```python
import functools

import jax
import jax.numpy as jnp
from jax import lax
from jax.experimental import pallas as pl
from jax.experimental.pallas import tpu as pltpu
from jax.sharding import PartitionSpec as P

CODONS = 61

PRECISE = lax.Precision.HIGHEST
F32 = jnp.float32
VMEM_LIMIT = 56 * 1024 * 1024
VMEM = pl.BlockSpec(memory_space=pltpu.VMEM)
SMEM = pl.BlockSpec(memory_space=pltpu.SMEM)


def _dot(a, b):
    return jnp.dot(a, b, precision=PRECISE, preferred_element_type=F32)


def integrals(eig_values, branch):
    spread = (eig_values[:, None] - eig_values[None, :]) * branch
    near_zero = jnp.abs(spread) < 0.0001
    divisor = jnp.where(near_zero, jnp.ones_like(spread), spread)
    growth = jnp.where(
        near_zero, 1.0 + spread / 2.0 + spread * spread / 6.0, jnp.expm1(spread) / divisor
    )
    return branch * jnp.exp(eig_values[None, :] * branch) * growth


PARAMS = pltpu.CompilerParams(vmem_limit_bytes=VMEM_LIMIT)


def _cols(c, columns):
    return slice(c * columns, (c + 1) * columns)


def _climb_kernel(par_ref, len_ref, leaf_ref, v_ref, vi_ref, lam_ref,
                  root_ref, msg_ref, xw_ref, tr_ref, inner_ref):
    leaf_count = leaf_ref.shape[0]
    edge_count, states, columns = msg_ref.shape
    vecs = v_ref[...]
    inv = vi_ref[...]
    lam = lam_ref[...]
    inner_ref[...] = jnp.ones(inner_ref.shape, F32)
    keep = (lax.broadcasted_iota(jnp.int32, (states, columns), 0) < CODONS).astype(F32)
    logs = jnp.zeros((1, columns), F32)
    for c in range(edge_count):
        if c < leaf_count:
            x = leaf_ref[c] * keep
        else:
            x = inner_ref[c - leaf_count]
            big = jnp.max(x, axis=0, keepdims=True)
            x = x / big
            logs = logs + jnp.log(big)
        trans = _dot(vecs, jnp.exp(lam * len_ref[c]) * inv)
        tr_ref[c] = trans
        msg = _dot(trans, x)
        msg_ref[c] = msg
        xw_ref[:, _cols(c, columns)] = x
        p = par_ref[c] - leaf_count
        inner_ref[p] = inner_ref[p] * msg
    x = inner_ref[leaf_count - 2]
    big = jnp.max(x, axis=0, keepdims=True)
    root_ref[0:states, :] = x / big
    root_ref[states:states + 1, :] = logs + jnp.log(big)


def climb(parents, lengths, tips, vecs, inv, lam_col):
    leaf_count, states, columns = tips.shape
    edge_count = parents.shape[0]
    return pl.pallas_call(
        _climb_kernel,
        out_shape=(
            jax.ShapeDtypeStruct((states + 1, columns), F32),
            jax.ShapeDtypeStruct((edge_count, states, columns), F32),
            jax.ShapeDtypeStruct((states, edge_count * columns), F32),
            jax.ShapeDtypeStruct((edge_count, states, states), F32),
        ),
        in_specs=[SMEM, SMEM, VMEM, VMEM, VMEM, VMEM],
        out_specs=(VMEM,) * 4,
        scratch_shapes=[pltpu.VMEM((leaf_count - 1, states, columns), F32)],
        compiler_params=PARAMS,
    )(parents, lengths, tips, vecs, inv, lam_col)


def _matrix_kernel(top_len_ref, v_ref, vi_ref, lab_ref, lam_ref, jl_ref, xw_ref, trl_ref,
                   mixed_ref, ptl_ref, tp_ref, tpt_ref, basis_ref, vw_ref):
    local_edges, states, columns = mixed_ref.shape
    top_edges = tp_ref.shape[0]
    vecs = v_ref[...]
    inv = vi_ref[...]
    lam = lam_ref[...]
    basis = _dot(_dot(inv, lab_ref[...]), vecs)
    basis_ref[...] = basis
    vw_ref[...] = _dot(inv, xw_ref[...])
    for c in range(local_edges):
        mixed_ref[c] = _dot(basis * jl_ref[c], vw_ref[:, _cols(c, columns)])
        ptl_ref[c] = trl_ref[c].T
    for c in range(top_edges):
        trans = _dot(vecs, jnp.exp(lam * top_len_ref[c]) * inv)
        tp_ref[c] = trans
        tpt_ref[c] = trans.T


def matrices(top_lengths, vecs, inv, labeled, lam_col, j_local, xw, trl):
    local_edges, states, _ = trl.shape
    columns = xw.shape[1] // local_edges
    top_edges = top_lengths.shape[0]
    sq = (states, states)
    return pl.pallas_call(
        _matrix_kernel,
        out_shape=(
            jax.ShapeDtypeStruct((local_edges, states, columns), F32),
            jax.ShapeDtypeStruct((local_edges,) + sq, F32),
            jax.ShapeDtypeStruct((top_edges,) + sq, F32),
            jax.ShapeDtypeStruct((top_edges,) + sq, F32),
            jax.ShapeDtypeStruct(sq, F32),
        ),
        in_specs=[SMEM] + [VMEM] * 7,
        out_specs=(VMEM,) * 5,
        scratch_shapes=[pltpu.VMEM((states, local_edges * columns), F32)],
        compiler_params=PARAMS,
    )(top_lengths, vecs, inv, labeled, lam_col, j_local, xw, trl)


def _lane_put(row, lane, value):
    lanes = lax.broadcasted_iota(jnp.int32, row.shape, 1)
    return jnp.where(lanes == lane, value, row)


def _descend(par_ref, kids_ref, outside_ref, arr_ref, msg_ref, pt_ref, root_out, pick=None):
    edge_count = par_ref.shape[0]
    leaf_count = (edge_count + 2) // 2
    columns = msg_ref.shape[2]
    for n in range(edge_count + 1):
        kids_ref[n] = 0
    for e in range(edge_count):
        p = par_ref[e]
        kids_ref[p] = kids_ref[p] + e
    outside_ref[leaf_count - 2] = root_out

    def arriving_of(c):
        p = par_ref[c]
        s = kids_ref[p] - c
        return outside_ref[p - leaf_count] * msg_ref[s]

    def outward(c, arriving):
        out = _dot(pt_ref[c], arriving)
        return out / jnp.max(out, axis=0, keepdims=True)

    for c in range(edge_count - 1, -1, -1):
        arriving = arriving_of(c)
        arr_ref[:, _cols(c, columns)] = arriving
        if c >= leaf_count:
            outside_ref[c - leaf_count] = outward(c, arriving)
    if pick is not None:
        return outward(pick, arriving_of(pick))
    return None


def _counts(row, lane_offset, w, vt, arr_ref, msg_ref, mixed_of):
    edge_count, _, columns = msg_ref.shape
    weighted = _dot(vt, arr_ref[...])
    for c in range(edge_count):
        cols = _cols(c, columns)
        num = jnp.sum(weighted[:, cols] * mixed_of(c), axis=0, keepdims=True)
        den = jnp.sum(arr_ref[:, cols] * msg_ref[c], axis=0, keepdims=True)
        total = jnp.sum(w * num / den, axis=1, keepdims=True)
        row = _lane_put(row, lane_offset + c, total)
    return row


def _join_kernel(tpar_ref, pick_ref, lpar_ref,
                 gat_ref, tp_ref, tpt_ref, basis_ref, jt_ref, v_ref, vi_ref, rf_ref, w_ref,
                 lmsg_ref, lmixed_ref, lpt_ref,
                 row_ref, loglik_ref,
                 tinner_ref, tmsg_ref, txw_ref, tvw_ref, toutside_ref, tarr_ref,
                 loutside_ref, larr_ref, tkids_ref, lkids_ref, *, taxon_count):
    top_edges = tpar_ref.shape[0]
    leaf_count = gat_ref.shape[0]
    local_edges = lpar_ref.shape[0]
    states, columns = tmsg_ref.shape[1], tmsg_ref.shape[2]
    g = pick_ref[0]
    tinner_ref[...] = jnp.ones(tinner_ref.shape, F32)
    logs = jnp.zeros((1, columns), F32)
    leaf_logs = jnp.zeros((1, columns), F32)
    for c in range(top_edges):
        if c < leaf_count:
            block = gat_ref[jnp.bitwise_xor(c, g)]
            x = block[0:states, :]
            leaf_logs = leaf_logs + block[states:states + 1, :]
        else:
            x = tinner_ref[c - leaf_count]
            big = jnp.max(x, axis=0, keepdims=True)
            x = x / big
            logs = logs + jnp.log(big)
        msg = _dot(tp_ref[c], x)
        tmsg_ref[c] = msg
        txw_ref[:, _cols(c, columns)] = x
        p = tpar_ref[c] - leaf_count
        tinner_ref[p] = tinner_ref[p] * msg
    x = tinner_ref[leaf_count - 2]
    big = jnp.max(x, axis=0, keepdims=True)
    logs = logs + jnp.log(big)
    rf = rf_ref[...]
    likelihood = jnp.sum(rf * (x / big), axis=0, keepdims=True)
    loglik_ref[...] = (jnp.log(likelihood) + logs + leaf_logs) / taxon_count

    inv = vi_ref[...]
    vt = v_ref[...].T
    basis = basis_ref[...]
    tvw_ref[...] = _dot(inv, txw_ref[...])
    subtree_out = _descend(
        tpar_ref, tkids_ref, toutside_ref, tarr_ref, tmsg_ref, tpt_ref,
        jnp.broadcast_to(rf, (states, columns)), pick=g,
    )
    _descend(lpar_ref, lkids_ref, loutside_ref, larr_ref, lmsg_ref, lpt_ref, subtree_out)
    w = w_ref[...]
    row = jnp.zeros((1, row_ref.shape[1]), F32)
    row = _counts(
        row, local_edges, w, vt, tarr_ref, tmsg_ref,
        lambda c: _dot(basis * jt_ref[c], tvw_ref[:, _cols(c, columns)]),
    )
    row = _counts(row, 0, w, vt, larr_ref, lmsg_ref, lambda c: lmixed_ref[c])
    row_ref[...] = _lane_put(row, local_edges + top_edges, jnp.sum(w, axis=1, keepdims=True))


def join(top_parents, pick, parents, gathered, tp, tpt, basis, j_top, vecs, inv, rf_col, w_row,
         lmsgs, lmixed, lpt, taxon_count):
    leaf_count, _, columns = gathered.shape
    top_edges = top_parents.shape[0]
    local_edges, states, _ = lmsgs.shape
    local_leaves = (local_edges + 2) // 2
    lanes = max(128, -(-(local_edges + top_edges + 1) // 128) * 128)
    return pl.pallas_call(
        functools.partial(_join_kernel, taxon_count=taxon_count),
        out_shape=(
            jax.ShapeDtypeStruct((1, lanes), F32),
            jax.ShapeDtypeStruct((1, columns), F32),
        ),
        in_specs=[SMEM] * 3 + [VMEM] * 12,
        out_specs=(VMEM, VMEM),
        scratch_shapes=[
            pltpu.VMEM((leaf_count - 1, states, columns), F32),
            pltpu.VMEM((top_edges, states, columns), F32),
            pltpu.VMEM((states, top_edges * columns), F32),
            pltpu.VMEM((states, top_edges * columns), F32),
            pltpu.VMEM((leaf_count - 1, states, columns), F32),
            pltpu.VMEM((states, top_edges * columns), F32),
            pltpu.VMEM((local_leaves - 1, states, columns), F32),
            pltpu.VMEM((states, local_edges * columns), F32),
            pltpu.SMEM((top_edges + 1,), jnp.int32),
            pltpu.SMEM((local_edges + 1,), jnp.int32),
        ],
        compiler_params=PARAMS,
    )(top_parents, pick, parents, gathered, tp, tpt, basis, j_top, vecs, inv, rf_col, w_row,
      lmsgs, lmixed, lpt)


def gather_roots(block, groups):
    buf = block[None]
    step = groups // 2
    while step >= 1:
        other = lax.ppermute(buf, "leaf", [(i, i ^ step) for i in range(groups)])
        buf = jnp.stack([buf, other], axis=1).reshape((-1,) + block.shape)
        step //= 2
    return buf


def on_device(
    tips,
    parents,
    branch_lengths,
    top_parents,
    top_lengths,
    weights,
    eig_vectors,
    eig_inverse,
    eig_values,
    labeled_rates,
    root_freq,
):
    local_edges = parents.shape[0]
    top_edges = top_parents.shape[0]
    groups = lax.axis_size("leaf")
    member_index = lax.axis_index("leaf")
    taxon_count = tips.shape[0] * groups
    lam_col = eig_values[:, None]

    root_block, msgs, xw, trl = climb(
        parents, branch_lengths, tips, eig_vectors, eig_inverse, lam_col
    )
    if groups & (groups - 1) == 0:
        gathered = gather_roots(root_block, groups)
        pick = jnp.reshape(member_index, (1,)).astype(jnp.int32)
    else:
        gathered = lax.all_gather(root_block, "leaf", axis=0, tiled=False)
        pick = jnp.zeros((1,), jnp.int32)
    j_local = jax.vmap(lambda t: integrals(eig_values, t))(branch_lengths)
    j_top = jax.vmap(lambda t: integrals(eig_values, t))(top_lengths)
    lmixed, lpt, tp, tpt, basis = matrices(
        top_lengths, eig_vectors, eig_inverse, labeled_rates, lam_col, j_local, xw, trl
    )
    w_row = weights.astype(F32)[None, :]
    row, loglik = join(
        top_parents, pick, parents, gathered, tp, tpt, basis, j_top, eig_vectors, eig_inverse,
        root_freq[:, None], w_row, msgs, lmixed, lpt, taxon_count,
    )
    sums = lax.psum(row[0], "site")
    weight_total = sums[local_edges + top_edges]
    return (
        sums[:local_edges] / weight_total,
        sums[local_edges:local_edges + top_edges] / weight_total,
        loglik[0],
    )


def solution(mesh):
    placed = (
        P("leaf", None, "site"),
        P("leaf"),
        P("leaf"),
        P(),
        P(),
        P("site"),
        P(),
        P(),
        P(),
        P(),
        P(),
    )
    return jax.shard_map(
        on_device,
        mesh=mesh,
        in_specs=placed,
        out_specs=(P("leaf"), P(), P("site")),
        check_vma=False,
    )
```

time: 61.9 us -> 50.4 us (0.81)
  Pallas kernels: 30.5 us -> 21.4 us
  waiting for transfers between devices: 6.79 us -> 4.23 us
    pallas_call x1, Pallas kernels: 14.3 us -> 4.64 us  [matrices(): pl.pallas_call(_matrix_kernel, out_shape=(jax.ShapeDtypeStruct((local_edg...]
    ppermute x4, waiting for transfers between devices: 6.79 us -> 4.23 us  [gather_roots(): other = lax.ppermute(buf, 'leaf', [(i, i ^ step) for i in range(groups)])]
    unnamed x14 -> x16, local copies, waits for them, and re-layouts: 2 us -> 2.55 us
  transfers between devices with their start and end apart: 4 -> 4, of which waited for: 3 -> 2; matrix products, arithmetic and copies ran while one was open for 7% -> 8% of each run, Pallas kernels for 23% -> 9%
where the time goes in v3:
time: 50.4 us; the launch traced here: 50.2 us
  Pallas kernels  21.4 us (42%)
  starting transfers between devices  7.32 us (15%)
  other arithmetic  5.94 us (12%)
  local copies, waits for them, and re-layouts  5.65 us (11%)
  blocking collectives  4.91 us (10%)
  waiting for transfers between devices  4.23 us (8%)
  between operations  0.72 us (1%)
    pallas_call x1, Pallas kernels, join(): pl.pallas_call(functools.partial(_join_kernel, taxon_count=taxon_count),...  12.9 us
    ppermute x4, starting transfers between devices, gather_roots(): other = lax.ppermute(buf, 'leaf', [(i, i ^ step) for i in range(groups)])  7.32 us
    psum x1, blocking collectives, on_device(): sums = lax.psum(row[0], 'site')  4.91 us
    pallas_call x1, Pallas kernels, matrices(): pl.pallas_call(_matrix_kernel, out_shape=(jax.ShapeDtypeStruct((local_edg...  4.64 us
    ppermute x4, waiting for transfers between devices, gather_roots(): other = lax.ppermute(buf, 'leaf', [(i, i ^ step) for i in range(groups)])  4.23 us
    pallas_call x1, Pallas kernels, climb(): pl.pallas_call(_climb_kernel, out_shape=(jax.ShapeDtypeStruct((states + 1...  3.89 us
    mul x4, other arithmetic, integrals(): return branch * jnp.exp(eig_values[None, :] * branch) * growth  2.98 us
    unnamed x16, local copies, waits for them, and re-layouts  2.55 us
  transfers between devices with their start and end apart: 4, of which 2 were waited for; matrix products, arithmetic and copies ran while one was open for 8% of the time, Pallas kernels for 9%

profile of v3, /device:TPU:0, one launch (start us, length us, event | category | flops | bytes accessed | tf_op | source)
XLA Modules:
  0.0 50.2 jit_solution(9924744661815606094)
XLA Ops:
  0.6 0.6 %copy-done.1 = f32[64]{0:T(128)S(1)} copy-done((f32[64]{0:T(128)S(1)}, f32[64]{0:T(128)}, u32[]{:S(2)}) %copy-start.1) | copy-done | bytes 280
  1.3 0.7 %copy.22.lam_ref = f32[64,1]{1,0:T(8,128)} copy(f32[64,1]{0,1:T(1,128)S(1)} %bitcast.34) | data formatting | bytes 512 | tf_op jit(solution)/shard_map/broadcast_in_dim | solution.py:291
  2.0 3.9 %shard_map.130 = (f32[65,128]{1,0:T(8,128)}, f32[14,64,128]{2,1,0:T(8,128)}, f32[64,1792]{1,0:T(8,128)}, f32[14,64,64]{2,1,0:T(8,128)}) custom-call(s32[14]{0:T(128)} %lpar_ref.1, f32[14]{0:T(128)} %len_ref.1, f32[8,64,128]{2,1,0:T(8,128)} %leaf_ref.1, f32[64,64]{1,0:T(8,128)} %v_ref.5, f32[64,64]{1,0:T(8,128)} %vi_ref.5, f32[64,1]{1,0:T(8,128)} %copy.22.lam_ref), custom_call_target="tpu_custom_call" | custom-call | tf_op jit(solution)/shard_map/pallas_call | solution.py:74
  5.9 4.1 %collective-permute-start = (f32[1,65,128]{2,1,0:T(8,128)}, f32[1,65,128]{2,1,0:T(8,128)S(1)}, u32[]{:S(2)}, u32[]{:S(2)}) collective-permute-start(f32[1,65,128]{2,1,0:T(8,128)} %bitcast.31), channel_id=1, source_target_pairs={{0,16},{2,18},{4,20},{6,22},{8,24},{10,26},{12,28},{14,30},{16,0},... | collective-permute-start | bytes 99848 | tf_op jit(solution)/shard_map/ppermute | solution.py:267
  10.0 0.1 broadcast_subtract_fusion
  10.1 0.1 exponential_multiply_fusion.1
  10.1 1.2 %fusion.11.jl_ref = f32[14,64,64]{2,1,0:T(8,128)} fusion(f32[14]{0:T(128)S(1)} %copy-done.4, f32[64,64]{1,0:T(8,128)S(1)} %broadcast_subtract_fusion, f32[14,64]{1,0:T(8,128)S(1)} %exponential_multiply_fusion.1), kind=kLoop, calls=%fused_computation.22 | loop fusion | flops 688128 | bytes 249400 | tf_op jit(solution)/shard_map/vmap()/mul | solution.py:30
  11.3 1.2 %collective-permute-done = f32[1,65,128]{2,1,0:T(8,128)S(1)} collective-permute-done((f32[1,65,128]{2,1,0:T(8,128)}, f32[1,65,128]{2,1,0:T(8,128)S(1)}, u32[]{:S(2)}, u32[]{:S(2)}) %collective-permute-start) | collective-permute-done | bytes 33312 | tf_op jit(solution)/shard_map/ppermute | solution.py:267
  12.6 0.0 copy-start.2
  12.6 1.6 %collective-permute-start.1 = (f32[2,65,128]{2,1,0:T(8,128)S(1)}, f32[2,65,128]{2,1,0:T(8,128)S(1)}, u32[]{:S(2)}, u32[]{:S(2)}) collective-permute-start(f32[2,65,128]{2,1,0:T(8,128)S(1)} %get-tuple-element.26), channel_id=1, source_target_pairs={{0,8},{2,10},{4,12},{6,14},{8,0},{10,2},{12,4},{14,6},{16,24},{18,... | collective-permute-start | bytes 199688 | tf_op jit(solution)/shard_map/ppermute | solution.py:267
  14.2 0.1 exponential_multiply_fusion
  14.2 0.7 %copy-done.5 = f32[64]{0:T(128)S(1)} copy-done((f32[64]{0:T(128)S(1)}, f32[64]{0:T(128)}, u32[]{:S(2)}) %copy-start.5) | copy-done | bytes 280
  14.9 0.7 %copy.29.rf_ref = f32[64,1]{1,0:T(8,128)} copy(f32[64,1]{0,1:T(1,128)S(1)} %bitcast.35) | data formatting | bytes 512 | tf_op jit(solution)/shard_map/broadcast_in_dim | solution.py:310
  15.6 4.6 %shard_map.131 = (f32[14,64,128]{2,1,0:T(8,128)}, f32[14,64,64]{2,1,0:T(8,128)}, f32[30,64,64]{2,1,0:T(8,128)}, f32[30,64,64]{2,1,0:T(8,128)}, f32[64,64]{1,0:T(8,128)}) custom-call(f32[30]{0:T(128)} %top_len_ref.1, f32[64,64]{1,0:T(8,128)} %v_ref.5, f32[64,64]{1,0:T(8,128)} %vi_ref.5, f32[64,64]{1,0:T(8,128)} %lab_ref.1, f32[64,1]{1,0:T(8,128)} %copy.22.lam_ref, ...), custom_call_target="tpu_custom_call" | custom-call | tf_op jit(solution)/shard_map/pallas_call | solution.py:113
  20.2 0.1 copy.23
  20.3 0.0 copy-start.6
  20.3 1.5 %collective-permute-start.2 = (f32[4,65,128]{2,0,1:T(4,128)S(1)}, f32[4,65,128]{2,0,1:T(4,128)S(1)}, u32[]{:S(2)}, u32[]{:S(2)}) collective-permute-start(f32[4,65,128]{2,0,1:T(4,128)S(1)} %bitcast.26), channel_id=1, source_target_pairs={{0,4},{2,6},{4,0},{6,2},{8,12},{10,14},{12,8},{14,10},{16,20},{18,... | collective-permute-start | bytes 399368 | tf_op jit(solution)/shard_map/ppermute | solution.py:267
  21.9 0.5 %convert_bitcast_fusion.w_ref = f32[1,128]{1,0:T(1,128)} fusion(s32[128]{0:T(128)S(1)} %copy-done.6), kind=kLoop, calls=%fused_computation.35 | loop fusion | flops 128 | bytes 1024 | tf_op jit(solution)/shard_map/broadcast_in_dim | solution.py:307
  22.4 3.0 %collective-permute-done.2 = f32[4,65,128]{2,0,1:T(4,128)S(1)} collective-permute-done((f32[4,65,128]{2,0,1:T(4,128)S(1)}, f32[4,65,128]{2,0,1:T(4,128)S(1)}, u32[]{:S(2)}, u32[]{:S(2)}) %collective-permute-start.2) | collective-permute-done | bytes 133152 | tf_op jit(solution)/shard_map/ppermute | solution.py:267
  25.4 0.1 pad_maximum_fusion.1
  25.5 0.1 copy.25
  25.6 0.1 collective-permute-start.3
  25.7 0.6 %copy-done.3 = f32[30]{0:T(128)S(1)} copy-done((f32[30]{0:T(128)S(1)}, f32[30]{0:T(128)}, u32[]{:S(2)}) %copy-start.3) | copy-done | bytes 144
  26.3 1.7 %fusion.4.jt_ref = f32[30,64,64]{2,1,0:T(8,128)} fusion(f32[30]{0:T(128)S(1)} %copy-done.3, f32[64,64]{1,0:T(8,128)S(1)} %broadcast_subtract_fusion, f32[30,64]{1,0:T(8,128)S(1)} %exponential_multiply_fusion), kind=kLoop, calls=%fused_computation.14 | loop fusion | flops 1474560 | bytes 515704 | tf_op jit(solution)/shard_map/vmap()/mul | solution.py:30
  27.9 0.1 pad_maximum_fusion
  28.0 0.9 %copy.27 = f32[8,2,65,128]{3,2,1,0:T(8,128)} copy(f32[8,2,65,128]{3,0,2,1:T(8,128)S(1)} %pad_maximum_fusion) | data formatting | bytes 1064960 | tf_op jit(solution)/shard_map/stack | solution.py:268
  28.9 12.9 %shard_map.132 = (f32[1,128]{1,0:T(1,128)}, f32[1,128]{1,0:T(1,128)}) custom-call(s32[30]{0:T(128)} %tpar_ref.1, s32[1]{0:T(128)} %bitcast.pick_ref, s32[14]{0:T(128)} %lpar_ref.1, f32[16,65,128]{2,1,0:T(8,128)} %bitcast.23, f32[30,64,64]{2,1,0:T(8,128)} %get-tuple-element.17.tp_ref, f32[30,64,64]{2,1,0:T(8,128)} %get-tuple-element.18.tpt_ref, ...), custom_call_target="tpu_custom_call" | custom-call | tf_op jit(solution)/shard_map/pallas_call | solution.py:238
  41.8 0.7 %copy-done.7 = f32[1,128]{1,0:T(1,128)S(1)} copy-done((f32[1,128]{1,0:T(1,128)S(1)}, f32[1,128]{1,0:T(1,128)}, u32[]{:S(2)}) %copy-start.7) | copy-done | bytes 536
  42.5 4.9 %psum.7 = f32[128]{0:T(128)S(1)} all-reduce(f32[128]{0:T(128)S(1)} %bitcast.37), channel_id=1, replica_groups=mesh['leaf'=16,'site'=2] {'site'}, use_global_device_ids=true, to_apply=%region_0.1 | all-reduce | flops 128 | bytes 1024 | tf_op jit(solution)/shard_map/psum | solution.py:312
  47.4 0.6 %slice.10 = f32[1]{0:T(128)} slice(f32[128]{0:T(128)S(1)} %psum.7), slice={[44:45]} | slice | bytes 8 | tf_op jit(solution)/shard_map/slice | solution.py:313
  48.0 1.1 %slice_divide_fusion = f32[30]{0:T(128)} fusion(f32[128]{0:T(128)S(1)} %psum.7, f32[]{:T(128)} %bitcast.18), kind=kLoop, calls=%fused_computation.33 | loop fusion | flops 30 | bytes 244 | tf_op jit(solution)/shard_map/div | solution.py:316
  49.1 1.1 %slice_divide_fusion.1 = f32[14]{0:T(128)} fusion(f32[128]{0:T(128)S(1)} %psum.7, f32[]{:T(128)} %bitcast.18), kind=kLoop, calls=%fused_computation.34 | loop fusion | flops 14 | bytes 116 | tf_op jit(solution)/shard_map/div | solution.py:315
  (14 shorter events, 0.1 us)
Async XLA Ops:
  0.6 0.7 %copy-start.1 = (f32[64]{0:T(128)S(1)}, f32[64]{0:T(128)}, u32[]{:S(2)}) copy-start(f32[64]{0:T(128)} %param.19) | copy-start | bytes 772
  5.9 4.2 %copy-start.4 = (f32[14]{0:T(128)S(1)}, f32[14]{0:T(128)}, u32[]{:S(2)}) copy-start(f32[14]{0:T(128)} %len_ref.1) | copy-start | bytes 172
  5.9 6.7 %collective-permute-start = (f32[1,65,128]{2,1,0:T(8,128)}, f32[1,65,128]{2,1,0:T(8,128)S(1)}, u32[]{:S(2)}, u32[]{:S(2)}) collective-permute-start(f32[1,65,128]{2,1,0:T(8,128)} %bitcast.31), channel_id=1, source_target_pairs={{0,16},{2,18},{4,20},{6,22},{8,24},{10,26},{12,28},{14,30},{16,0},... | collective-permute-start | bytes 99848 | tf_op jit(solution)/shard_map/ppermute | solution.py:267
  10.1 2.4 %copy-start = (f32[65,128]{1,0:T(8,128)S(1)}, f32[65,128]{1,0:T(8,128)}, u32[]{:S(2)}) copy-start(f32[65,128]{1,0:T(8,128)} %get-tuple-element.14) | copy-start | bytes 99844
  12.6 1.6 %copy-start.2 = (f32[30]{0:T(128)S(1)}, f32[30]{0:T(128)}, u32[]{:S(2)}) copy-start(f32[30]{0:T(128)} %top_len_ref.1) | copy-start | bytes 364
  12.6 7.7 %collective-permute-start.1 = (f32[2,65,128]{2,1,0:T(8,128)S(1)}, f32[2,65,128]{2,1,0:T(8,128)S(1)}, u32[]{:S(2)}, u32[]{:S(2)}) collective-permute-start(f32[2,65,128]{2,1,0:T(8,128)S(1)} %get-tuple-element.26), channel_id=1, source_target_pairs={{0,8},{2,10},{4,12},{6,14},{8,0},{10,2},{12,4},{14,6},{16,24},{18,... | collective-permute-start | bytes 199688 | tf_op jit(solution)/shard_map/ppermute | solution.py:267
  14.2 0.7 %copy-start.5 = (f32[64]{0:T(128)S(1)}, f32[64]{0:T(128)}, u32[]{:S(2)}) copy-start(f32[64]{0:T(128)} %param.21) | copy-start | bytes 772
  20.3 1.6 %copy-start.6 = (s32[128]{0:T(128)S(1)}, s32[128]{0:T(128)}, u32[]{:S(2)}) copy-start(s32[128]{0:T(128)} %param.16) | copy-start | bytes 1540
  20.3 5.1 %collective-permute-start.2 = (f32[4,65,128]{2,0,1:T(4,128)S(1)}, f32[4,65,128]{2,0,1:T(4,128)S(1)}, u32[]{:S(2)}, u32[]{:S(2)}) collective-permute-start(f32[4,65,128]{2,0,1:T(4,128)S(1)} %bitcast.26), channel_id=1, source_target_pairs={{0,4},{2,6},{4,0},{6,2},{8,12},{10,14},{12,8},{14,10},{16,20},{18,... | collective-permute-start | bytes 399368 | tf_op jit(solution)/shard_map/ppermute | solution.py:267
  25.6 0.7 %copy-start.3 = (f32[30]{0:T(128)S(1)}, f32[30]{0:T(128)}, u32[]{:S(2)}) copy-start(f32[30]{0:T(128)} %top_len_ref.1) | copy-start | bytes 364
  25.6 2.3 %collective-permute-start.3 = (f32[8,65,128]{2,0,1:T(8,128)S(1)}, f32[8,65,128]{2,0,1:T(8,128)S(1)}, u32[]{:S(2)}, u32[]{:S(2)}) collective-permute-start(f32[8,65,128]{2,0,1:T(8,128)S(1)} %bitcast.24), channel_id=1, source_target_pairs={{0,2},{2,0},{4,6},{6,4},{8,10},{10,8},{12,14},{14,12},{16,18},{18,... | collective-permute-start | bytes 798728 | tf_op jit(solution)/shard_map/ppermute | solution.py:267
  41.8 0.7 %copy-start.7 = (f32[1,128]{1,0:T(1,128)S(1)}, f32[1,128]{1,0:T(1,128)}, u32[]{:S(2)}) copy-start(f32[1,128]{1,0:T(1,128)} %get-tuple-element.23) | copy-start | bytes 1540

commit v4 on v3

--- a/solution.py
+++ b/solution.py
@@ -10,6 +10,7 @@
 CODONS = 61
 
 PRECISE = lax.Precision.HIGHEST
+FAST = lax.Precision.HIGH
 F32 = jnp.float32
 VMEM_LIMIT = 56 * 1024 * 1024
 VMEM = pl.BlockSpec(memory_space=pltpu.VMEM)
@@ -17,7 +18,7 @@
 
 
 def _dot(a, b):
-    return jnp.dot(a, b, precision=PRECISE, preferred_element_type=F32)
+    return jnp.dot(a, b, precision=FAST, preferred_element_type=F32)
 
 
 def integrals(eig_values, branch):

time: 50.4 us -> 46.8 us (0.929)
  Pallas kernels: 21.4 us -> 17.8 us
    pallas_call x1, Pallas kernels: 12.9 us -> 10.5 us  [join(): pl.pallas_call(functools.partial(_join_kernel, taxon_count=taxon_count),...]
    pallas_call x1, Pallas kernels: 4.64 us -> 3.81 us  [matrices(): pl.pallas_call(_matrix_kernel, out_shape=(jax.ShapeDtypeStruct((local_edg...]
  transfers between devices with their start and end apart: 4 -> 4, of which waited for: 2 -> 2; matrix products, arithmetic and copies ran while one was open for 8% -> 9% of each run, Pallas kernels for 9% -> 8%
where the time goes in v4:
time: 46.8 us; the launch traced here: 46.6 us
  Pallas kernels  17.8 us (38%)
  starting transfers between devices  7.32 us (16%)
  other arithmetic  5.94 us (13%)
  local copies, waits for them, and re-layouts  5.65 us (12%)
  blocking collectives  4.91 us (10%)
  waiting for transfers between devices  4.23 us (9%)
  between operations  0.72 us (2%)
    pallas_call x1, Pallas kernels, join(): pl.pallas_call(functools.partial(_join_kernel, taxon_count=taxon_count),...  10.5 us
    ppermute x4, starting transfers between devices, gather_roots(): other = lax.ppermute(buf, 'leaf', [(i, i ^ step) for i in range(groups)])  7.32 us
    psum x1, blocking collectives, on_device(): sums = lax.psum(row[0], 'site')  4.91 us
    ppermute x4, waiting for transfers between devices, gather_roots(): other = lax.ppermute(buf, 'leaf', [(i, i ^ step) for i in range(groups)])  4.23 us
    pallas_call x1, Pallas kernels, matrices(): pl.pallas_call(_matrix_kernel, out_shape=(jax.ShapeDtypeStruct((local_edg...  3.81 us
    pallas_call x1, Pallas kernels, climb(): pl.pallas_call(_climb_kernel, out_shape=(jax.ShapeDtypeStruct((states + 1...  3.48 us
    mul x4, other arithmetic, integrals(): return branch * jnp.exp(eig_values[None, :] * branch) * growth  2.98 us
    unnamed x16, local copies, waits for them, and re-layouts  2.55 us
  transfers between devices with their start and end apart: 4, of which 2 were waited for; matrix products, arithmetic and copies ran while one was open for 9% of the time, Pallas kernels for 8%

profile of v4, /device:TPU:0, one launch (start us, length us, event | category | flops | bytes accessed | tf_op | source)
XLA Modules:
  0.0 46.6 jit_solution(14162424248436185583)
XLA Ops:
  0.6 0.6 %copy-done.1 = f32[64]{0:T(128)S(1)} copy-done((f32[64]{0:T(128)S(1)}, f32[64]{0:T(128)}, u32[]{:S(2)}) %copy-start.1) | copy-done | bytes 280
  1.3 0.7 %copy.22.lam_ref = f32[64,1]{1,0:T(8,128)} copy(f32[64,1]{0,1:T(1,128)S(1)} %bitcast.34) | data formatting | bytes 512 | tf_op jit(solution)/shard_map/broadcast_in_dim | solution.py:292
  2.0 3.5 %shard_map.130 = (f32[65,128]{1,0:T(8,128)}, f32[14,64,128]{2,1,0:T(8,128)}, f32[64,1792]{1,0:T(8,128)}, f32[14,64,64]{2,1,0:T(8,128)}) custom-call(s32[14]{0:T(128)} %lpar_ref.1, f32[14]{0:T(128)} %len_ref.1, f32[8,64,128]{2,1,0:T(8,128)} %leaf_ref.1, f32[64,64]{1,0:T(8,128)} %v_ref.5, f32[64,64]{1,0:T(8,128)} %vi_ref.5, f32[64,1]{1,0:T(8,128)} %copy.22.lam_ref), custom_call_target="tpu_custom_call" | custom-call | tf_op jit(solution)/shard_map/pallas_call | solution.py:75
  5.5 4.1 %collective-permute-start = (f32[1,65,128]{2,1,0:T(8,128)}, f32[1,65,128]{2,1,0:T(8,128)S(1)}, u32[]{:S(2)}, u32[]{:S(2)}) collective-permute-start(f32[1,65,128]{2,1,0:T(8,128)} %bitcast.31), channel_id=1, source_target_pairs={{0,16},{2,18},{4,20},{6,22},{8,24},{10,26},{12,28},{14,30},{16,0},... | collective-permute-start | bytes 99848 | tf_op jit(solution)/shard_map/ppermute | solution.py:268
  9.6 0.1 broadcast_subtract_fusion
  9.7 0.1 exponential_multiply_fusion.1
  9.7 1.2 %fusion.11.jl_ref = f32[14,64,64]{2,1,0:T(8,128)} fusion(f32[14]{0:T(128)S(1)} %copy-done.4, f32[64,64]{1,0:T(8,128)S(1)} %broadcast_subtract_fusion, f32[14,64]{1,0:T(8,128)S(1)} %exponential_multiply_fusion.1), kind=kLoop, calls=%fused_computation.22 | loop fusion | flops 688128 | bytes 249400 | tf_op jit(solution)/shard_map/vmap()/mul | solution.py:31
  10.9 1.2 %collective-permute-done = f32[1,65,128]{2,1,0:T(8,128)S(1)} collective-permute-done((f32[1,65,128]{2,1,0:T(8,128)}, f32[1,65,128]{2,1,0:T(8,128)S(1)}, u32[]{:S(2)}, u32[]{:S(2)}) %collective-permute-start) | collective-permute-done | bytes 33312 | tf_op jit(solution)/shard_map/ppermute | solution.py:268
  12.2 0.0 copy-start.2
  12.2 1.6 %collective-permute-start.1 = (f32[2,65,128]{2,1,0:T(8,128)S(1)}, f32[2,65,128]{2,1,0:T(8,128)S(1)}, u32[]{:S(2)}, u32[]{:S(2)}) collective-permute-start(f32[2,65,128]{2,1,0:T(8,128)S(1)} %get-tuple-element.26), channel_id=1, source_target_pairs={{0,8},{2,10},{4,12},{6,14},{8,0},{10,2},{12,4},{14,6},{16,24},{18,... | collective-permute-start | bytes 199688 | tf_op jit(solution)/shard_map/ppermute | solution.py:268
  13.8 0.1 exponential_multiply_fusion
  13.8 0.7 %copy-done.5 = f32[64]{0:T(128)S(1)} copy-done((f32[64]{0:T(128)S(1)}, f32[64]{0:T(128)}, u32[]{:S(2)}) %copy-start.5) | copy-done | bytes 280
  14.5 0.7 %copy.29.rf_ref = f32[64,1]{1,0:T(8,128)} copy(f32[64,1]{0,1:T(1,128)S(1)} %bitcast.35) | data formatting | bytes 512 | tf_op jit(solution)/shard_map/broadcast_in_dim | solution.py:311
  15.2 3.8 %shard_map.131 = (f32[14,64,128]{2,1,0:T(8,128)}, f32[14,64,64]{2,1,0:T(8,128)}, f32[30,64,64]{2,1,0:T(8,128)}, f32[30,64,64]{2,1,0:T(8,128)}, f32[64,64]{1,0:T(8,128)}) custom-call(f32[30]{0:T(128)} %top_len_ref.1, f32[64,64]{1,0:T(8,128)} %v_ref.5, f32[64,64]{1,0:T(8,128)} %vi_ref.5, f32[64,64]{1,0:T(8,128)} %lab_ref.1, f32[64,1]{1,0:T(8,128)} %copy.22.lam_ref, ...), custom_call_target="tpu_custom_call" | custom-call | tf_op jit(solution)/shard_map/pallas_call | solution.py:114
  19.0 0.1 copy.23
  19.1 1.5 %collective-permute-start.2 = (f32[4,65,128]{2,0,1:T(4,128)S(1)}, f32[4,65,128]{2,0,1:T(4,128)S(1)}, u32[]{:S(2)}, u32[]{:S(2)}) collective-permute-start(f32[4,65,128]{2,0,1:T(4,128)S(1)} %bitcast.26), channel_id=1, source_target_pairs={{0,4},{2,6},{4,0},{6,2},{8,12},{10,14},{12,8},{14,10},{16,20},{18,... | collective-permute-start | bytes 399368 | tf_op jit(solution)/shard_map/ppermute | solution.py:268
  20.6 0.5 %convert_bitcast_fusion.w_ref = f32[1,128]{1,0:T(1,128)} fusion(s32[128]{0:T(128)S(1)} %copy-done.6), kind=kLoop, calls=%fused_computation.35 | loop fusion | flops 128 | bytes 1024 | tf_op jit(solution)/shard_map/broadcast_in_dim | solution.py:308
  21.2 3.0 %collective-permute-done.2 = f32[4,65,128]{2,0,1:T(4,128)S(1)} collective-permute-done((f32[4,65,128]{2,0,1:T(4,128)S(1)}, f32[4,65,128]{2,0,1:T(4,128)S(1)}, u32[]{:S(2)}, u32[]{:S(2)}) %collective-permute-start.2) | collective-permute-done | bytes 133152 | tf_op jit(solution)/shard_map/ppermute | solution.py:268
  24.2 0.1 pad_maximum_fusion.1
  24.2 0.1 copy.25
  24.4 0.0 copy-start.3
  24.4 0.1 collective-permute-start.3
  24.5 0.6 %copy-done.3 = f32[30]{0:T(128)S(1)} copy-done((f32[30]{0:T(128)S(1)}, f32[30]{0:T(128)}, u32[]{:S(2)}) %copy-start.3) | copy-done | bytes 144
  25.0 1.7 %fusion.4.jt_ref = f32[30,64,64]{2,1,0:T(8,128)} fusion(f32[30]{0:T(128)S(1)} %copy-done.3, f32[64,64]{1,0:T(8,128)S(1)} %broadcast_subtract_fusion, f32[30,64]{1,0:T(8,128)S(1)} %exponential_multiply_fusion), kind=kLoop, calls=%fused_computation.14 | loop fusion | flops 1474560 | bytes 515704 | tf_op jit(solution)/shard_map/vmap()/mul | solution.py:31
  26.7 0.1 pad_maximum_fusion
  26.8 0.9 %copy.27 = f32[8,2,65,128]{3,2,1,0:T(8,128)} copy(f32[8,2,65,128]{3,0,2,1:T(8,128)S(1)} %pad_maximum_fusion) | data formatting | bytes 1064960 | tf_op jit(solution)/shard_map/stack | solution.py:269
  27.7 10.5 %shard_map.132 = (f32[1,128]{1,0:T(1,128)}, f32[1,128]{1,0:T(1,128)}) custom-call(s32[30]{0:T(128)} %tpar_ref.1, s32[1]{0:T(128)} %bitcast.pick_ref, s32[14]{0:T(128)} %lpar_ref.1, f32[16,65,128]{2,1,0:T(8,128)} %bitcast.23, f32[30,64,64]{2,1,0:T(8,128)} %get-tuple-element.17.tp_ref, f32[30,64,64]{2,1,0:T(8,128)} %get-tuple-element.18.tpt_ref, ...), custom_call_target="tpu_custom_call" | custom-call | tf_op jit(solution)/shard_map/pallas_call | solution.py:239
  38.2 0.7 %copy-done.7 = f32[1,128]{1,0:T(1,128)S(1)} copy-done((f32[1,128]{1,0:T(1,128)S(1)}, f32[1,128]{1,0:T(1,128)}, u32[]{:S(2)}) %copy-start.7) | copy-done | bytes 536
  38.9 4.9 %psum.7 = f32[128]{0:T(128)S(1)} all-reduce(f32[128]{0:T(128)S(1)} %bitcast.37), channel_id=1, replica_groups=mesh['leaf'=16,'site'=2] {'site'}, use_global_device_ids=true, to_apply=%region_0.1 | all-reduce | flops 128 | bytes 1024 | tf_op jit(solution)/shard_map/psum | solution.py:313
  43.8 0.6 %slice.10 = f32[1]{0:T(128)} slice(f32[128]{0:T(128)S(1)} %psum.7), slice={[44:45]} | slice | bytes 8 | tf_op jit(solution)/shard_map/slice | solution.py:314
  44.4 1.1 %slice_divide_fusion = f32[30]{0:T(128)} fusion(f32[128]{0:T(128)S(1)} %psum.7, f32[]{:T(128)} %bitcast.18), kind=kLoop, calls=%fused_computation.33 | loop fusion | flops 30 | bytes 244 | tf_op jit(solution)/shard_map/div | solution.py:317
  45.5 1.1 %slice_divide_fusion.1 = f32[14]{0:T(128)} fusion(f32[128]{0:T(128)S(1)} %psum.7, f32[]{:T(128)} %bitcast.18), kind=kLoop, calls=%fused_computation.34 | loop fusion | flops 14 | bytes 116 | tf_op jit(solution)/shard_map/div | solution.py:316
  (14 shorter events, 0.1 us)
Async XLA Ops:
  0.6 0.7 %copy-start.1 = (f32[64]{0:T(128)S(1)}, f32[64]{0:T(128)}, u32[]{:S(2)}) copy-start(f32[64]{0:T(128)} %param.19) | copy-start | bytes 772
  5.5 4.2 %copy-start.4 = (f32[14]{0:T(128)S(1)}, f32[14]{0:T(128)}, u32[]{:S(2)}) copy-start(f32[14]{0:T(128)} %len_ref.1) | copy-start | bytes 172
  5.5 6.7 %collective-permute-start = (f32[1,65,128]{2,1,0:T(8,128)}, f32[1,65,128]{2,1,0:T(8,128)S(1)}, u32[]{:S(2)}, u32[]{:S(2)}) collective-permute-start(f32[1,65,128]{2,1,0:T(8,128)} %bitcast.31), channel_id=1, source_target_pairs={{0,16},{2,18},{4,20},{6,22},{8,24},{10,26},{12,28},{14,30},{16,0},... | collective-permute-start | bytes 99848 | tf_op jit(solution)/shard_map/ppermute | solution.py:268
  9.7 2.4 %copy-start = (f32[65,128]{1,0:T(8,128)S(1)}, f32[65,128]{1,0:T(8,128)}, u32[]{:S(2)}) copy-start(f32[65,128]{1,0:T(8,128)} %get-tuple-element.14) | copy-start | bytes 99844
  12.2 1.6 %copy-start.2 = (f32[30]{0:T(128)S(1)}, f32[30]{0:T(128)}, u32[]{:S(2)}) copy-start(f32[30]{0:T(128)} %top_len_ref.1) | copy-start | bytes 364
  12.2 6.8 %collective-permute-start.1 = (f32[2,65,128]{2,1,0:T(8,128)S(1)}, f32[2,65,128]{2,1,0:T(8,128)S(1)}, u32[]{:S(2)}, u32[]{:S(2)}) collective-permute-start(f32[2,65,128]{2,1,0:T(8,128)S(1)} %get-tuple-element.26), channel_id=1, source_target_pairs={{0,8},{2,10},{4,12},{6,14},{8,0},{10,2},{12,4},{14,6},{16,24},{18,... | collective-permute-start | bytes 199688 | tf_op jit(solution)/shard_map/ppermute | solution.py:268
  13.8 0.7 %copy-start.5 = (f32[64]{0:T(128)S(1)}, f32[64]{0:T(128)}, u32[]{:S(2)}) copy-start(f32[64]{0:T(128)} %param.21) | copy-start | bytes 772
  19.1 1.6 %copy-start.6 = (s32[128]{0:T(128)S(1)}, s32[128]{0:T(128)}, u32[]{:S(2)}) copy-start(s32[128]{0:T(128)} %param.16) | copy-start | bytes 1540
  19.1 5.1 %collective-permute-start.2 = (f32[4,65,128]{2,0,1:T(4,128)S(1)}, f32[4,65,128]{2,0,1:T(4,128)S(1)}, u32[]{:S(2)}, u32[]{:S(2)}) collective-permute-start(f32[4,65,128]{2,0,1:T(4,128)S(1)} %bitcast.26), channel_id=1, source_target_pairs={{0,4},{2,6},{4,0},{6,2},{8,12},{10,14},{12,8},{14,10},{16,20},{18,... | collective-permute-start | bytes 399368 | tf_op jit(solution)/shard_map/ppermute | solution.py:268
  24.4 0.7 %copy-start.3 = (f32[30]{0:T(128)S(1)}, f32[30]{0:T(128)}, u32[]{:S(2)}) copy-start(f32[30]{0:T(128)} %top_len_ref.1) | copy-start | bytes 364
  24.4 2.3 %collective-permute-start.3 = (f32[8,65,128]{2,0,1:T(8,128)S(1)}, f32[8,65,128]{2,0,1:T(8,128)S(1)}, u32[]{:S(2)}, u32[]{:S(2)}) collective-permute-start(f32[8,65,128]{2,0,1:T(8,128)S(1)} %bitcast.24), channel_id=1, source_target_pairs={{0,2},{2,0},{4,6},{6,4},{8,10},{10,8},{12,14},{14,12},{16,18},{18,... | collective-permute-start | bytes 798728 | tf_op jit(solution)/shard_map/ppermute | solution.py:268
  38.2 0.7 %copy-start.7 = (f32[1,128]{1,0:T(1,128)S(1)}, f32[1,128]{1,0:T(1,128)}, u32[]{:S(2)}) copy-start(f32[1,128]{1,0:T(1,128)} %get-tuple-element.23) | copy-start | bytes 1540

commit v5 on v4

--- a/solution.py
+++ b/solution.py
@@ -56,7 +56,7 @@
             big = jnp.max(x, axis=0, keepdims=True)
             x = x / big
             logs = logs + jnp.log(big)
-        trans = _dot(vecs, jnp.exp(lam * len_ref[c]) * inv)
+        trans = _dot(vecs * jnp.exp(lam * len_ref[c]), inv)
         tr_ref[c] = trans
         msg = _dot(trans, x)
         msg_ref[c] = msg
@@ -69,7 +69,7 @@
     root_ref[states:states + 1, :] = logs + jnp.log(big)
 
 
-def climb(parents, lengths, tips, vecs, inv, lam_col):
+def climb(parents, lengths, tips, vecs, inv, lam_row):
     leaf_count, states, columns = tips.shape
     edge_count = parents.shape[0]
     return pl.pallas_call(
@@ -84,7 +84,7 @@
         out_specs=(VMEM,) * 4,
         scratch_shapes=[pltpu.VMEM((leaf_count - 1, states, columns), F32)],
         compiler_params=PARAMS,
-    )(parents, lengths, tips, vecs, inv, lam_col)
+    )(parents, lengths, tips, vecs, inv, lam_row)
 
 
 def _matrix_kernel(top_len_ref, v_ref, vi_ref, lab_ref, lam_ref, jl_ref, xw_ref, trl_ref,
@@ -101,12 +101,12 @@
         mixed_ref[c] = _dot(basis * jl_ref[c], vw_ref[:, _cols(c, columns)])
         ptl_ref[c] = trl_ref[c].T
     for c in range(top_edges):
-        trans = _dot(vecs, jnp.exp(lam * top_len_ref[c]) * inv)
+        trans = _dot(vecs * jnp.exp(lam * top_len_ref[c]), inv)
         tp_ref[c] = trans
         tpt_ref[c] = trans.T
 
 
-def matrices(top_lengths, vecs, inv, labeled, lam_col, j_local, xw, trl):
+def matrices(top_lengths, vecs, inv, labeled, lam_row, j_local, xw, trl):
     local_edges, states, _ = trl.shape
     columns = xw.shape[1] // local_edges
     top_edges = top_lengths.shape[0]
@@ -124,7 +124,7 @@
         out_specs=(VMEM,) * 5,
         scratch_shapes=[pltpu.VMEM((states, local_edges * columns), F32)],
         compiler_params=PARAMS,
-    )(top_lengths, vecs, inv, labeled, lam_col, j_local, xw, trl)
+    )(top_lengths, vecs, inv, labeled, lam_row, j_local, xw, trl)
 
 
 def _lane_put(row, lane, value):
@@ -175,13 +175,13 @@
 
 
 def _join_kernel(tpar_ref, pick_ref, lpar_ref,
-                 gat_ref, tp_ref, tpt_ref, basis_ref, jt_ref, v_ref, vi_ref, rf_ref, w_ref,
-                 lmsg_ref, lmixed_ref, lpt_ref,
-                 row_ref, loglik_ref,
+                 gat0_ref, gat1_ref, tp_ref, tpt_ref, basis_ref, jt_ref, v_ref, vi_ref, rf_ref,
+                 w_ref, wo_ref, lmsg_ref, lmixed_ref, lpt_ref,
+                 local_ref, top_ref, loglik_ref,
                  tinner_ref, tmsg_ref, txw_ref, tvw_ref, toutside_ref, tarr_ref,
-                 loutside_ref, larr_ref, tkids_ref, lkids_ref, *, taxon_count):
+                 loutside_ref, larr_ref, tkids_ref, lkids_ref, *, taxon_count, paired):
     top_edges = tpar_ref.shape[0]
-    leaf_count = gat_ref.shape[0]
+    leaf_count = (top_edges + 2) // 2
     local_edges = lpar_ref.shape[0]
     states, columns = tmsg_ref.shape[1], tmsg_ref.shape[2]
     g = pick_ref[0]
@@ -190,7 +190,12 @@
     leaf_logs = jnp.zeros((1, columns), F32)
     for c in range(top_edges):
         if c < leaf_count:
-            block = gat_ref[jnp.bitwise_xor(c, g)]
+            if paired:
+                spot = jnp.bitwise_xor(c, g)
+                half = spot // 2
+                block = jnp.where(spot % 2 == 0, gat0_ref[half], gat1_ref[half])
+            else:
+                block = gat0_ref[c]
             x = block[0:states, :]
             leaf_logs = leaf_logs + block[states:states + 1, :]
         else:
@@ -207,43 +212,52 @@
     big = jnp.max(x, axis=0, keepdims=True)
     logs = logs + jnp.log(big)
     rf = rf_ref[...]
-    likelihood = jnp.sum(rf * (x / big), axis=0, keepdims=True)
+    likelihood = jnp.dot(rf, x / big, precision=PRECISE, preferred_element_type=F32)
     loglik_ref[...] = (jnp.log(likelihood) + logs + leaf_logs) / taxon_count
 
+    eye = (lax.broadcasted_iota(jnp.int32, (states, states), 0)
+           == lax.broadcasted_iota(jnp.int32, (states, states), 1))
+    rf_col = jnp.sum(jnp.where(eye, rf, 0.0), axis=1, keepdims=True)
     inv = vi_ref[...]
     vt = v_ref[...].T
     basis = basis_ref[...]
     tvw_ref[...] = _dot(inv, txw_ref[...])
     subtree_out = _descend(
         tpar_ref, tkids_ref, toutside_ref, tarr_ref, tmsg_ref, tpt_ref,
-        jnp.broadcast_to(rf, (states, columns)), pick=g,
+        jnp.broadcast_to(rf_col, (states, columns)), pick=g,
     )
     _descend(lpar_ref, lkids_ref, loutside_ref, larr_ref, lmsg_ref, lpt_ref, subtree_out)
     w = w_ref[...]
-    row = jnp.zeros((1, row_ref.shape[1]), F32)
+    weight_total = jnp.sum(w, axis=1, keepdims=True) + jnp.sum(wo_ref[...], axis=1, keepdims=True)
+    lanes = max(local_edges, top_edges)
+    row = jnp.zeros((1, lanes), F32)
     row = _counts(
-        row, local_edges, w, vt, tarr_ref, tmsg_ref,
+        row, 0, w, vt, tarr_ref, tmsg_ref,
         lambda c: _dot(basis * jt_ref[c], tvw_ref[:, _cols(c, columns)]),
     )
+    top_ref[...] = row[:, 0:top_edges] / weight_total
+    row = jnp.zeros((1, lanes), F32)
     row = _counts(row, 0, w, vt, larr_ref, lmsg_ref, lambda c: lmixed_ref[c])
-    row_ref[...] = _lane_put(row, local_edges + top_edges, jnp.sum(w, axis=1, keepdims=True))
-
-
-def join(top_parents, pick, parents, gathered, tp, tpt, basis, j_top, vecs, inv, rf_col, w_row,
-         lmsgs, lmixed, lpt, taxon_count):
-    leaf_count, _, columns = gathered.shape
+    local_ref[...] = row[:, 0:local_edges] / weight_total
+
+
+def join(top_parents, pick, parents, halves, tp, tpt, basis, j_top, vecs, inv, rf_row, w_row,
+         w_other, lmsgs, lmixed, lpt, taxon_count, paired):
+    gat0, gat1 = halves
+    columns = gat0.shape[2]
     top_edges = top_parents.shape[0]
+    leaf_count = (top_edges + 2) // 2
     local_edges, states, _ = lmsgs.shape
     local_leaves = (local_edges + 2) // 2
-    lanes = max(128, -(-(local_edges + top_edges + 1) // 128) * 128)
     return pl.pallas_call(
-        functools.partial(_join_kernel, taxon_count=taxon_count),
+        functools.partial(_join_kernel, taxon_count=taxon_count, paired=paired),
         out_shape=(
-            jax.ShapeDtypeStruct((1, lanes), F32),
+            jax.ShapeDtypeStruct((1, local_edges), F32),
+            jax.ShapeDtypeStruct((1, top_edges), F32),
             jax.ShapeDtypeStruct((1, columns), F32),
         ),
-        in_specs=[SMEM] * 3 + [VMEM] * 12,
-        out_specs=(VMEM, VMEM),
+        in_specs=[SMEM] * 3 + [VMEM] * 14,
+        out_specs=(VMEM, VMEM, VMEM),
         scratch_shapes=[
             pltpu.VMEM((leaf_count - 1, states, columns), F32),
             pltpu.VMEM((top_edges, states, columns), F32),
@@ -257,8 +271,8 @@
             pltpu.SMEM((local_edges + 1,), jnp.int32),
         ],
         compiler_params=PARAMS,
-    )(top_parents, pick, parents, gathered, tp, tpt, basis, j_top, vecs, inv, rf_col, w_row,
-      lmsgs, lmixed, lpt)
+    )(top_parents, pick, parents, gat0, gat1, tp, tpt, basis, j_top, vecs, inv, rf_row, w_row,
+      w_other, lmsgs, lmixed, lpt)
 
 
 def gather_roots(block, groups):
@@ -266,9 +280,11 @@
     step = groups // 2
     while step >= 1:
         other = lax.ppermute(buf, "leaf", [(i, i ^ step) for i in range(groups)])
+        if step == 1:
+            return buf, other
         buf = jnp.stack([buf, other], axis=1).reshape((-1,) + block.shape)
         step //= 2
-    return buf
+    return buf, buf
 
 
 def on_device(
@@ -284,39 +300,40 @@
     labeled_rates,
     root_freq,
 ):
-    local_edges = parents.shape[0]
-    top_edges = top_parents.shape[0]
     groups = lax.axis_size("leaf")
+    sites = lax.axis_size("site")
     member_index = lax.axis_index("leaf")
     taxon_count = tips.shape[0] * groups
-    lam_col = eig_values[:, None]
+    lam_row = eig_values[None, :]
+    w_row = weights.astype(F32)[None, :]
+    if sites == 2:
+        w_other = lax.ppermute(w_row, "site", [(0, 1), (1, 0)])
+    else:
+        w_other = lax.psum(jnp.sum(w_row), "site") - jnp.sum(w_row)
+        w_other = jnp.reshape(w_other, (1, 1))
 
     root_block, msgs, xw, trl = climb(
-        parents, branch_lengths, tips, eig_vectors, eig_inverse, lam_col
-    )
-    if groups & (groups - 1) == 0:
-        gathered = gather_roots(root_block, groups)
+        parents, branch_lengths, tips, eig_vectors, eig_inverse, lam_row
+    )
+    paired = groups & (groups - 1) == 0
+    if paired:
+        halves = gather_roots(root_block, groups)
         pick = jnp.reshape(member_index, (1,)).astype(jnp.int32)
     else:
         gathered = lax.all_gather(root_block, "leaf", axis=0, tiled=False)
+        halves = (gathered, gathered)
         pick = jnp.zeros((1,), jnp.int32)
     j_local = jax.vmap(lambda t: integrals(eig_values, t))(branch_lengths)
     j_top = jax.vmap(lambda t: integrals(eig_values, t))(top_lengths)
     lmixed, lpt, tp, tpt, basis = matrices(
-        top_lengths, eig_vectors, eig_inverse, labeled_rates, lam_col, j_local, xw, trl
-    )
-    w_row = weights.astype(F32)[None, :]
-    row, loglik = join(
-        top_parents, pick, parents, gathered, tp, tpt, basis, j_top, eig_vectors, eig_inverse,
-        root_freq[:, None], w_row, msgs, lmixed, lpt, taxon_count,
-    )
-    sums = lax.psum(row[0], "site")
-    weight_total = sums[local_edges + top_edges]
-    return (
-        sums[:local_edges] / weight_total,
-        sums[local_edges:local_edges + top_edges] / weight_total,
-        loglik[0],
-    )
+        top_lengths, eig_vectors, eig_inverse, labeled_rates, lam_row, j_local, xw, trl
+    )
+    local_row, top_row, loglik = join(
+        top_parents, pick, parents, halves, tp, tpt, basis, j_top, eig_vectors, eig_inverse,
+        root_freq[None, :], w_row, w_other, msgs, lmixed, lpt, taxon_count, paired,
+    )
+    local_sum, top_sum = lax.psum((local_row[0], top_row[0]), "site")
+    return (local_sum, top_sum, loglik[0])
 
 
 def solution(mesh):

time: 46.8 us -> 43.8 us (0.936)
  local copies, waits for them, and re-layouts: 5.65 us -> 1.5 us
  other arithmetic: 5.94 us -> 3.18 us
  starting transfers between devices: 7.32 us -> 9.11 us
  waiting for transfers between devices: 4.23 us -> 5.67 us
  blocking collectives: 4.91 us -> 5.41 us
    div x2 -> x0, other arithmetic: 2.22 us -> none  [the longest x1 1.14 us: on_device(): sums[local_edges:local_edges + top_edges] / weight_total]
    ppermute x0 -> x1, starting transfers between devices: none -> 1.59 us  [on_device(): w_other = lax.ppermute(w_row, 'site', [(0, 1), (1, 0)])]
    ppermute x4, waiting for transfers between devices: 4.23 us -> 5.67 us  [gather_roots(): other = lax.ppermute(buf, 'leaf', [(i, i ^ step) for i in range(groups)])]
    broadcast_in_dim x2 -> x0, local copies, waits for them, and re-layouts: 1.39 us -> none  [the longest x1 0.7 us: on_device(): lam_col = eig_values[:, None]]
    unnamed x16 -> x22, local copies, waits for them, and re-layouts: 2.55 us -> 1.4 us
    another operation x3 -> x2, local copies, waits for them, and re-layouts: 1.13 us -> 0.09 us  [gather_roots(): buf = jnp.stack([buf, other], axis=1).reshape((-1,) + block.shape)]
    slice x1 -> x0, local copies, waits for them, and re-layouts: 0.59 us -> none  [on_device(): weight_total = sums[local_edges + top_edges]]
    broadcast_in_dim x1, other arithmetic: 0.51 us -> 0.01 us  [on_device(): w_row = weights.astype(F32)[None, :]]
  transfers between devices with their start and end apart: 4 -> 5, of which waited for: 2 -> 3; matrix products, arithmetic and copies ran while one was open for 9% -> 8% of each run, Pallas kernels for 8% -> 9%
where the time goes in v5:
time: 43.8 us; the launch traced here: 43.6 us
  Pallas kernels  18 us (41%)
  starting transfers between devices  9.11 us (21%)
  waiting for transfers between devices  5.67 us (13%)
  blocking collectives  5.41 us (12%)
  other arithmetic  3.18 us (7%)
  local copies, waits for them, and re-layouts  1.5 us (3%)
  between operations  0.75 us (2%)
    pallas_call x1, Pallas kernels, join(): pl.pallas_call(functools.partial(_join_kernel, taxon_count=taxon_count, p...  10.7 us
    ppermute x4, starting transfers between devices, gather_roots(): other = lax.ppermute(buf, 'leaf', [(i, i ^ step) for i in range(groups)])  7.52 us
    ppermute x4, waiting for transfers between devices, gather_roots(): other = lax.ppermute(buf, 'leaf', [(i, i ^ step) for i in range(groups)])  5.67 us
    psum x1, blocking collectives, on_device(): local_sum, top_sum = lax.psum((local_row[0], top_row[0]), 'site')  5.41 us
    pallas_call x1, Pallas kernels, matrices(): pl.pallas_call(_matrix_kernel, out_shape=(jax.ShapeDtypeStruct((local_edg...  3.77 us
    pallas_call x1, Pallas kernels, climb(): pl.pallas_call(_climb_kernel, out_shape=(jax.ShapeDtypeStruct((states + 1...  3.44 us
    mul x4, other arithmetic, integrals(): return branch * jnp.exp(eig_values[None, :] * branch) * growth  3.02 us
    ppermute x1, starting transfers between devices, on_device(): w_other = lax.ppermute(w_row, 'site', [(0, 1), (1, 0)])  1.59 us
  transfers between devices with their start and end apart: 5, of which 3 were waited for; matrix products, arithmetic and copies ran while one was open for 8% of the time, Pallas kernels for 9%

profile of v5, /device:TPU:0, one launch (start us, length us, event | category | flops | bytes accessed | tf_op | source)
XLA Modules:
  0.0 43.6 jit_solution(10441972767567296148)
XLA Ops:
  0.6 0.0 copy-start.8
  0.6 0.0 copy-start.3
  0.7 3.4 %shard_map.130 = (f32[65,128]{1,0:T(8,128)}, f32[14,64,128]{2,1,0:T(8,128)}, f32[64,1792]{1,0:T(8,128)}, f32[14,64,64]{2,1,0:T(8,128)}) custom-call(s32[14]{0:T(128)} %lpar_ref.1, f32[14]{0:T(128)} %len_ref.1, f32[8,64,128]{2,1,0:T(8,128)} %leaf_ref.1, f32[64,64]{1,0:T(8,128)} %v_ref.5, f32[64,64]{1,0:T(8,128)} %vi_ref.5, f32[1,64]{1,0:T(1,128)} %bitcast.29), custom_call_target="tpu_custom_call" | custom-call | tf_op jit(solution)/shard_map/pallas_call | solution.py:75
  4.1 4.1 %collective-permute-start = (f32[1,65,128]{2,1,0:T(8,128)}, f32[1,65,128]{2,1,0:T(8,128)S(1)}, u32[]{:S(2)}, u32[]{:S(2)}) collective-permute-start(f32[1,65,128]{2,1,0:T(8,128)} %bitcast.26), channel_id=1, source_target_pairs={{0,16},{2,18},{4,20},{6,22},{8,24},{10,26},{12,28},{14,30},{16,0},... | collective-permute-start | bytes 99848 | tf_op jit(solution)/shard_map/ppermute | solution.py:282
  8.2 1.6 %collective-permute-start.4 = (f32[1,128]{1,0:T(1,128)S(1)}, f32[1,128]{1,0:T(1,128)S(1)}, u32[]{:S(2)}, u32[]{:S(2)}) collective-permute-start(f32[1,128]{1,0:T(1,128)S(1)} %convert_bitcast_fusion.w_ref), channel_id=1, source_target_pairs={{0,1},{1,0},{2,3},{3,2},{4,5},{5,4},{6,7},{7,6},{8,9},{9,8},{10,11... | collective-permute-start | bytes 1544 | tf_op jit(solution)/shard_map/ppermute | solution.py:310
  9.8 0.0 copy-done.3
  9.8 0.1 broadcast_subtract_fusion
  9.9 0.0 copy-done.6
  9.9 0.1 exponential_multiply_fusion.1
  10.0 0.8 %collective-permute-done = f32[1,65,128]{2,1,0:T(8,128)S(1)} collective-permute-done((f32[1,65,128]{2,1,0:T(8,128)}, f32[1,65,128]{2,1,0:T(8,128)S(1)}, u32[]{:S(2)}, u32[]{:S(2)}) %collective-permute-start) | collective-permute-done | bytes 33312 | tf_op jit(solution)/shard_map/ppermute | solution.py:282
  10.8 1.6 %collective-permute-start.1 = (f32[2,65,128]{2,1,0:T(8,128)S(1)}, f32[2,65,128]{2,1,0:T(8,128)S(1)}, u32[]{:S(2)}, u32[]{:S(2)}) collective-permute-start(f32[2,65,128]{2,1,0:T(8,128)S(1)} %get-tuple-element.30), channel_id=1, source_target_pairs={{0,8},{2,10},{4,12},{6,14},{8,0},{10,2},{12,4},{14,6},{16,24},{18,... | collective-permute-start | bytes 199688 | tf_op jit(solution)/shard_map/ppermute | solution.py:282
  12.4 1.2 %fusion.11.jl_ref = f32[14,64,64]{2,1,0:T(8,128)} fusion(f32[14]{0:T(128)S(1)} %copy-done.5, f32[64,64]{1,0:T(8,128)S(1)} %broadcast_subtract_fusion, f32[14,64]{1,0:T(8,128)S(1)} %exponential_multiply_fusion.1), kind=kLoop, calls=%fused_computation.21 | loop fusion | flops 688128 | bytes 249400 | tf_op jit(solution)/shard_map/vmap()/mul | solution.py:31
  13.5 1.7 %collective-permute-done.1 = f32[2,65,128]{2,1,0:T(8,128)S(1)} collective-permute-done((f32[2,65,128]{2,1,0:T(8,128)S(1)}, f32[2,65,128]{2,1,0:T(8,128)S(1)}, u32[]{:S(2)}, u32[]{:S(2)}) %collective-permute-start.1) | collective-permute-done | bytes 66592 | tf_op jit(solution)/shard_map/ppermute | solution.py:282
  15.2 0.1 copy.14
  15.3 0.0 copy-start.4
  15.3 1.8 %collective-permute-start.2 = (f32[4,65,128]{2,0,1:T(4,128)S(1)}, f32[4,65,128]{2,0,1:T(4,128)S(1)}, u32[]{:S(2)}, u32[]{:S(2)}) collective-permute-start(f32[4,65,128]{2,0,1:T(4,128)S(1)} %bitcast.22), channel_id=1, source_target_pairs={{0,4},{2,6},{4,0},{6,2},{8,12},{10,14},{12,8},{14,10},{16,20},{18,... | collective-permute-start | bytes 399368 | tf_op jit(solution)/shard_map/ppermute | solution.py:282
  17.1 0.1 exponential_multiply_fusion
  17.1 3.2 %collective-permute-done.2 = f32[4,65,128]{2,0,1:T(4,128)S(1)} collective-permute-done((f32[4,65,128]{2,0,1:T(4,128)S(1)}, f32[4,65,128]{2,0,1:T(4,128)S(1)}, u32[]{:S(2)}, u32[]{:S(2)}) %collective-permute-start.2) | collective-permute-done | bytes 133152 | tf_op jit(solution)/shard_map/ppermute | solution.py:282
  20.4 0.1 pad_maximum_fusion
  20.5 0.1 collective-permute-start.3
  20.5 1.7 %fusion.4.jt_ref = f32[30,64,64]{2,1,0:T(8,128)} fusion(f32[30]{0:T(128)S(1)} %copy-done.4, f32[64,64]{1,0:T(8,128)S(1)} %broadcast_subtract_fusion, f32[30,64]{1,0:T(8,128)S(1)} %exponential_multiply_fusion), kind=kLoop, calls=%fused_computation.14 | loop fusion | flops 1474560 | bytes 515704 | tf_op jit(solution)/shard_map/vmap()/mul | solution.py:31
  22.2 0.0 copy-done
  22.2 3.8 %shard_map.131 = (f32[14,64,128]{2,1,0:T(8,128)}, f32[14,64,64]{2,1,0:T(8,128)}, f32[30,64,64]{2,1,0:T(8,128)}, f32[30,64,64]{2,1,0:T(8,128)}, f32[64,64]{1,0:T(8,128)}) custom-call(f32[30]{0:T(128)} %top_len_ref.1, f32[64,64]{1,0:T(8,128)} %v_ref.5, f32[64,64]{1,0:T(8,128)} %vi_ref.5, f32[64,64]{1,0:T(8,128)} %lab_ref.1, f32[1,64]{1,0:T(1,128)} %bitcast.30, ...), custom_call_target="tpu_custom_call" | custom-call | tf_op jit(solution)/shard_map/pallas_call | solution.py:114
  26.0 0.0 collective-permute-done.4.wo_ref
  26.0 0.0 collective-permute-done.3.gat1_ref
  26.0 0.0 copy-start.1
  26.0 0.6 %copy-done.7 = f32[1,128]{1,0:T(1,128)} copy-done((f32[1,128]{1,0:T(1,128)}, f32[1,128]{1,0:T(1,128)S(1)}, u32[]{:S(2)}) %copy-start.7) | copy-done | bytes 536
  26.6 0.1 copy-done.1
  26.7 10.7 %shard_map.132 = (f32[1,14]{1,0:T(1,128)}, f32[1,30]{1,0:T(1,128)}, f32[1,128]{1,0:T(1,128)}) custom-call(s32[30]{0:T(128)} %tpar_ref.1, s32[1]{0:T(128)} %bitcast.pick_ref, s32[14]{0:T(128)} %lpar_ref.1, f32[8,65,128]{2,1,0:T(8,128)} %bitcast.21, f32[8,65,128]{2,1,0:T(8,128)} %copy-done.1, f32[30,64,64]{2,1,0:T(8,128)} %get-tuple-element.18.tp_ref, ...), custom_call_target="tpu_custom_call" | custom-call | tf_op jit(solution)/shard_map/pallas_call | solution.py:252
  37.5 0.6 %copy-done.9 = f32[1,14]{1,0:T(1,128)S(1)} copy-done((f32[1,14]{1,0:T(1,128)S(1)}, f32[1,14]{1,0:T(1,128)}, u32[]{:S(2)}) %copy-start.9) | copy-done | bytes 80
  38.1 0.0 copy-done.10
  38.2 5.4 %all-reduce = (f32[14]{0:T(128)}, f32[30]{0:T(128)}) all-reduce(f32[14]{0:T(128)S(1)} %bitcast.33, f32[30]{0:T(128)S(1)} %bitcast.34), channel_id=1, replica_groups=mesh['leaf'=16,'site'=2] {'site'}, use_global_device_ids=true, to_apply=%region_0.1 | all-reduce | flops 44 | bytes 352 | tf_op jit(solution)/shard_map/psum | solution.py:335
  (15 shorter events, 0.1 us)
Async XLA Ops:
  0.6 7.6 %copy-start.8 = (s32[128]{0:T(128)S(1)}, s32[128]{0:T(128)}, u32[]{:S(2)}) copy-start(s32[128]{0:T(128)} %param.16) | copy-start | bytes 1540
  0.6 9.2 %copy-start.3 = (f32[64]{0:T(128)S(1)}, f32[64]{0:T(128)}, u32[]{:S(2)}) copy-start(f32[64]{0:T(128)} %param.19) | copy-start | bytes 772
  4.1 6.7 %copy-start.2 = (f32[65,128]{1,0:T(8,128)S(1)}, f32[65,128]{1,0:T(8,128)}, u32[]{:S(2)}) copy-start(f32[65,128]{1,0:T(8,128)} %get-tuple-element.15) | copy-start | bytes 99844
  4.1 6.7 %collective-permute-start = (f32[1,65,128]{2,1,0:T(8,128)}, f32[1,65,128]{2,1,0:T(8,128)S(1)}, u32[]{:S(2)}, u32[]{:S(2)}) collective-permute-start(f32[1,65,128]{2,1,0:T(8,128)} %bitcast.26), channel_id=1, source_target_pairs={{0,16},{2,18},{4,20},{6,22},{8,24},{10,26},{12,28},{14,30},{16,0},... | collective-permute-start | bytes 99848 | tf_op jit(solution)/shard_map/ppermute | solution.py:282
  8.2 1.7 %copy-start.6 = (f32[1,128]{1,0:T(1,128)}, f32[1,128]{1,0:T(1,128)S(1)}, u32[]{:S(2)}) copy-start(f32[1,128]{1,0:T(1,128)S(1)} %convert_bitcast_fusion.w_ref) | copy-start | bytes 1540
  8.2 1.7 %copy-start.5 = (f32[14]{0:T(128)S(1)}, f32[14]{0:T(128)}, u32[]{:S(2)}) copy-start(f32[14]{0:T(128)} %len_ref.1) | copy-start | bytes 172
  8.2 17.8 %collective-permute-start.4 = (f32[1,128]{1,0:T(1,128)S(1)}, f32[1,128]{1,0:T(1,128)S(1)}, u32[]{:S(2)}, u32[]{:S(2)}) collective-permute-start(f32[1,128]{1,0:T(1,128)S(1)} %convert_bitcast_fusion.w_ref), channel_id=1, source_target_pairs={{0,1},{1,0},{2,3},{3,2},{4,5},{5,4},{6,7},{7,6},{8,9},{9,8},{10,11... | collective-permute-start | bytes 1544 | tf_op jit(solution)/shard_map/ppermute | solution.py:310
  10.8 4.4 %collective-permute-start.1 = (f32[2,65,128]{2,1,0:T(8,128)S(1)}, f32[2,65,128]{2,1,0:T(8,128)S(1)}, u32[]{:S(2)}, u32[]{:S(2)}) collective-permute-start(f32[2,65,128]{2,1,0:T(8,128)S(1)} %get-tuple-element.30), channel_id=1, source_target_pairs={{0,8},{2,10},{4,12},{6,14},{8,0},{10,2},{12,4},{14,6},{16,24},{18,... | collective-permute-start | bytes 199688 | tf_op jit(solution)/shard_map/ppermute | solution.py:282
  15.3 1.8 %copy-start.4 = (f32[30]{0:T(128)S(1)}, f32[30]{0:T(128)}, u32[]{:S(2)}) copy-start(f32[30]{0:T(128)} %top_len_ref.1) | copy-start | bytes 364
  15.3 5.1 %collective-permute-start.2 = (f32[4,65,128]{2,0,1:T(4,128)S(1)}, f32[4,65,128]{2,0,1:T(4,128)S(1)}, u32[]{:S(2)}, u32[]{:S(2)}) collective-permute-start(f32[4,65,128]{2,0,1:T(4,128)S(1)} %bitcast.22), channel_id=1, source_target_pairs={{0,4},{2,6},{4,0},{6,2},{8,12},{10,14},{12,8},{14,10},{16,20},{18,... | collective-permute-start | bytes 399368 | tf_op jit(solution)/shard_map/ppermute | solution.py:282
  20.5 1.8 %copy-start = (f32[4,2,65,128]{3,2,1,0:T(8,128)}, f32[4,2,65,128]{3,2,1,0:T(8,128)S(1)}, u32[]{:S(2)}) copy-start(f32[4,2,65,128]{3,2,1,0:T(8,128)S(1)} %copy.16) | copy-start | bytes 798724
  20.5 5.5 %collective-permute-start.3 = (f32[8,65,128]{2,1,0:T(8,128)S(1)}, f32[8,65,128]{2,1,0:T(8,128)S(1)}, u32[]{:S(2)}, u32[]{:S(2)}) collective-permute-start(f32[8,65,128]{2,1,0:T(8,128)S(1)} %bitcast.20), channel_id=1, source_target_pairs={{0,2},{2,0},{4,6},{6,4},{8,10},{10,8},{12,14},{14,12},{16,18},{18,... | collective-permute-start | bytes 798728 | tf_op jit(solution)/shard_map/ppermute | solution.py:282
  26.0 0.6 %copy-start.7 = (f32[1,128]{1,0:T(1,128)}, f32[1,128]{1,0:T(1,128)S(1)}, u32[]{:S(2)}) copy-start(f32[1,128]{1,0:T(1,128)S(1)} %collective-permute-done.4.wo_ref) | copy-start | bytes 1540
  26.0 0.7 %copy-start.1 = (f32[8,65,128]{2,1,0:T(8,128)}, f32[8,65,128]{2,1,0:T(8,128)S(1)}, u32[]{:S(2)}) copy-start(f32[8,65,128]{2,1,0:T(8,128)S(1)} %collective-permute-done.3.gat1_ref) | copy-start | bytes 798724
  37.5 0.6 %copy-start.9 = (f32[1,14]{1,0:T(1,128)S(1)}, f32[1,14]{1,0:T(1,128)}, u32[]{:S(2)}) copy-start(f32[1,14]{1,0:T(1,128)} %get-tuple-element.24) | copy-start | bytes 172
  37.5 0.7 %copy-start.10 = (f32[1,30]{1,0:T(1,128)S(1)}, f32[1,30]{1,0:T(1,128)}, u32[]{:S(2)}) copy-start(f32[1,30]{1,0:T(1,128)} %get-tuple-element.25) | copy-start | bytes 364

commit v6 on v5

--- a/solution.py
+++ b/solution.py
@@ -87,44 +87,69 @@
     )(parents, lengths, tips, vecs, inv, lam_row)
 
 
-def _matrix_kernel(top_len_ref, v_ref, vi_ref, lab_ref, lam_ref, jl_ref, xw_ref, trl_ref,
-                   mixed_ref, ptl_ref, tp_ref, tpt_ref, basis_ref, vw_ref):
+def _local_matrix_kernel(v_ref, vi_ref, lab_ref, jl_ref, xw_ref, trl_ref, w_ref, wo_ref,
+                         mixed_ref, ptl_ref, basis_ref, token_ref, wt_ref, vw_ref):
     local_edges, states, columns = mixed_ref.shape
-    top_edges = tp_ref.shape[0]
+    token_ref[...] = jnp.zeros(token_ref.shape, F32)
+    wt_ref[...] = (jnp.sum(w_ref[...], axis=1, keepdims=True)
+                   + jnp.sum(wo_ref[...], axis=1, keepdims=True))
     vecs = v_ref[...]
     inv = vi_ref[...]
-    lam = lam_ref[...]
     basis = _dot(_dot(inv, lab_ref[...]), vecs)
     basis_ref[...] = basis
     vw_ref[...] = _dot(inv, xw_ref[...])
     for c in range(local_edges):
         mixed_ref[c] = _dot(basis * jl_ref[c], vw_ref[:, _cols(c, columns)])
         ptl_ref[c] = trl_ref[c].T
+
+
+def local_matrices(vecs, inv, labeled, j_local, xw, trl, w_row, w_other):
+    local_edges, states, _ = trl.shape
+    columns = xw.shape[1] // local_edges
+    sq = (states, states)
+    return pl.pallas_call(
+        _local_matrix_kernel,
+        out_shape=(
+            jax.ShapeDtypeStruct((local_edges, states, columns), F32),
+            jax.ShapeDtypeStruct((local_edges,) + sq, F32),
+            jax.ShapeDtypeStruct(sq, F32),
+            jax.ShapeDtypeStruct((1, 1), F32),
+            jax.ShapeDtypeStruct((1, 1), F32),
+        ),
+        in_specs=[VMEM] * 8,
+        out_specs=(VMEM,) * 5,
+        scratch_shapes=[pltpu.VMEM((states, local_edges * columns), F32)],
+        compiler_params=PARAMS,
+    )(vecs, inv, labeled, j_local, xw, trl, w_row, w_other)
+
+
+def _top_matrix_kernel(top_len_ref, v_ref, vi_ref, lam_ref, tp_ref, tpt_ref, token_ref):
+    top_edges = tp_ref.shape[0]
+    token_ref[...] = jnp.zeros(token_ref.shape, F32)
+    vecs = v_ref[...]
+    inv = vi_ref[...]
+    lam = lam_ref[...]
     for c in range(top_edges):
         trans = _dot(vecs * jnp.exp(lam * top_len_ref[c]), inv)
         tp_ref[c] = trans
         tpt_ref[c] = trans.T
 
 
-def matrices(top_lengths, vecs, inv, labeled, lam_row, j_local, xw, trl):
-    local_edges, states, _ = trl.shape
-    columns = xw.shape[1] // local_edges
+def top_matrices(top_lengths, vecs, inv, lam_row):
     top_edges = top_lengths.shape[0]
+    states = vecs.shape[0]
     sq = (states, states)
     return pl.pallas_call(
-        _matrix_kernel,
+        _top_matrix_kernel,
         out_shape=(
-            jax.ShapeDtypeStruct((local_edges, states, columns), F32),
-            jax.ShapeDtypeStruct((local_edges,) + sq, F32),
             jax.ShapeDtypeStruct((top_edges,) + sq, F32),
             jax.ShapeDtypeStruct((top_edges,) + sq, F32),
-            jax.ShapeDtypeStruct(sq, F32),
+            jax.ShapeDtypeStruct((1, 1), F32),
         ),
-        in_specs=[SMEM] + [VMEM] * 7,
-        out_specs=(VMEM,) * 5,
-        scratch_shapes=[pltpu.VMEM((states, local_edges * columns), F32)],
+        in_specs=[SMEM] + [VMEM] * 3,
+        out_specs=(VMEM,) * 3,
         compiler_params=PARAMS,
-    )(top_lengths, vecs, inv, labeled, lam_row, j_local, xw, trl)
+    )(top_lengths, vecs, inv, lam_row)
 
 
 def _lane_put(row, lane, value):
@@ -228,7 +253,7 @@
     )
     _descend(lpar_ref, lkids_ref, loutside_ref, larr_ref, lmsg_ref, lpt_ref, subtree_out)
     w = w_ref[...]
-    weight_total = jnp.sum(w, axis=1, keepdims=True) + jnp.sum(wo_ref[...], axis=1, keepdims=True)
+    weight_total = wo_ref[...]
     lanes = max(local_edges, top_edges)
     row = jnp.zeros((1, lanes), F32)
     row = _counts(
@@ -275,7 +300,7 @@
       w_other, lmsgs, lmixed, lpt)
 
 
-def gather_roots(block, groups):
+def gather_roots(block, groups, tokens):
     buf = block[None]
     step = groups // 2
     while step >= 1:
@@ -284,6 +309,8 @@
             return buf, other
         buf = jnp.stack([buf, other], axis=1).reshape((-1,) + block.shape)
         step //= 2
+        if step in tokens:
+            buf = buf + tokens[step]
     return buf, buf
 
 
@@ -316,21 +343,27 @@
         parents, branch_lengths, tips, eig_vectors, eig_inverse, lam_row
     )
     paired = groups & (groups - 1) == 0
+    j_local = jax.vmap(lambda t: integrals(eig_values, t))(branch_lengths)
+    j_top = jax.vmap(lambda t: integrals(eig_values, t))(top_lengths)
+    tp, tpt, top_token = top_matrices(top_lengths, eig_vectors, eig_inverse, lam_row)
+    lmixed, lpt, basis, local_token, weight_total = local_matrices(
+        eig_vectors, eig_inverse, labeled_rates, j_local, xw, trl, w_row, w_other
+    )
     if paired:
-        halves = gather_roots(root_block, groups)
+        tokens = {
+            groups // 4: j_top[0, 0, 0] * 0.0,
+            groups // 8: top_token[0, 0],
+            1: local_token[0, 0],
+        }
+        halves = gather_roots(root_block, groups, tokens)
         pick = jnp.reshape(member_index, (1,)).astype(jnp.int32)
     else:
         gathered = lax.all_gather(root_block, "leaf", axis=0, tiled=False)
         halves = (gathered, gathered)
         pick = jnp.zeros((1,), jnp.int32)
-    j_local = jax.vmap(lambda t: integrals(eig_values, t))(branch_lengths)
-    j_top = jax.vmap(lambda t: integrals(eig_values, t))(top_lengths)
-    lmixed, lpt, tp, tpt, basis = matrices(
-        top_lengths, eig_vectors, eig_inverse, labeled_rates, lam_row, j_local, xw, trl
-    )
     local_row, top_row, loglik = join(
         top_parents, pick, parents, halves, tp, tpt, basis, j_top, eig_vectors, eig_inverse,
-        root_freq[None, :], w_row, w_other, msgs, lmixed, lpt, taxon_count, paired,
+        root_freq[None, :], w_row, weight_total, msgs, lmixed, lpt, taxon_count, paired,
     )
     local_sum, top_sum = lax.psum((local_row[0], top_row[0]), "site")
     return (local_sum, top_sum, loglik[0])

time: 43.8 us -> 45.1 us (1.030)
  waiting for transfers between devices: 5.67 us -> 1.98 us
  Pallas kernels: 18 us -> 20.3 us
  local copies, waits for them, and re-layouts: 1.5 us -> 2.58 us
  other arithmetic: 3.18 us -> 4.13 us
  between operations: 0.75 us -> 1.4 us
    ppermute x4, waiting for transfers between devices: 5.67 us -> 1.97 us  [gather_roots(): other = lax.ppermute(buf, 'leaf', [(i, i ^ step) for i in range(groups)])]
    pallas_call x1 -> x2, Pallas kernels: 3.77 us -> 5.57 us  [the longest x1 2.92 us: local_matrices(): pl.pallas_call(_local_matrix_kernel, out_shape=(jax.ShapeDtypeStruct((loc...]
    ppermute x4, starting transfers between devices: 7.52 us -> 5.95 us  [gather_roots(): other = lax.ppermute(buf, 'leaf', [(i, i ^ step) for i in range(groups)])]
    ppermute x1, starting transfers between devices: 1.59 us -> 3 us  [on_device(): w_other = lax.ppermute(w_row, 'site', [(0, 1), (1, 0)])]
    add x0 -> x3, other arithmetic: none -> 1.38 us  [gather_roots(): buf = buf + tokens[step]]
    mul x4, other arithmetic: 3.02 us -> 2.02 us  [integrals(): return branch * jnp.exp(eig_values[None, :] * branch) * growth]
    broadcast_in_dim x1, other arithmetic: 0.01 us -> 0.66 us  [on_device(): w_row = weights.astype(F32)[None, :]]
    pallas_call x1, Pallas kernels: 10.7 us -> 11.3 us  [join(): pl.pallas_call(functools.partial(_join_kernel, taxon_count=taxon_count, p...]
  transfers between devices with their start and end apart: 5 -> 5, of which waited for: 3 -> 2; matrix products, arithmetic and copies ran while one was open for 8% -> 8% of each run, Pallas kernels for 9% -> 20%
where the time goes in v6:
time: 45.1 us; the launch traced here: 44.8 us
  Pallas kernels  20.3 us (45%)
  starting transfers between devices  8.94 us (20%)
  blocking collectives  5.41 us (12%)
  other arithmetic  4.13 us (9%)
  local copies, waits for them, and re-layouts  2.58 us (6%)
  waiting for transfers between devices  1.98 us (4%)
  between operations  1.4 us (3%)
    pallas_call x1, Pallas kernels, join(): pl.pallas_call(functools.partial(_join_kernel, taxon_count=taxon_count, p...  11.3 us
    ppermute x4, starting transfers between devices, gather_roots(): other = lax.ppermute(buf, 'leaf', [(i, i ^ step) for i in range(groups)])  5.95 us
    psum x1, blocking collectives, on_device(): local_sum, top_sum = lax.psum((local_row[0], top_row[0]), 'site')  5.41 us
    pallas_call x1, Pallas kernels, climb(): pl.pallas_call(_climb_kernel, out_shape=(jax.ShapeDtypeStruct((states + 1...  3.41 us
    ppermute x1, starting transfers between devices, on_device(): w_other = lax.ppermute(w_row, 'site', [(0, 1), (1, 0)])  3 us
    pallas_call x1, Pallas kernels, local_matrices(): pl.pallas_call(_local_matrix_kernel, out_shape=(jax.ShapeDtypeStruct((loc...  2.92 us
    pallas_call x1, Pallas kernels, top_matrices(): pl.pallas_call(_top_matrix_kernel, out_shape=(jax.ShapeDtypeStruct((top_e...  2.65 us
    mul x4, other arithmetic, integrals(): return branch * jnp.exp(eig_values[None, :] * branch) * growth  2.02 us
  transfers between devices with their start and end apart: 5, of which 2 were waited for; matrix products, arithmetic and copies ran while one was open for 8% of the time, Pallas kernels for 20%

profile of v6, /device:TPU:0, one launch (start us, length us, event | category | flops | bytes accessed | tf_op | source)
XLA Modules:
  0.0 44.8 jit_solution(12840482725809197267)
XLA Ops:
  0.6 0.7 %convert_bitcast_fusion.w_ref = f32[1,128]{1,0:T(1,128)S(1)} fusion(s32[128]{0:T(128)} %param.16), kind=kLoop, calls=%fused_computation.32 | loop fusion | flops 128 | bytes 1024 | tf_op jit(solution)/shard_map/broadcast_in_dim | solution.py:335
  1.3 3.0 %collective-permute-start.3 = (f32[1,128]{1,0:T(1,128)S(1)}, f32[1,128]{1,0:T(1,128)S(1)}, u32[]{:S(2)}, u32[]{:S(2)}) collective-permute-start(f32[1,128]{1,0:T(1,128)S(1)} %convert_bitcast_fusion.w_ref), channel_id=1, source_target_pairs={{0,1},{1,0},{2,3},{3,2},{4,5},{5,4},{6,7},{7,6},{8,9},{9,8},{10,11... | collective-permute-start | bytes 1544 | tf_op jit(solution)/shard_map/ppermute | solution.py:337
  4.3 3.4 %shard_map.130 = (f32[65,128]{1,0:T(8,128)}, f32[14,64,128]{2,1,0:T(8,128)}, f32[64,1792]{1,0:T(8,128)}, f32[14,64,64]{2,1,0:T(8,128)}) custom-call(s32[14]{0:T(128)} %lpar_ref.1, f32[14]{0:T(128)} %len_ref.1, f32[8,64,128]{2,1,0:T(8,128)} %leaf_ref.1, f32[64,64]{1,0:T(8,128)} %v_ref.7, f32[64,64]{1,0:T(8,128)} %vi_ref.7, f32[1,64]{1,0:T(1,128)} %bitcast.32), custom_call_target="tpu_custom_call" | custom-call | tf_op jit(solution)/shard_map/pallas_call | solution.py:75
  7.7 2.7 %collective-permute-start = (f32[1,65,128]{2,1,0:T(8,128)}, f32[1,65,128]{2,1,0:T(8,128)S(1)}, u32[]{:S(2)}, u32[]{:S(2)}) collective-permute-start(f32[1,65,128]{2,1,0:T(8,128)} %bitcast.29), channel_id=1, source_target_pairs={{0,16},{2,18},{4,20},{6,22},{8,24},{10,26},{12,28},{14,30},{16,0},... | collective-permute-start | bytes 99848 | tf_op jit(solution)/shard_map/ppermute | solution.py:307
  10.4 0.1 broadcast_subtract_fusion
  10.4 0.1 exponential_multiply_fusion
  10.5 0.0 copy-start.3
  10.5 0.7 %fusion.4.jt_ref = f32[30,64,64]{2,1,0:T(8,128)S(1)} fusion(f32[30]{0:T(128)S(1)} %copy-done.5, f32[64,64]{1,0:T(8,128)S(1)} %broadcast_subtract_fusion, f32[30,64]{1,0:T(8,128)S(1)} %exponential_multiply_fusion), kind=kLoop, calls=%fused_computation.14 | loop fusion | flops 1474560 | bytes 515704 | tf_op jit(solution)/shard_map/vmap()/mul | solution.py:31
  11.3 0.6 %slice.4 = f32[1,1,1]{2,1,0:T(1,128)} slice(f32[30,64,64]{2,1,0:T(8,128)S(1)} %fusion.4.jt_ref), slice={[0:1], [0:1], [0:1]} | slice | bytes 8 | tf_op jit(solution)/shard_map/slice | solution.py:354
  12.5 0.4 collective-permute-done
  12.9 0.0 copy-start.6
  12.9 1.7 %collective-permute-start.1 = (f32[2,65,128]{2,1,0:T(8,128)S(1)}, f32[2,65,128]{2,1,0:T(8,128)S(1)}, u32[]{:S(2)}, u32[]{:S(2)}) collective-permute-start(f32[2,65,128]{2,1,0:T(8,128)S(1)} %get-tuple-element.36), channel_id=1, source_target_pairs={{0,8},{2,10},{4,12},{6,14},{8,0},{10,2},{12,4},{14,6},{16,24},{18,... | collective-permute-start | bytes 199688 | tf_op jit(solution)/shard_map/ppermute | solution.py:307
  14.5 0.1 exponential_multiply_fusion.1
  14.6 2.7 %shard_map.131 = (f32[30,64,64]{2,1,0:T(8,128)}, f32[30,64,64]{2,1,0:T(8,128)}, f32[1,1]{1,0:T(1,128)}) custom-call(f32[30]{0:T(128)} %top_len_ref.1, f32[64,64]{1,0:T(8,128)} %v_ref.7, f32[64,64]{1,0:T(8,128)} %vi_ref.7, f32[1,64]{1,0:T(1,128)} %bitcast.33), custom_call_target="tpu_custom_call" | custom-call | tf_op jit(solution)/shard_map/pallas_call | solution.py:142
  17.3 0.0 collective-permute-done.1
  17.3 0.7 %maximum_add_fusion.1 = f32[2,2,65,128]{3,2,0,1:T(8,128)S(1)} fusion(f32[2,1,65,128]{3,2,0,1:T(8,128)S(1)} %bitcast.28, f32[2,1,65,128]{3,2,0,1:T(8,128)S(1)} %get-tuple-element.35, f32[]{:T(128)} %bitcast.9), kind=kLoop, calls=%fused_computation.25 | loop fusion | flops 66560 | bytes 266244 | tf_op jit(solution)/shard_map/add | solution.py:313
  18.0 0.1 copy.14
  18.0 1.6 %collective-permute-start.2 = (f32[4,65,128]{2,0,1:T(4,128)S(1)}, f32[4,65,128]{2,0,1:T(4,128)S(1)}, u32[]{:S(2)}, u32[]{:S(2)}) collective-permute-start(f32[4,65,128]{2,0,1:T(4,128)S(1)} %bitcast.25), channel_id=1, source_target_pairs={{0,4},{2,6},{4,0},{6,2},{8,12},{10,14},{12,8},{14,10},{16,20},{18,... | collective-permute-start | bytes 399368 | tf_op jit(solution)/shard_map/ppermute | solution.py:307
  19.6 1.2 %fusion.11.jl_ref = f32[14,64,64]{2,1,0:T(8,128)} fusion(f32[14]{0:T(128)S(1)} %copy-done.6, f32[64,64]{1,0:T(8,128)S(1)} %broadcast_subtract_fusion, f32[14,64]{1,0:T(8,128)S(1)} %exponential_multiply_fusion.1), kind=kLoop, calls=%fused_computation.21 | loop fusion | flops 688128 | bytes 249400 | tf_op jit(solution)/shard_map/vmap()/mul | solution.py:31
  20.8 0.0 collective-permute-done.3.wo_ref
  20.8 0.5 %copy-done.8 = f32[1,128]{1,0:T(1,128)} copy-done((f32[1,128]{1,0:T(1,128)}, f32[1,128]{1,0:T(1,128)S(1)}, u32[]{:S(2)}) %copy-start.8) | copy-done | bytes 536
  21.3 2.9 %shard_map.132 = (f32[14,64,128]{2,1,0:T(8,128)}, f32[14,64,64]{2,1,0:T(8,128)}, f32[64,64]{1,0:T(8,128)}, f32[1,1]{1,0:T(1,128)}, f32[1,1]{1,0:T(1,128)}) custom-call(f32[64,64]{1,0:T(8,128)} %v_ref.7, f32[64,64]{1,0:T(8,128)} %vi_ref.7, f32[64,64]{1,0:T(8,128)} %lab_ref.1, f32[14,64,64]{2,1,0:T(8,128)} %fusion.11.jl_ref, ...), custom_call_target="tpu_custom_call" | custom-call | tf_op jit(solution)/shard_map/pallas_call | solution.py:110
  24.2 0.0 copy-done
  24.2 0.0 collective-permute-done.2
  24.2 0.7 %maximum_add_fusion = f32[4,2,65,128]{3,0,2,1:T(4,128)S(1)} fusion(f32[4,1,65,128]{3,0,2,1:T(4,128)S(1)} %bitcast.27, f32[4,1,65,128]{3,0,2,1:T(4,128)S(1)} %bitcast.26, f32[]{:T(128)} %bitcast.14), kind=kLoop, calls=%fused_computation.24 | loop fusion | flops 133120 | bytes 532484 | tf_op jit(solution)/shard_map/add | solution.py:313
  25.0 0.1 collective-permute-start.4
  25.1 1.6 %collective-permute-done.4.gat1_ref = f32[8,65,128]{2,1,0:T(8,128)S(1)} collective-permute-done((f32[8,65,128]{2,1,0:T(8,128)S(1)}, f32[8,65,128]{2,1,0:T(8,128)S(1)}, u32[]{:S(2)}, u32[]{:S(2)}) %collective-permute-start.4) | collective-permute-done | bytes 266272 | tf_op jit(solution)/shard_map/ppermute | solution.py:307
  26.6 0.7 %copy-done.2 = f32[8,65,128]{2,1,0:T(8,128)} copy-done((f32[8,65,128]{2,1,0:T(8,128)}, f32[8,65,128]{2,1,0:T(8,128)S(1)}, u32[]{:S(2)}) %copy-start.2) | copy-done | bytes 266264
  27.3 11.3 %shard_map.133 = (f32[1,14]{1,0:T(1,128)}, f32[1,30]{1,0:T(1,128)}, f32[1,128]{1,0:T(1,128)}) custom-call(s32[30]{0:T(128)} %tpar_ref.1, s32[1]{0:T(128)} %bitcast.pick_ref, s32[14]{0:T(128)} %lpar_ref.1, f32[8,65,128]{2,1,0:T(8,128)} %bitcast.24, f32[8,65,128]{2,1,0:T(8,128)} %copy-done.2, f32[30,64,64]{2,1,0:T(8,128)} %get-tuple-element.23.tp_ref, ...), custom_call_target="tpu_custom_call" | custom-call | tf_op jit(solution)/shard_map/pallas_call | solution.py:277
  38.7 0.6 %copy-done.9 = f32[1,14]{1,0:T(1,128)S(1)} copy-done((f32[1,14]{1,0:T(1,128)S(1)}, f32[1,14]{1,0:T(1,128)}, u32[]{:S(2)}) %copy-start.9) | copy-done | bytes 80
  39.3 0.0 copy-done.10
  39.3 5.4 %all-reduce = (f32[14]{0:T(128)}, f32[30]{0:T(128)}) all-reduce(f32[14]{0:T(128)S(1)} %bitcast.36, f32[30]{0:T(128)S(1)} %bitcast.37), channel_id=1, replica_groups=mesh['leaf'=16,'site'=2] {'site'}, use_global_device_ids=true, to_apply=%region_0.1 | all-reduce | flops 44 | bytes 352 | tf_op jit(solution)/shard_map/psum | solution.py:368
  (17 shorter events, 0.1 us)
Async XLA Ops:
  1.3 3.0 %copy-start.7 = (f32[1,128]{1,0:T(1,128)}, f32[1,128]{1,0:T(1,128)S(1)}, u32[]{:S(2)}) copy-start(f32[1,128]{1,0:T(1,128)S(1)} %convert_bitcast_fusion.w_ref) | copy-start | bytes 1540
  1.3 19.5 %collective-permute-start.3 = (f32[1,128]{1,0:T(1,128)S(1)}, f32[1,128]{1,0:T(1,128)S(1)}, u32[]{:S(2)}, u32[]{:S(2)}) collective-permute-start(f32[1,128]{1,0:T(1,128)S(1)} %convert_bitcast_fusion.w_ref), channel_id=1, source_target_pairs={{0,1},{1,0},{2,3},{3,2},{4,5},{5,4},{6,7},{7,6},{8,9},{9,8},{10,11... | collective-permute-start | bytes 1544 | tf_op jit(solution)/shard_map/ppermute | solution.py:337
  7.7 2.7 %copy-start.4 = (f32[64]{0:T(128)S(1)}, f32[64]{0:T(128)}, u32[]{:S(2)}) copy-start(f32[64]{0:T(128)} %param.19) | copy-start | bytes 772
  7.7 2.7 %copy-start.5 = (f32[30]{0:T(128)S(1)}, f32[30]{0:T(128)}, u32[]{:S(2)}) copy-start(f32[30]{0:T(128)} %top_len_ref.1) | copy-start | bytes 364
  7.7 5.1 %collective-permute-start = (f32[1,65,128]{2,1,0:T(8,128)}, f32[1,65,128]{2,1,0:T(8,128)S(1)}, u32[]{:S(2)}, u32[]{:S(2)}) collective-permute-start(f32[1,65,128]{2,1,0:T(8,128)} %bitcast.29), channel_id=1, source_target_pairs={{0,16},{2,18},{4,20},{6,22},{8,24},{10,26},{12,28},{14,30},{16,0},... | collective-permute-start | bytes 99848 | tf_op jit(solution)/shard_map/ppermute | solution.py:307
  10.5 2.3 %copy-start.3 = (f32[65,128]{1,0:T(8,128)S(1)}, f32[65,128]{1,0:T(8,128)}, u32[]{:S(2)}) copy-start(f32[65,128]{1,0:T(8,128)} %get-tuple-element.18) | copy-start | bytes 99844
  11.3 13.0 %copy-start = (f32[30,64,64]{2,1,0:T(8,128)}, f32[30,64,64]{2,1,0:T(8,128)S(1)}, u32[]{:S(2)}) copy-start(f32[30,64,64]{2,1,0:T(8,128)S(1)} %fusion.4.jt_ref) | copy-start | bytes 1474564
  12.9 1.7 %copy-start.6 = (f32[14]{0:T(128)S(1)}, f32[14]{0:T(128)}, u32[]{:S(2)}) copy-start(f32[14]{0:T(128)} %len_ref.1) | copy-start | bytes 172
  12.9 4.4 %collective-permute-start.1 = (f32[2,65,128]{2,1,0:T(8,128)S(1)}, f32[2,65,128]{2,1,0:T(8,128)S(1)}, u32[]{:S(2)}, u32[]{:S(2)}) collective-permute-start(f32[2,65,128]{2,1,0:T(8,128)S(1)} %get-tuple-element.36), channel_id=1, source_target_pairs={{0,8},{2,10},{4,12},{6,14},{8,0},{10,2},{12,4},{14,6},{16,24},{18,... | collective-permute-start | bytes 199688 | tf_op jit(solution)/shard_map/ppermute | solution.py:307
  18.0 6.2 %collective-permute-start.2 = (f32[4,65,128]{2,0,1:T(4,128)S(1)}, f32[4,65,128]{2,0,1:T(4,128)S(1)}, u32[]{:S(2)}, u32[]{:S(2)}) collective-permute-start(f32[4,65,128]{2,0,1:T(4,128)S(1)} %bitcast.25), channel_id=1, source_target_pairs={{0,4},{2,6},{4,0},{6,2},{8,12},{10,14},{12,8},{14,10},{16,20},{18,... | collective-permute-start | bytes 399368 | tf_op jit(solution)/shard_map/ppermute | solution.py:307
  20.8 0.5 %copy-start.8 = (f32[1,128]{1,0:T(1,128)}, f32[1,128]{1,0:T(1,128)S(1)}, u32[]{:S(2)}) copy-start(f32[1,128]{1,0:T(1,128)S(1)} %collective-permute-done.3.wo_ref) | copy-start | bytes 1540
  25.0 1.7 %copy-start.1 = (f32[4,2,65,128]{3,2,1,0:T(8,128)}, f32[4,2,65,128]{3,2,1,0:T(8,128)S(1)}, u32[]{:S(2)}) copy-start(f32[4,2,65,128]{3,2,1,0:T(8,128)S(1)} %copy.16) | copy-start | bytes 798724
  25.0 1.6 %collective-permute-start.4 = (f32[8,65,128]{2,1,0:T(8,128)S(1)}, f32[8,65,128]{2,1,0:T(8,128)S(1)}, u32[]{:S(2)}, u32[]{:S(2)}) collective-permute-start(f32[8,65,128]{2,1,0:T(8,128)S(1)} %bitcast.23), channel_id=1, source_target_pairs={{0,2},{2,0},{4,6},{6,4},{8,10},{10,8},{12,14},{14,12},{16,18},{18,... | collective-permute-start | bytes 798728 | tf_op jit(solution)/shard_map/ppermute | solution.py:307
  26.6 0.7 %copy-start.2 = (f32[8,65,128]{2,1,0:T(8,128)}, f32[8,65,128]{2,1,0:T(8,128)S(1)}, u32[]{:S(2)}) copy-start(f32[8,65,128]{2,1,0:T(8,128)S(1)} %collective-permute-done.4.gat1_ref) | copy-start | bytes 798724
  38.7 0.6 %copy-start.9 = (f32[1,14]{1,0:T(1,128)S(1)}, f32[1,14]{1,0:T(1,128)}, u32[]{:S(2)}) copy-start(f32[1,14]{1,0:T(1,128)} %get-tuple-element.30) | copy-start | bytes 172
  38.7 0.7 %copy-start.10 = (f32[1,30]{1,0:T(1,128)S(1)}, f32[1,30]{1,0:T(1,128)}, u32[]{:S(2)}) copy-start(f32[1,30]{1,0:T(1,128)} %get-tuple-element.31) | copy-start | bytes 364

commit v7 on v6

--- a/solution.py
+++ b/solution.py
@@ -157,10 +157,9 @@
     return jnp.where(lanes == lane, value, row)
 
 
-def _descend(par_ref, kids_ref, outside_ref, arr_ref, msg_ref, pt_ref, root_out, pick=None):
+def _descend(par_ref, kids_ref, outside_ref, msg_ref, pt_ref, root_out, count, row, pick=None):
     edge_count = par_ref.shape[0]
     leaf_count = (edge_count + 2) // 2
-    columns = msg_ref.shape[2]
     for n in range(edge_count + 1):
         kids_ref[n] = 0
     for e in range(edge_count):
@@ -179,37 +178,37 @@
 
     for c in range(edge_count - 1, -1, -1):
         arriving = arriving_of(c)
-        arr_ref[:, _cols(c, columns)] = arriving
         if c >= leaf_count:
             outside_ref[c - leaf_count] = outward(c, arriving)
+        row = count(c, arriving, row)
     if pick is not None:
-        return outward(pick, arriving_of(pick))
-    return None
-
-
-def _counts(row, lane_offset, w, vt, arr_ref, msg_ref, mixed_of):
-    edge_count, _, columns = msg_ref.shape
-    weighted = _dot(vt, arr_ref[...])
-    for c in range(edge_count):
-        cols = _cols(c, columns)
-        num = jnp.sum(weighted[:, cols] * mixed_of(c), axis=0, keepdims=True)
-        den = jnp.sum(arr_ref[:, cols] * msg_ref[c], axis=0, keepdims=True)
+        return row, outward(pick, arriving_of(pick))
+    return row, None
+
+
+def _count_fn(w, vt, weight_total, msg_ref, mixed_ref):
+    def count(c, arriving, row):
+        weighted = _dot(vt, arriving)
+        num = jnp.sum(weighted * mixed_ref[c], axis=0, keepdims=True)
+        den = jnp.sum(arriving * msg_ref[c], axis=0, keepdims=True)
         total = jnp.sum(w * num / den, axis=1, keepdims=True)
-        row = _lane_put(row, lane_offset + c, total)
-    return row
+        return _lane_put(row, c, total / weight_total)
+    return count
 
 
 def _join_kernel(tpar_ref, pick_ref, lpar_ref,
                  gat0_ref, gat1_ref, tp_ref, tpt_ref, basis_ref, jt_ref, v_ref, vi_ref, rf_ref,
                  w_ref, wo_ref, lmsg_ref, lmixed_ref, lpt_ref,
                  local_ref, top_ref, loglik_ref,
-                 tinner_ref, tmsg_ref, txw_ref, tvw_ref, toutside_ref, tarr_ref,
-                 loutside_ref, larr_ref, tkids_ref, lkids_ref, *, taxon_count, paired):
+                 tinner_ref, tmsg_ref, tmixed_ref, toutside_ref,
+                 loutside_ref, tkids_ref, lkids_ref, *, taxon_count, paired):
     top_edges = tpar_ref.shape[0]
     leaf_count = (top_edges + 2) // 2
     local_edges = lpar_ref.shape[0]
     states, columns = tmsg_ref.shape[1], tmsg_ref.shape[2]
     g = pick_ref[0]
+    inv = vi_ref[...]
+    basis = basis_ref[...]
     tinner_ref[...] = jnp.ones(tinner_ref.shape, F32)
     logs = jnp.zeros((1, columns), F32)
     leaf_logs = jnp.zeros((1, columns), F32)
@@ -230,9 +229,9 @@
             logs = logs + jnp.log(big)
         msg = _dot(tp_ref[c], x)
         tmsg_ref[c] = msg
-        txw_ref[:, _cols(c, columns)] = x
         p = tpar_ref[c] - leaf_count
         tinner_ref[p] = tinner_ref[p] * msg
+        tmixed_ref[c] = _dot(basis * jt_ref[c], _dot(inv, x))
     x = tinner_ref[leaf_count - 2]
     big = jnp.max(x, axis=0, keepdims=True)
     logs = logs + jnp.log(big)
@@ -243,27 +242,21 @@
     eye = (lax.broadcasted_iota(jnp.int32, (states, states), 0)
            == lax.broadcasted_iota(jnp.int32, (states, states), 1))
     rf_col = jnp.sum(jnp.where(eye, rf, 0.0), axis=1, keepdims=True)
-    inv = vi_ref[...]
     vt = v_ref[...].T
-    basis = basis_ref[...]
-    tvw_ref[...] = _dot(inv, txw_ref[...])
-    subtree_out = _descend(
-        tpar_ref, tkids_ref, toutside_ref, tarr_ref, tmsg_ref, tpt_ref,
-        jnp.broadcast_to(rf_col, (states, columns)), pick=g,
-    )
-    _descend(lpar_ref, lkids_ref, loutside_ref, larr_ref, lmsg_ref, lpt_ref, subtree_out)
     w = w_ref[...]
     weight_total = wo_ref[...]
     lanes = max(local_edges, top_edges)
-    row = jnp.zeros((1, lanes), F32)
-    row = _counts(
-        row, 0, w, vt, tarr_ref, tmsg_ref,
-        lambda c: _dot(basis * jt_ref[c], tvw_ref[:, _cols(c, columns)]),
-    )
-    top_ref[...] = row[:, 0:top_edges] / weight_total
-    row = jnp.zeros((1, lanes), F32)
-    row = _counts(row, 0, w, vt, larr_ref, lmsg_ref, lambda c: lmixed_ref[c])
-    local_ref[...] = row[:, 0:local_edges] / weight_total
+    row, subtree_out = _descend(
+        tpar_ref, tkids_ref, toutside_ref, tmsg_ref, tpt_ref,
+        jnp.broadcast_to(rf_col, (states, columns)),
+        _count_fn(w, vt, weight_total, tmsg_ref, tmixed_ref), jnp.zeros((1, lanes), F32), pick=g,
+    )
+    top_ref[...] = row[:, 0:top_edges]
+    row, _ = _descend(
+        lpar_ref, lkids_ref, loutside_ref, lmsg_ref, lpt_ref, subtree_out,
+        _count_fn(w, vt, weight_total, lmsg_ref, lmixed_ref), jnp.zeros((1, lanes), F32),
+    )
+    local_ref[...] = row[:, 0:local_edges]
 
 
 def join(top_parents, pick, parents, halves, tp, tpt, basis, j_top, vecs, inv, rf_row, w_row,
@@ -286,12 +279,9 @@
         scratch_shapes=[
             pltpu.VMEM((leaf_count - 1, states, columns), F32),
             pltpu.VMEM((top_edges, states, columns), F32),
-            pltpu.VMEM((states, top_edges * columns), F32),
-            pltpu.VMEM((states, top_edges * columns), F32),
+            pltpu.VMEM((top_edges, states, columns), F32),
             pltpu.VMEM((leaf_count - 1, states, columns), F32),
-            pltpu.VMEM((states, top_edges * columns), F32),
             pltpu.VMEM((local_leaves - 1, states, columns), F32),
-            pltpu.VMEM((states, local_edges * columns), F32),
             pltpu.SMEM((top_edges + 1,), jnp.int32),
             pltpu.SMEM((local_edges + 1,), jnp.int32),
         ],

time: 45.1 us -> 46.7 us (1.035)
  Pallas kernels: 20.3 us -> 22 us
    pallas_call x1, Pallas kernels: 11.3 us -> 13 us  [join(): pl.pallas_call(functools.partial(_join_kernel, taxon_count=taxon_count, p...]
  transfers between devices with their start and end apart: 5 -> 5, of which waited for: 2 -> 2; matrix products, arithmetic and copies ran while one was open for 8% -> 7% of each run, Pallas kernels for 20% -> 19%
where the time goes in v7:
time: 46.7 us; the launch traced here: 46.4 us
  Pallas kernels  22 us (47%)
  starting transfers between devices  8.92 us (19%)
  blocking collectives  5.41 us (12%)
  other arithmetic  4.13 us (9%)
  local copies, waits for them, and re-layouts  2.58 us (6%)
  waiting for transfers between devices  1.99 us (4%)
  between operations  1.4 us (3%)
    pallas_call x1, Pallas kernels, join(): pl.pallas_call(functools.partial(_join_kernel, taxon_count=taxon_count, p...  13 us
    ppermute x4, starting transfers between devices, gather_roots(): other = lax.ppermute(buf, 'leaf', [(i, i ^ step) for i in range(groups)])  5.92 us
    psum x1, blocking collectives, on_device(): local_sum, top_sum = lax.psum((local_row[0], top_row[0]), 'site')  5.41 us
    pallas_call x1, Pallas kernels, climb(): pl.pallas_call(_climb_kernel, out_shape=(jax.ShapeDtypeStruct((states + 1...  3.42 us
    ppermute x1, starting transfers between devices, on_device(): w_other = lax.ppermute(w_row, 'site', [(0, 1), (1, 0)])  3 us
    pallas_call x1, Pallas kernels, local_matrices(): pl.pallas_call(_local_matrix_kernel, out_shape=(jax.ShapeDtypeStruct((loc...  2.92 us
    pallas_call x1, Pallas kernels, top_matrices(): pl.pallas_call(_top_matrix_kernel, out_shape=(jax.ShapeDtypeStruct((top_e...  2.66 us
    mul x4, other arithmetic, integrals(): return branch * jnp.exp(eig_values[None, :] * branch) * growth  2.02 us
  transfers between devices with their start and end apart: 5, of which 2 were waited for; matrix products, arithmetic and copies ran while one was open for 7% of the time, Pallas kernels for 19%

profile of v7, /device:TPU:0, one launch (start us, length us, event | category | flops | bytes accessed | tf_op | source)
XLA Modules:
  0.0 46.4 jit_solution(3646869953220644749)
XLA Ops:
  0.6 0.7 %convert_bitcast_fusion.w_ref = f32[1,128]{1,0:T(1,128)S(1)} fusion(s32[128]{0:T(128)} %param.16), kind=kLoop, calls=%fused_computation.32 | loop fusion | flops 128 | bytes 1024 | tf_op jit(solution)/shard_map/broadcast_in_dim | solution.py:325
  1.3 3.0 %collective-permute-start.3 = (f32[1,128]{1,0:T(1,128)S(1)}, f32[1,128]{1,0:T(1,128)S(1)}, u32[]{:S(2)}, u32[]{:S(2)}) collective-permute-start(f32[1,128]{1,0:T(1,128)S(1)} %convert_bitcast_fusion.w_ref), channel_id=1, source_target_pairs={{0,1},{1,0},{2,3},{3,2},{4,5},{5,4},{6,7},{7,6},{8,9},{9,8},{10,11... | collective-permute-start | bytes 1544 | tf_op jit(solution)/shard_map/ppermute | solution.py:327
  4.3 3.4 %shard_map.130 = (f32[65,128]{1,0:T(8,128)}, f32[14,64,128]{2,1,0:T(8,128)}, f32[64,1792]{1,0:T(8,128)}, f32[14,64,64]{2,1,0:T(8,128)}) custom-call(s32[14]{0:T(128)} %lpar_ref.1, f32[14]{0:T(128)} %len_ref.1, f32[8,64,128]{2,1,0:T(8,128)} %leaf_ref.1, f32[64,64]{1,0:T(8,128)} %v_ref.7, f32[64,64]{1,0:T(8,128)} %vi_ref.7, f32[1,64]{1,0:T(1,128)} %bitcast.32), custom_call_target="tpu_custom_call" | custom-call | tf_op jit(solution)/shard_map/pallas_call | solution.py:75
  7.7 2.7 %collective-permute-start = (f32[1,65,128]{2,1,0:T(8,128)}, f32[1,65,128]{2,1,0:T(8,128)S(1)}, u32[]{:S(2)}, u32[]{:S(2)}) collective-permute-start(f32[1,65,128]{2,1,0:T(8,128)} %bitcast.29), channel_id=1, source_target_pairs={{0,16},{2,18},{4,20},{6,22},{8,24},{10,26},{12,28},{14,30},{16,0},... | collective-permute-start | bytes 99848 | tf_op jit(solution)/shard_map/ppermute | solution.py:297
  10.4 0.0 copy-done.4
  10.4 0.1 broadcast_subtract_fusion
  10.4 0.1 exponential_multiply_fusion
  10.5 0.0 copy-start.3
  10.5 0.7 %fusion.4.jt_ref = f32[30,64,64]{2,1,0:T(8,128)S(1)} fusion(f32[30]{0:T(128)S(1)} %copy-done.5, f32[64,64]{1,0:T(8,128)S(1)} %broadcast_subtract_fusion, f32[30,64]{1,0:T(8,128)S(1)} %exponential_multiply_fusion), kind=kLoop, calls=%fused_computation.14 | loop fusion | flops 1474560 | bytes 515704 | tf_op jit(solution)/shard_map/vmap()/mul | solution.py:31
  11.3 0.6 %slice.4 = f32[1,1,1]{2,1,0:T(1,128)} slice(f32[30,64,64]{2,1,0:T(8,128)S(1)} %fusion.4.jt_ref), slice={[0:1], [0:1], [0:1]} | slice | bytes 8 | tf_op jit(solution)/shard_map/slice | solution.py:344
  12.5 0.4 collective-permute-done
  12.9 0.0 copy-start.6
  12.9 1.6 %collective-permute-start.1 = (f32[2,65,128]{2,1,0:T(8,128)S(1)}, f32[2,65,128]{2,1,0:T(8,128)S(1)}, u32[]{:S(2)}, u32[]{:S(2)}) collective-permute-start(f32[2,65,128]{2,1,0:T(8,128)S(1)} %get-tuple-element.36), channel_id=1, source_target_pairs={{0,8},{2,10},{4,12},{6,14},{8,0},{10,2},{12,4},{14,6},{16,24},{18,... | collective-permute-start | bytes 199688 | tf_op jit(solution)/shard_map/ppermute | solution.py:297
  14.5 0.1 exponential_multiply_fusion.1
  14.6 2.7 %shard_map.131 = (f32[30,64,64]{2,1,0:T(8,128)}, f32[30,64,64]{2,1,0:T(8,128)}, f32[1,1]{1,0:T(1,128)}) custom-call(f32[30]{0:T(128)} %top_len_ref.1, f32[64,64]{1,0:T(8,128)} %v_ref.7, f32[64,64]{1,0:T(8,128)} %vi_ref.7, f32[1,64]{1,0:T(1,128)} %bitcast.33), custom_call_target="tpu_custom_call" | custom-call | tf_op jit(solution)/shard_map/pallas_call | solution.py:142
  17.3 0.0 collective-permute-done.1
  17.3 0.7 %maximum_add_fusion.1 = f32[2,2,65,128]{3,2,0,1:T(8,128)S(1)} fusion(f32[2,1,65,128]{3,2,0,1:T(8,128)S(1)} %bitcast.28, f32[2,1,65,128]{3,2,0,1:T(8,128)S(1)} %get-tuple-element.35, f32[]{:T(128)} %bitcast.9), kind=kLoop, calls=%fused_computation.25 | loop fusion | flops 66560 | bytes 266244 | tf_op jit(solution)/shard_map/add | solution.py:303
  18.0 0.1 copy.14
  18.0 1.6 %collective-permute-start.2 = (f32[4,65,128]{2,0,1:T(4,128)S(1)}, f32[4,65,128]{2,0,1:T(4,128)S(1)}, u32[]{:S(2)}, u32[]{:S(2)}) collective-permute-start(f32[4,65,128]{2,0,1:T(4,128)S(1)} %bitcast.25), channel_id=1, source_target_pairs={{0,4},{2,6},{4,0},{6,2},{8,12},{10,14},{12,8},{14,10},{16,20},{18,... | collective-permute-start | bytes 399368 | tf_op jit(solution)/shard_map/ppermute | solution.py:297
  19.6 1.2 %fusion.11.jl_ref = f32[14,64,64]{2,1,0:T(8,128)} fusion(f32[14]{0:T(128)S(1)} %copy-done.6, f32[64,64]{1,0:T(8,128)S(1)} %broadcast_subtract_fusion, f32[14,64]{1,0:T(8,128)S(1)} %exponential_multiply_fusion.1), kind=kLoop, calls=%fused_computation.21 | loop fusion | flops 688128 | bytes 249400 | tf_op jit(solution)/shard_map/vmap()/mul | solution.py:31
  20.8 0.0 collective-permute-done.3.wo_ref
  20.8 0.5 %copy-done.8 = f32[1,128]{1,0:T(1,128)} copy-done((f32[1,128]{1,0:T(1,128)}, f32[1,128]{1,0:T(1,128)S(1)}, u32[]{:S(2)}) %copy-start.8) | copy-done | bytes 536
  21.3 2.9 %shard_map.132 = (f32[14,64,128]{2,1,0:T(8,128)}, f32[14,64,64]{2,1,0:T(8,128)}, f32[64,64]{1,0:T(8,128)}, f32[1,1]{1,0:T(1,128)}, f32[1,1]{1,0:T(1,128)}) custom-call(f32[64,64]{1,0:T(8,128)} %v_ref.7, f32[64,64]{1,0:T(8,128)} %vi_ref.7, f32[64,64]{1,0:T(8,128)} %lab_ref.1, f32[14,64,64]{2,1,0:T(8,128)} %fusion.11.jl_ref, ...), custom_call_target="tpu_custom_call" | custom-call | tf_op jit(solution)/shard_map/pallas_call | solution.py:110
  24.2 0.0 collective-permute-done.2
  24.2 0.7 %maximum_add_fusion = f32[4,2,65,128]{3,0,2,1:T(4,128)S(1)} fusion(f32[4,1,65,128]{3,0,2,1:T(4,128)S(1)} %bitcast.27, f32[4,1,65,128]{3,0,2,1:T(4,128)S(1)} %bitcast.26, f32[]{:T(128)} %bitcast.14), kind=kLoop, calls=%fused_computation.24 | loop fusion | flops 133120 | bytes 532484 | tf_op jit(solution)/shard_map/add | solution.py:303
  25.0 0.1 collective-permute-start.4
  25.0 1.6 %collective-permute-done.4.gat1_ref = f32[8,65,128]{2,1,0:T(8,128)S(1)} collective-permute-done((f32[8,65,128]{2,1,0:T(8,128)S(1)}, f32[8,65,128]{2,1,0:T(8,128)S(1)}, u32[]{:S(2)}, u32[]{:S(2)}) %collective-permute-start.4) | collective-permute-done | bytes 266272 | tf_op jit(solution)/shard_map/ppermute | solution.py:297
  26.6 0.7 %copy-done.2 = f32[8,65,128]{2,1,0:T(8,128)} copy-done((f32[8,65,128]{2,1,0:T(8,128)}, f32[8,65,128]{2,1,0:T(8,128)S(1)}, u32[]{:S(2)}) %copy-start.2) | copy-done | bytes 266264
  27.3 13.0 %shard_map.133 = (f32[1,14]{1,0:T(1,128)}, f32[1,30]{1,0:T(1,128)}, f32[1,128]{1,0:T(1,128)}) custom-call(s32[30]{0:T(128)} %tpar_ref.1, s32[1]{0:T(128)} %bitcast.pick_ref, s32[14]{0:T(128)} %lpar_ref.1, f32[8,65,128]{2,1,0:T(8,128)} %bitcast.24, f32[8,65,128]{2,1,0:T(8,128)} %copy-done.2, f32[30,64,64]{2,1,0:T(8,128)} %get-tuple-element.23.tp_ref, ...), custom_call_target="tpu_custom_call" | custom-call | tf_op jit(solution)/shard_map/pallas_call | solution.py:270
  40.3 0.6 %copy-done.9 = f32[1,14]{1,0:T(1,128)S(1)} copy-done((f32[1,14]{1,0:T(1,128)S(1)}, f32[1,14]{1,0:T(1,128)}, u32[]{:S(2)}) %copy-start.9) | copy-done | bytes 80
  41.0 0.0 copy-done.10
  41.0 5.4 %all-reduce = (f32[14]{0:T(128)}, f32[30]{0:T(128)}) all-reduce(f32[14]{0:T(128)S(1)} %bitcast.36, f32[30]{0:T(128)S(1)} %bitcast.37), channel_id=1, replica_groups=mesh['leaf'=16,'site'=2] {'site'}, use_global_device_ids=true, to_apply=%region_0.1 | all-reduce | flops 44 | bytes 352 | tf_op jit(solution)/shard_map/psum | solution.py:358
  (17 shorter events, 0.1 us)
Async XLA Ops:
  1.3 3.0 %copy-start.7 = (f32[1,128]{1,0:T(1,128)}, f32[1,128]{1,0:T(1,128)S(1)}, u32[]{:S(2)}) copy-start(f32[1,128]{1,0:T(1,128)S(1)} %convert_bitcast_fusion.w_ref) | copy-start | bytes 1540
  1.3 19.5 %collective-permute-start.3 = (f32[1,128]{1,0:T(1,128)S(1)}, f32[1,128]{1,0:T(1,128)S(1)}, u32[]{:S(2)}, u32[]{:S(2)}) collective-permute-start(f32[1,128]{1,0:T(1,128)S(1)} %convert_bitcast_fusion.w_ref), channel_id=1, source_target_pairs={{0,1},{1,0},{2,3},{3,2},{4,5},{5,4},{6,7},{7,6},{8,9},{9,8},{10,11... | collective-permute-start | bytes 1544 | tf_op jit(solution)/shard_map/ppermute | solution.py:327
  7.7 2.7 %copy-start.4 = (f32[64]{0:T(128)S(1)}, f32[64]{0:T(128)}, u32[]{:S(2)}) copy-start(f32[64]{0:T(128)} %param.19) | copy-start | bytes 772
  7.7 2.7 %copy-start.5 = (f32[30]{0:T(128)S(1)}, f32[30]{0:T(128)}, u32[]{:S(2)}) copy-start(f32[30]{0:T(128)} %top_len_ref.1) | copy-start | bytes 364
  7.7 5.1 %collective-permute-start = (f32[1,65,128]{2,1,0:T(8,128)}, f32[1,65,128]{2,1,0:T(8,128)S(1)}, u32[]{:S(2)}, u32[]{:S(2)}) collective-permute-start(f32[1,65,128]{2,1,0:T(8,128)} %bitcast.29), channel_id=1, source_target_pairs={{0,16},{2,18},{4,20},{6,22},{8,24},{10,26},{12,28},{14,30},{16,0},... | collective-permute-start | bytes 99848 | tf_op jit(solution)/shard_map/ppermute | solution.py:297
  10.5 2.3 %copy-start.3 = (f32[65,128]{1,0:T(8,128)S(1)}, f32[65,128]{1,0:T(8,128)}, u32[]{:S(2)}) copy-start(f32[65,128]{1,0:T(8,128)} %get-tuple-element.18) | copy-start | bytes 99844
  11.2 13.0 %copy-start = (f32[30,64,64]{2,1,0:T(8,128)}, f32[30,64,64]{2,1,0:T(8,128)S(1)}, u32[]{:S(2)}) copy-start(f32[30,64,64]{2,1,0:T(8,128)S(1)} %fusion.4.jt_ref) | copy-start | bytes 1474564
  12.9 1.7 %copy-start.6 = (f32[14]{0:T(128)S(1)}, f32[14]{0:T(128)}, u32[]{:S(2)}) copy-start(f32[14]{0:T(128)} %len_ref.1) | copy-start | bytes 172
  12.9 4.4 %collective-permute-start.1 = (f32[2,65,128]{2,1,0:T(8,128)S(1)}, f32[2,65,128]{2,1,0:T(8,128)S(1)}, u32[]{:S(2)}, u32[]{:S(2)}) collective-permute-start(f32[2,65,128]{2,1,0:T(8,128)S(1)} %get-tuple-element.36), channel_id=1, source_target_pairs={{0,8},{2,10},{4,12},{6,14},{8,0},{10,2},{12,4},{14,6},{16,24},{18,... | collective-permute-start | bytes 199688 | tf_op jit(solution)/shard_map/ppermute | solution.py:297
  18.0 6.2 %collective-permute-start.2 = (f32[4,65,128]{2,0,1:T(4,128)S(1)}, f32[4,65,128]{2,0,1:T(4,128)S(1)}, u32[]{:S(2)}, u32[]{:S(2)}) collective-permute-start(f32[4,65,128]{2,0,1:T(4,128)S(1)} %bitcast.25), channel_id=1, source_target_pairs={{0,4},{2,6},{4,0},{6,2},{8,12},{10,14},{12,8},{14,10},{16,20},{18,... | collective-permute-start | bytes 399368 | tf_op jit(solution)/shard_map/ppermute | solution.py:297
  20.8 0.5 %copy-start.8 = (f32[1,128]{1,0:T(1,128)}, f32[1,128]{1,0:T(1,128)S(1)}, u32[]{:S(2)}) copy-start(f32[1,128]{1,0:T(1,128)S(1)} %collective-permute-done.3.wo_ref) | copy-start | bytes 1540
  25.0 1.7 %copy-start.1 = (f32[4,2,65,128]{3,2,1,0:T(8,128)}, f32[4,2,65,128]{3,2,1,0:T(8,128)S(1)}, u32[]{:S(2)}) copy-start(f32[4,2,65,128]{3,2,1,0:T(8,128)S(1)} %copy.16) | copy-start | bytes 798724
  25.0 1.6 %collective-permute-start.4 = (f32[8,65,128]{2,1,0:T(8,128)S(1)}, f32[8,65,128]{2,1,0:T(8,128)S(1)}, u32[]{:S(2)}, u32[]{:S(2)}) collective-permute-start(f32[8,65,128]{2,1,0:T(8,128)S(1)} %bitcast.23), channel_id=1, source_target_pairs={{0,2},{2,0},{4,6},{6,4},{8,10},{10,8},{12,14},{14,12},{16,18},{18,... | collective-permute-start | bytes 798728 | tf_op jit(solution)/shard_map/ppermute | solution.py:297
  26.6 0.7 %copy-start.2 = (f32[8,65,128]{2,1,0:T(8,128)}, f32[8,65,128]{2,1,0:T(8,128)S(1)}, u32[]{:S(2)}) copy-start(f32[8,65,128]{2,1,0:T(8,128)S(1)} %collective-permute-done.4.gat1_ref) | copy-start | bytes 798724
  40.3 0.6 %copy-start.9 = (f32[1,14]{1,0:T(1,128)S(1)}, f32[1,14]{1,0:T(1,128)}, u32[]{:S(2)}) copy-start(f32[1,14]{1,0:T(1,128)} %get-tuple-element.30) | copy-start | bytes 172
  40.3 0.7 %copy-start.10 = (f32[1,30]{1,0:T(1,128)S(1)}, f32[1,30]{1,0:T(1,128)}, u32[]{:S(2)}) copy-start(f32[1,30]{1,0:T(1,128)} %get-tuple-element.31) | copy-start | bytes 364

commit v8 on v6

--- a/solution.py
+++ b/solution.py
@@ -87,12 +87,10 @@
     )(parents, lengths, tips, vecs, inv, lam_row)
 
 
-def _local_matrix_kernel(v_ref, vi_ref, lab_ref, jl_ref, xw_ref, trl_ref, w_ref, wo_ref,
-                         mixed_ref, ptl_ref, basis_ref, token_ref, wt_ref, vw_ref):
+def _local_matrix_kernel(v_ref, vi_ref, lab_ref, jl_ref, xw_ref, trl_ref,
+                         mixed_ref, ptl_ref, basis_ref, token_ref, vw_ref):
     local_edges, states, columns = mixed_ref.shape
     token_ref[...] = jnp.zeros(token_ref.shape, F32)
-    wt_ref[...] = (jnp.sum(w_ref[...], axis=1, keepdims=True)
-                   + jnp.sum(wo_ref[...], axis=1, keepdims=True))
     vecs = v_ref[...]
     inv = vi_ref[...]
     basis = _dot(_dot(inv, lab_ref[...]), vecs)
@@ -103,7 +101,7 @@
         ptl_ref[c] = trl_ref[c].T
 
 
-def local_matrices(vecs, inv, labeled, j_local, xw, trl, w_row, w_other):
+def local_matrices(vecs, inv, labeled, j_local, xw, trl):
     local_edges, states, _ = trl.shape
     columns = xw.shape[1] // local_edges
     sq = (states, states)
@@ -114,13 +112,12 @@
             jax.ShapeDtypeStruct((local_edges,) + sq, F32),
             jax.ShapeDtypeStruct(sq, F32),
             jax.ShapeDtypeStruct((1, 1), F32),
-            jax.ShapeDtypeStruct((1, 1), F32),
         ),
-        in_specs=[VMEM] * 8,
-        out_specs=(VMEM,) * 5,
+        in_specs=[VMEM] * 6,
+        out_specs=(VMEM,) * 4,
         scratch_shapes=[pltpu.VMEM((states, local_edges * columns), F32)],
         compiler_params=PARAMS,
-    )(vecs, inv, labeled, j_local, xw, trl, w_row, w_other)
+    )(vecs, inv, labeled, j_local, xw, trl)
 
 
 def _top_matrix_kernel(top_len_ref, v_ref, vi_ref, lam_ref, tp_ref, tpt_ref, token_ref):
@@ -253,7 +250,7 @@
     )
     _descend(lpar_ref, lkids_ref, loutside_ref, larr_ref, lmsg_ref, lpt_ref, subtree_out)
     w = w_ref[...]
-    weight_total = wo_ref[...]
+    weight_total = jnp.sum(w, axis=1, keepdims=True) + jnp.sum(wo_ref[...], axis=1, keepdims=True)
     lanes = max(local_edges, top_edges)
     row = jnp.zeros((1, lanes), F32)
     row = _counts(
@@ -346,8 +343,8 @@
     j_local = jax.vmap(lambda t: integrals(eig_values, t))(branch_lengths)
     j_top = jax.vmap(lambda t: integrals(eig_values, t))(top_lengths)
     tp, tpt, top_token = top_matrices(top_lengths, eig_vectors, eig_inverse, lam_row)
-    lmixed, lpt, basis, local_token, weight_total = local_matrices(
-        eig_vectors, eig_inverse, labeled_rates, j_local, xw, trl, w_row, w_other
+    lmixed, lpt, basis, local_token = local_matrices(
+        eig_vectors, eig_inverse, labeled_rates, j_local, xw, trl
     )
     if paired:
         tokens = {
@@ -363,7 +360,7 @@
         pick = jnp.zeros((1,), jnp.int32)
     local_row, top_row, loglik = join(
         top_parents, pick, parents, halves, tp, tpt, basis, j_top, eig_vectors, eig_inverse,
-        root_freq[None, :], w_row, weight_total, msgs, lmixed, lpt, taxon_count, paired,
+        root_freq[None, :], w_row, w_other, msgs, lmixed, lpt, taxon_count, paired,
     )
     local_sum, top_sum = lax.psum((local_row[0], top_row[0]), "site")
     return (local_sum, top_sum, loglik[0])

time: 45.1 us -> 44.7 us (level)
  other arithmetic: 4.13 us -> 3.46 us
  waiting for transfers between devices: 1.98 us -> 2.6 us
  Pallas kernels: 20.3 us -> 19.8 us
    ppermute x1, waiting for transfers between devices: 0.01 us -> 2.05 us  [on_device(): w_other = lax.ppermute(w_row, 'site', [(0, 1), (1, 0)])]
    ppermute x4, starting transfers between devices: 5.95 us -> 7.55 us  [gather_roots(): other = lax.ppermute(buf, 'leaf', [(i, i ^ step) for i in range(groups)])]
    ppermute x1, starting transfers between devices: 3 us -> 1.52 us  [on_device(): w_other = lax.ppermute(w_row, 'site', [(0, 1), (1, 0)])]
    ppermute x4, waiting for transfers between devices: 1.97 us -> 0.56 us  [gather_roots(): other = lax.ppermute(buf, 'leaf', [(i, i ^ step) for i in range(groups)])]
    broadcast_in_dim x1, other arithmetic: 0.66 us -> 0.01 us  [on_device(): w_row = weights.astype(F32)[None, :]]
    pallas_call x1, Pallas kernels: 11.3 us -> 10.8 us  [join(): pl.pallas_call(functools.partial(_join_kernel, taxon_count=taxon_count, p...]
    unnamed x22 -> x24, local copies, waits for them, and re-layouts: 1.93 us -> 2.02 us
  transfers between devices with their start and end apart: 5 -> 5, of which waited for: 2 -> 3; matrix products, arithmetic and copies ran while one was open for 8% -> 6% of each run, Pallas kernels for 20% -> 13%
where the time goes in v8:
time: 44.7 us; the launch traced here: 44.4 us
  Pallas kernels  19.8 us (44%)
  starting transfers between devices  9.07 us (20%)
  blocking collectives  5.41 us (12%)
  other arithmetic  3.46 us (8%)
  local copies, waits for them, and re-layouts  2.67 us (6%)
  waiting for transfers between devices  2.6 us (6%)
  between operations  1.41 us (3%)
    pallas_call x1, Pallas kernels, join(): pl.pallas_call(functools.partial(_join_kernel, taxon_count=taxon_count, p...  10.8 us
    ppermute x4, starting transfers between devices, gather_roots(): other = lax.ppermute(buf, 'leaf', [(i, i ^ step) for i in range(groups)])  7.55 us
    psum x1, blocking collectives, on_device(): local_sum, top_sum = lax.psum((local_row[0], top_row[0]), 'site')  5.41 us
    pallas_call x1, Pallas kernels, climb(): pl.pallas_call(_climb_kernel, out_shape=(jax.ShapeDtypeStruct((states + 1...  3.42 us
    pallas_call x1, Pallas kernels, local_matrices(): pl.pallas_call(_local_matrix_kernel, out_shape=(jax.ShapeDtypeStruct((loc...  2.93 us
    pallas_call x1, Pallas kernels, top_matrices(): pl.pallas_call(_top_matrix_kernel, out_shape=(jax.ShapeDtypeStruct((top_e...  2.65 us
    ppermute x1, waiting for transfers between devices, on_device(): w_other = lax.ppermute(w_row, 'site', [(0, 1), (1, 0)])  2.05 us
    unnamed x24, local copies, waits for them, and re-layouts  2.02 us
  transfers between devices with their start and end apart: 5, of which 3 were waited for; matrix products, arithmetic and copies ran while one was open for 6% of the time, Pallas kernels for 13%

profile of v8, /device:TPU:0, one launch (start us, length us, event | category | flops | bytes accessed | tf_op | source)
XLA Modules:
  0.0 44.4 jit_solution(575616924590154302)
XLA Ops:
  0.6 3.4 %shard_map.130 = (f32[65,128]{1,0:T(8,128)}, f32[14,64,128]{2,1,0:T(8,128)}, f32[64,1792]{1,0:T(8,128)}, f32[14,64,64]{2,1,0:T(8,128)}) custom-call(s32[14]{0:T(128)} %lpar_ref.1, f32[14]{0:T(128)} %len_ref.1, f32[8,64,128]{2,1,0:T(8,128)} %leaf_ref.1, f32[64,64]{1,0:T(8,128)} %v_ref.7, f32[64,64]{1,0:T(8,128)} %vi_ref.7, f32[1,64]{1,0:T(1,128)} %bitcast.32), custom_call_target="tpu_custom_call" | custom-call | tf_op jit(solution)/shard_map/pallas_call | solution.py:75
  4.1 4.1 %collective-permute-start = (f32[1,65,128]{2,1,0:T(8,128)}, f32[1,65,128]{2,1,0:T(8,128)S(1)}, u32[]{:S(2)}, u32[]{:S(2)}) collective-permute-start(f32[1,65,128]{2,1,0:T(8,128)} %bitcast.29), channel_id=1, source_target_pairs={{0,16},{2,18},{4,20},{6,22},{8,24},{10,26},{12,28},{14,30},{16,0},... | collective-permute-start | bytes 99848 | tf_op jit(solution)/shard_map/ppermute | solution.py:304
  8.2 0.0 copy-done.4
  8.2 0.1 broadcast_subtract_fusion
  8.3 0.1 exponential_multiply_fusion
  8.3 0.0 copy-start.3
  8.4 0.7 %fusion.4.jt_ref = f32[30,64,64]{2,1,0:T(8,128)S(1)} fusion(f32[30]{0:T(128)S(1)} %copy-done.5, f32[64,64]{1,0:T(8,128)S(1)} %broadcast_subtract_fusion, f32[30,64]{1,0:T(8,128)S(1)} %exponential_multiply_fusion), kind=kLoop, calls=%fused_computation.14 | loop fusion | flops 1474560 | bytes 515704 | tf_op jit(solution)/shard_map/vmap()/mul | solution.py:31
  9.1 0.6 %slice.4 = f32[1,1,1]{2,1,0:T(1,128)} slice(f32[30,64,64]{2,1,0:T(8,128)S(1)} %fusion.4.jt_ref), slice={[0:1], [0:1], [0:1]} | slice | bytes 8 | tf_op jit(solution)/shard_map/slice | solution.py:351
  10.3 0.4 %collective-permute-done = f32[1,65,128]{2,1,0:T(8,128)S(1)} collective-permute-done((f32[1,65,128]{2,1,0:T(8,128)}, f32[1,65,128]{2,1,0:T(8,128)S(1)}, u32[]{:S(2)}, u32[]{:S(2)}) %collective-permute-start) | collective-permute-done | bytes 33312 | tf_op jit(solution)/shard_map/ppermute | solution.py:304
  10.8 0.0 copy-start.6
  10.8 1.6 %collective-permute-start.1 = (f32[2,65,128]{2,1,0:T(8,128)S(1)}, f32[2,65,128]{2,1,0:T(8,128)S(1)}, u32[]{:S(2)}, u32[]{:S(2)}) collective-permute-start(f32[2,65,128]{2,1,0:T(8,128)S(1)} %get-tuple-element.34), channel_id=1, source_target_pairs={{0,8},{2,10},{4,12},{6,14},{8,0},{10,2},{12,4},{14,6},{16,24},{18,... | collective-permute-start | bytes 199688 | tf_op jit(solution)/shard_map/ppermute | solution.py:304
  12.3 0.1 exponential_multiply_fusion.1
  12.4 2.7 %shard_map.131 = (f32[30,64,64]{2,1,0:T(8,128)}, f32[30,64,64]{2,1,0:T(8,128)}, f32[1,1]{1,0:T(1,128)}) custom-call(f32[30]{0:T(128)} %top_len_ref.1, f32[64,64]{1,0:T(8,128)} %v_ref.7, f32[64,64]{1,0:T(8,128)} %vi_ref.7, f32[1,64]{1,0:T(1,128)} %bitcast.33), custom_call_target="tpu_custom_call" | custom-call | tf_op jit(solution)/shard_map/pallas_call | solution.py:139
  15.1 0.1 collective-permute-done.1
  15.2 0.7 %maximum_add_fusion.1 = f32[2,2,65,128]{3,2,0,1:T(8,128)S(1)} fusion(f32[2,1,65,128]{3,2,0,1:T(8,128)S(1)} %bitcast.28, f32[2,1,65,128]{3,2,0,1:T(8,128)S(1)} %get-tuple-element.33, f32[]{:T(128)} %bitcast.9), kind=kLoop, calls=%fused_computation.25 | loop fusion | flops 66560 | bytes 266244 | tf_op jit(solution)/shard_map/add | solution.py:310
  15.8 0.1 copy.14
  15.9 1.8 %collective-permute-start.2 = (f32[4,65,128]{2,0,1:T(4,128)S(1)}, f32[4,65,128]{2,0,1:T(4,128)S(1)}, u32[]{:S(2)}, u32[]{:S(2)}) collective-permute-start(f32[4,65,128]{2,0,1:T(4,128)S(1)} %bitcast.25), channel_id=1, source_target_pairs={{0,4},{2,6},{4,0},{6,2},{8,12},{10,14},{12,8},{14,10},{16,20},{18,... | collective-permute-start | bytes 399368 | tf_op jit(solution)/shard_map/ppermute | solution.py:304
  17.7 1.1 %fusion.11.jl_ref = f32[14,64,64]{2,1,0:T(8,128)} fusion(f32[14]{0:T(128)S(1)} %copy-done.6, f32[64,64]{1,0:T(8,128)S(1)} %broadcast_subtract_fusion, f32[14,64]{1,0:T(8,128)S(1)} %exponential_multiply_fusion.1), kind=kLoop, calls=%fused_computation.21 | loop fusion | flops 688128 | bytes 249400 | tf_op jit(solution)/shard_map/vmap()/mul | solution.py:31
  18.8 2.9 %shard_map.132 = (f32[14,64,128]{2,1,0:T(8,128)}, f32[14,64,64]{2,1,0:T(8,128)}, f32[64,64]{1,0:T(8,128)}, f32[1,1]{1,0:T(1,128)}) custom-call(f32[64,64]{1,0:T(8,128)} %v_ref.7, f32[64,64]{1,0:T(8,128)} %vi_ref.7, f32[64,64]{1,0:T(8,128)} %lab_ref.1, f32[14,64,64]{2,1,0:T(8,128)} %fusion.11.jl_ref, f32[64,1792]{1,0:T(8,128)} %get-tuple-element.19.xw_ref, ...), custom_call_target="tpu_custom_call" | custom-call | tf_op jit(solution)/shard_map/pallas_call | solution.py:108
  21.8 0.0 collective-permute-done.2
  21.8 0.7 %maximum_add_fusion = f32[4,2,65,128]{3,0,2,1:T(4,128)S(1)} fusion(f32[4,1,65,128]{3,0,2,1:T(4,128)S(1)} %bitcast.27, f32[4,1,65,128]{3,0,2,1:T(4,128)S(1)} %bitcast.26, f32[]{:T(128)} %bitcast.13), kind=kLoop, calls=%fused_computation.24 | loop fusion | flops 133120 | bytes 532484 | tf_op jit(solution)/shard_map/add | solution.py:310
  22.5 0.0 copy-start.9
  22.6 0.1 collective-permute-start.3
  22.6 0.6 %copy-done.9 = s32[128]{0:T(128)S(1)} copy-done((s32[128]{0:T(128)S(1)}, s32[128]{0:T(128)}, u32[]{:S(2)}) %copy-start.9) | copy-done | bytes 536
  23.2 1.5 %collective-permute-start.4 = (f32[1,128]{1,0:T(1,128)S(1)}, f32[1,128]{1,0:T(1,128)S(1)}, u32[]{:S(2)}, u32[]{:S(2)}) collective-permute-start(f32[1,128]{1,0:T(1,128)S(1)} %convert_bitcast_fusion.w_ref), channel_id=1, source_target_pairs={{0,1},{1,0},{2,3},{3,2},{4,5},{5,4},{6,7},{7,6},{8,9},{9,8},{10,11... | collective-permute-start | bytes 1544 | tf_op jit(solution)/shard_map/ppermute | solution.py:334
  24.8 2.0 %collective-permute-done.4.wo_ref = f32[1,128]{1,0:T(1,128)S(1)} collective-permute-done((f32[1,128]{1,0:T(1,128)S(1)}, f32[1,128]{1,0:T(1,128)S(1)}, u32[]{:S(2)}, u32[]{:S(2)}) %collective-permute-start.4) | collective-permute-done | bytes 544 | tf_op jit(solution)/shard_map/ppermute | solution.py:334
  26.8 0.0 collective-permute-done.3.gat1_ref
  26.8 0.6 %copy-done.8 = f32[1,128]{1,0:T(1,128)} copy-done((f32[1,128]{1,0:T(1,128)}, f32[1,128]{1,0:T(1,128)S(1)}, u32[]{:S(2)}) %copy-start.8) | copy-done | bytes 536
  27.4 0.1 copy-done.2
  27.5 10.8 %shard_map.133 = (f32[1,14]{1,0:T(1,128)}, f32[1,30]{1,0:T(1,128)}, f32[1,128]{1,0:T(1,128)}) custom-call(s32[30]{0:T(128)} %tpar_ref.1, s32[1]{0:T(128)} %bitcast.pick_ref, s32[14]{0:T(128)} %lpar_ref.1, f32[8,65,128]{2,1,0:T(8,128)} %bitcast.24, f32[8,65,128]{2,1,0:T(8,128)} %copy-done.2, f32[30,64,64]{2,1,0:T(8,128)} %get-tuple-element.22.tp_ref, ...), custom_call_target="tpu_custom_call" | custom-call | tf_op jit(solution)/shard_map/pallas_call | solution.py:274
  38.3 0.7 %copy-done.10 = f32[1,14]{1,0:T(1,128)S(1)} copy-done((f32[1,14]{1,0:T(1,128)S(1)}, f32[1,14]{1,0:T(1,128)}, u32[]{:S(2)}) %copy-start.10) | copy-done | bytes 80
  39.0 5.4 %all-reduce = (f32[14]{0:T(128)}, f32[30]{0:T(128)}) all-reduce(f32[14]{0:T(128)S(1)} %bitcast.36, f32[30]{0:T(128)S(1)} %bitcast.37), channel_id=1, replica_groups=mesh['leaf'=16,'site'=2] {'site'}, use_global_device_ids=true, to_apply=%region_0.1 | all-reduce | flops 44 | bytes 352 | tf_op jit(solution)/shard_map/psum | solution.py:365
  (19 shorter events, 0.1 us)
Async XLA Ops:
  4.0 4.1 %copy-start.4 = (f32[64]{0:T(128)S(1)}, f32[64]{0:T(128)}, u32[]{:S(2)}) copy-start(f32[64]{0:T(128)} %param.19) | copy-start | bytes 772
  4.1 4.2 %copy-start.5 = (f32[30]{0:T(128)S(1)}, f32[30]{0:T(128)}, u32[]{:S(2)}) copy-start(f32[30]{0:T(128)} %top_len_ref.1) | copy-start | bytes 364
  4.1 6.7 %collective-permute-start = (f32[1,65,128]{2,1,0:T(8,128)}, f32[1,65,128]{2,1,0:T(8,128)S(1)}, u32[]{:S(2)}, u32[]{:S(2)}) collective-permute-start(f32[1,65,128]{2,1,0:T(8,128)} %bitcast.29), channel_id=1, source_target_pairs={{0,16},{2,18},{4,20},{6,22},{8,24},{10,26},{12,28},{14,30},{16,0},... | collective-permute-start | bytes 99848 | tf_op jit(solution)/shard_map/ppermute | solution.py:304
  8.3 2.4 %copy-start.3 = (f32[65,128]{1,0:T(8,128)S(1)}, f32[65,128]{1,0:T(8,128)}, u32[]{:S(2)}) copy-start(f32[65,128]{1,0:T(8,128)} %get-tuple-element.17) | copy-start | bytes 99844
  9.1 12.7 %copy-start = (f32[30,64,64]{2,1,0:T(8,128)}, f32[30,64,64]{2,1,0:T(8,128)S(1)}, u32[]{:S(2)}) copy-start(f32[30,64,64]{2,1,0:T(8,128)S(1)} %fusion.4.jt_ref) | copy-start | bytes 1474564
  10.8 1.6 %copy-start.6 = (f32[14]{0:T(128)S(1)}, f32[14]{0:T(128)}, u32[]{:S(2)}) copy-start(f32[14]{0:T(128)} %len_ref.1) | copy-start | bytes 172
  10.8 4.4 %collective-permute-start.1 = (f32[2,65,128]{2,1,0:T(8,128)S(1)}, f32[2,65,128]{2,1,0:T(8,128)S(1)}, u32[]{:S(2)}, u32[]{:S(2)}) collective-permute-start(f32[2,65,128]{2,1,0:T(8,128)S(1)} %get-tuple-element.34), channel_id=1, source_target_pairs={{0,8},{2,10},{4,12},{6,14},{8,0},{10,2},{12,4},{14,6},{16,24},{18,... | collective-permute-start | bytes 199688 | tf_op jit(solution)/shard_map/ppermute | solution.py:304
  15.9 5.9 %collective-permute-start.2 = (f32[4,65,128]{2,0,1:T(4,128)S(1)}, f32[4,65,128]{2,0,1:T(4,128)S(1)}, u32[]{:S(2)}, u32[]{:S(2)}) collective-permute-start(f32[4,65,128]{2,0,1:T(4,128)S(1)} %bitcast.25), channel_id=1, source_target_pairs={{0,4},{2,6},{4,0},{6,2},{8,12},{10,14},{12,8},{14,10},{16,20},{18,... | collective-permute-start | bytes 399368 | tf_op jit(solution)/shard_map/ppermute | solution.py:304
  22.5 4.8 %copy-start.1 = (f32[4,2,65,128]{3,2,1,0:T(8,128)}, f32[4,2,65,128]{3,2,1,0:T(8,128)S(1)}, u32[]{:S(2)}) copy-start(f32[4,2,65,128]{3,2,1,0:T(8,128)S(1)} %copy.16) | copy-start | bytes 798724
  22.5 0.7 %copy-start.9 = (s32[128]{0:T(128)S(1)}, s32[128]{0:T(128)}, u32[]{:S(2)}) copy-start(s32[128]{0:T(128)} %param.16) | copy-start | bytes 1540
  22.6 4.2 %collective-permute-start.3 = (f32[8,65,128]{2,1,0:T(8,128)S(1)}, f32[8,65,128]{2,1,0:T(8,128)S(1)}, u32[]{:S(2)}, u32[]{:S(2)}) collective-permute-start(f32[8,65,128]{2,1,0:T(8,128)S(1)} %bitcast.23), channel_id=1, source_target_pairs={{0,2},{2,0},{4,6},{6,4},{8,10},{10,8},{12,14},{14,12},{16,18},{18,... | collective-permute-start | bytes 798728 | tf_op jit(solution)/shard_map/ppermute | solution.py:304
  23.2 1.5 %copy-start.7 = (f32[1,128]{1,0:T(1,128)}, f32[1,128]{1,0:T(1,128)S(1)}, u32[]{:S(2)}) copy-start(f32[1,128]{1,0:T(1,128)S(1)} %convert_bitcast_fusion.w_ref) | copy-start | bytes 1540
  23.2 3.6 %collective-permute-start.4 = (f32[1,128]{1,0:T(1,128)S(1)}, f32[1,128]{1,0:T(1,128)S(1)}, u32[]{:S(2)}, u32[]{:S(2)}) collective-permute-start(f32[1,128]{1,0:T(1,128)S(1)} %convert_bitcast_fusion.w_ref), channel_id=1, source_target_pairs={{0,1},{1,0},{2,3},{3,2},{4,5},{5,4},{6,7},{7,6},{8,9},{9,8},{10,11... | collective-permute-start | bytes 1544 | tf_op jit(solution)/shard_map/ppermute | solution.py:334
  26.8 0.6 %copy-start.8 = (f32[1,128]{1,0:T(1,128)}, f32[1,128]{1,0:T(1,128)S(1)}, u32[]{:S(2)}) copy-start(f32[1,128]{1,0:T(1,128)S(1)} %collective-permute-done.4.wo_ref) | copy-start | bytes 1540
  26.8 0.7 %copy-start.2 = (f32[8,65,128]{2,1,0:T(8,128)}, f32[8,65,128]{2,1,0:T(8,128)S(1)}, u32[]{:S(2)}) copy-start(f32[8,65,128]{2,1,0:T(8,128)S(1)} %collective-permute-done.3.gat1_ref) | copy-start | bytes 798724
  38.3 0.7 %copy-start.10 = (f32[1,14]{1,0:T(1,128)S(1)}, f32[1,14]{1,0:T(1,128)}, u32[]{:S(2)}) copy-start(f32[1,14]{1,0:T(1,128)} %get-tuple-element.28) | copy-start | bytes 172
  38.3 0.7 %copy-start.11 = (f32[1,30]{1,0:T(1,128)S(1)}, f32[1,30]{1,0:T(1,128)}, u32[]{:S(2)}) copy-start(f32[1,30]{1,0:T(1,128)} %get-tuple-element.29) | copy-start | bytes 364

commit v9 on v8

--- a/solution.py
+++ b/solution.py
@@ -307,7 +307,8 @@
         buf = jnp.stack([buf, other], axis=1).reshape((-1,) + block.shape)
         step //= 2
         if step in tokens:
-            buf = buf + tokens[step]
+            spot = (0, block.shape[0] - 1, 0)
+            buf = buf.at[spot].add(tokens[step])
     return buf, buf
 
 

time: 44.7 us -> 47.7 us (1.067)
  between operations: 1.41 us -> 4.68 us
  local copies, waits for them, and re-layouts: 2.67 us -> 4.29 us
  other arithmetic: 3.46 us -> 2.18 us
  waiting for transfers between devices: 2.6 us -> 2.09 us
    another operation x0 -> x5, local copies, waits for them, and re-layouts: none -> 1.63 us
    add x3 -> x0, other arithmetic: 1.38 us -> none  [gather_roots(): buf = buf + tokens[step]]
    ppermute x4, waiting for transfers between devices: 0.56 us -> 0.04 us  [gather_roots(): other = lax.ppermute(buf, 'leaf', [(i, i ^ step) for i in range(groups)])]
  transfers between devices with their start and end apart: 5 -> 5, of which waited for: 3 -> 1; matrix products, arithmetic and copies ran while one was open for 6% -> 7% of each run, Pallas kernels for 13% -> 12%
where the time goes in v9:
time: 47.7 us; the launch traced here: 47.4 us
  Pallas kernels  19.8 us (42%)
  starting transfers between devices  8.93 us (19%)
  blocking collectives  5.41 us (11%)
  between operations  4.68 us (10%)
  local copies, waits for them, and re-layouts  4.29 us (9%)
  other arithmetic  2.18 us (5%)
  waiting for transfers between devices  2.09 us (4%)
    pallas_call x1, Pallas kernels, join(): pl.pallas_call(functools.partial(_join_kernel, taxon_count=taxon_count, p...  10.8 us
    ppermute x4, starting transfers between devices, gather_roots(): other = lax.ppermute(buf, 'leaf', [(i, i ^ step) for i in range(groups)])  7.41 us
    psum x1, blocking collectives, on_device(): local_sum, top_sum = lax.psum((local_row[0], top_row[0]), 'site')  5.41 us
    pallas_call x1, Pallas kernels, climb(): pl.pallas_call(_climb_kernel, out_shape=(jax.ShapeDtypeStruct((states + 1...  3.42 us
    pallas_call x1, Pallas kernels, local_matrices(): pl.pallas_call(_local_matrix_kernel, out_shape=(jax.ShapeDtypeStruct((loc...  2.94 us
    pallas_call x1, Pallas kernels, top_matrices(): pl.pallas_call(_top_matrix_kernel, out_shape=(jax.ShapeDtypeStruct((top_e...  2.66 us
    ppermute x1, waiting for transfers between devices, on_device(): w_other = lax.ppermute(w_row, 'site', [(0, 1), (1, 0)])  2.05 us
    mul x4, other arithmetic, integrals(): return branch * jnp.exp(eig_values[None, :] * branch) * growth  2.02 us
  transfers between devices with their start and end apart: 5, of which 1 were waited for; matrix products, arithmetic and copies ran while one was open for 7% of the time, Pallas kernels for 12%

profile of v9, /device:TPU:0, one launch (start us, length us, event | category | flops | bytes accessed | tf_op | source)
XLA Modules:
  0.0 47.4 jit_solution(18426303805233020190)
XLA Ops:
  0.6 3.4 %shard_map.130 = (f32[65,128]{1,0:T(8,128)}, f32[14,64,128]{2,1,0:T(8,128)}, f32[64,1792]{1,0:T(8,128)}, f32[14,64,64]{2,1,0:T(8,128)}) custom-call(s32[14]{0:T(128)} %lpar_ref.1, f32[14]{0:T(128)} %len_ref.1, f32[8,64,128]{2,1,0:T(8,128)} %leaf_ref.1, f32[64,64]{1,0:T(8,128)} %v_ref.7, f32[64,64]{1,0:T(8,128)} %vi_ref.7, f32[1,64]{1,0:T(1,128)} %bitcast.36), custom_call_target="tpu_custom_call" | custom-call | tf_op jit(solution)/shard_map/pallas_call | solution.py:75
  4.1 4.1 %collective-permute-start = (f32[1,65,128]{2,1,0:T(8,128)}, f32[1,65,128]{2,1,0:T(8,128)S(1)}, u32[]{:S(2)}, u32[]{:S(2)}) collective-permute-start(f32[1,65,128]{2,1,0:T(8,128)} %bitcast.32), channel_id=1, source_target_pairs={{0,16},{2,18},{4,20},{6,22},{8,24},{10,26},{12,28},{14,30},{16,0},... | collective-permute-start | bytes 99848 | tf_op jit(solution)/shard_map/ppermute | solution.py:304
  8.2 0.1 broadcast_subtract_fusion
  8.3 0.1 exponential_multiply_fusion
  8.4 0.7 %fusion.4.jt_ref = f32[30,64,64]{2,1,0:T(8,128)S(1)} fusion(f32[30]{0:T(128)S(1)} %copy-done.5, f32[64,64]{1,0:T(8,128)S(1)} %broadcast_subtract_fusion, f32[30,64]{1,0:T(8,128)S(1)} %exponential_multiply_fusion), kind=kLoop, calls=%fused_computation.14 | loop fusion | flops 1474560 | bytes 515704 | tf_op jit(solution)/shard_map/vmap()/mul | solution.py:31
  9.1 0.6 %slice.84 = f32[1,1,1]{2,1,0:T(1,128)} slice(f32[30,64,64]{2,1,0:T(8,128)S(1)} %fusion.4.jt_ref), slice={[0:1], [0:1], [0:1]} | slice | bytes 8 | tf_op jit(solution)/shard_map/slice | solution.py:352
  9.6 0.5 %slice.83 = f32[1,1,1,1]{3,2,1,0:T(1,128)} slice(f32[1,1,65,128]{3,2,1,0:T(8,128)S(1)} %bitcast.33), slice={[0:1], [0:1], [64:65], [0:1]} | slice | bytes 8 | tf_op jit(solution)/shard_map/slice.67
  11.5 0.0 copy-start.6
  11.5 0.1 scatter-add.10
  11.6 1.6 %collective-permute-start.1 = (f32[2,65,128]{2,1,0:T(8,128)S(1)}, f32[2,65,128]{2,1,0:T(8,128)S(1)}, u32[]{:S(2)}, u32[]{:S(2)}) collective-permute-start(f32[2,65,128]{2,1,0:T(8,128)S(1)} %scatter-add.10), channel_id=1, source_target_pairs={{0,8},{2,10},{4,12},{6,14},{8,0},{10,2},{12,4},{14,6},{16,24},{18,... | collective-permute-start | bytes 199688 | tf_op jit(solution)/shard_map/ppermute | solution.py:304
  13.2 0.1 exponential_multiply_fusion.1
  13.3 2.7 %shard_map.131 = (f32[30,64,64]{2,1,0:T(8,128)}, f32[30,64,64]{2,1,0:T(8,128)}, f32[1,1]{1,0:T(1,128)}) custom-call(f32[30]{0:T(128)} %top_len_ref.1, f32[64,64]{1,0:T(8,128)} %v_ref.7, f32[64,64]{1,0:T(8,128)} %vi_ref.7, f32[1,64]{1,0:T(1,128)} %bitcast.37), custom_call_target="tpu_custom_call" | custom-call | tf_op jit(solution)/shard_map/pallas_call | solution.py:139
  16.0 0.0 collective-permute-done.1
  16.0 0.1 copy.15
  16.1 0.5 %slice.85 = f32[1,1,1]{2,0,1:T(1,128)} slice(f32[4,65,128]{2,0,1:T(4,128)S(1)} %bitcast.26), slice={[0:1], [64:65], [0:1]} | slice | bytes 8 | tf_op jit(solution)/shard_map/slice.68
  17.9 1.6 %collective-permute-start.2 = (f32[4,65,128]{2,0,1:T(4,128)S(1)}, f32[4,65,128]{2,0,1:T(4,128)S(1)}, u32[]{:S(2)}, u32[]{:S(2)}) collective-permute-start(f32[4,65,128]{2,0,1:T(4,128)S(1)} %scatter-add.11), channel_id=1, source_target_pairs={{0,4},{2,6},{4,0},{6,2},{8,12},{10,14},{12,8},{14,10},{16,20},{18,... | collective-permute-start | bytes 399368 | tf_op jit(solution)/shard_map/ppermute | solution.py:304
  19.5 1.2 %fusion.11.jl_ref = f32[14,64,64]{2,1,0:T(8,128)} fusion(f32[14]{0:T(128)S(1)} %copy-done.6, f32[64,64]{1,0:T(8,128)S(1)} %broadcast_subtract_fusion, f32[14,64]{1,0:T(8,128)S(1)} %exponential_multiply_fusion.1), kind=kLoop, calls=%fused_computation.21 | loop fusion | flops 688128 | bytes 249400 | tf_op jit(solution)/shard_map/vmap()/mul | solution.py:31
  20.7 2.9 %shard_map.132 = (f32[14,64,128]{2,1,0:T(8,128)}, f32[14,64,64]{2,1,0:T(8,128)}, f32[64,64]{1,0:T(8,128)}, f32[1,1]{1,0:T(1,128)}) custom-call(f32[64,64]{1,0:T(8,128)} %v_ref.7, f32[64,64]{1,0:T(8,128)} %vi_ref.7, f32[64,64]{1,0:T(8,128)} %lab_ref.1, f32[14,64,64]{2,1,0:T(8,128)} %fusion.11.jl_ref, f32[64,1792]{1,0:T(8,128)} %get-tuple-element.55.xw_ref, ...), custom_call_target="tpu_custom_call" | custom-call | tf_op jit(solution)/shard_map/pallas_call | solution.py:108
  23.6 0.1 pad_maximum_fusion
  23.7 0.5 %slice.86 = f32[1,1,1]{2,1,0:T(1,128)} slice(f32[8,65,128]{2,1,0:T(8,128)S(1)} %bitcast.24), slice={[0:1], [64:65], [0:1]} | slice | bytes 8 | tf_op jit(solution)/shard_map/slice.69
  25.5 0.0 copy-start.9
  25.6 0.1 scatter-add.14.gat0_ref
  25.6 0.1 collective-permute-start.3
  25.7 0.5 %copy-done.9 = s32[128]{0:T(128)S(1)} copy-done((s32[128]{0:T(128)S(1)}, s32[128]{0:T(128)}, u32[]{:S(2)}) %copy-start.9) | copy-done | bytes 536
  26.2 1.5 %collective-permute-start.4 = (f32[1,128]{1,0:T(1,128)S(1)}, f32[1,128]{1,0:T(1,128)S(1)}, u32[]{:S(2)}, u32[]{:S(2)}) collective-permute-start(f32[1,128]{1,0:T(1,128)S(1)} %convert_bitcast_fusion.w_ref), channel_id=1, source_target_pairs={{0,1},{1,0},{2,3},{3,2},{4,5},{5,4},{6,7},{7,6},{8,9},{9,8},{10,11... | collective-permute-start | bytes 1544 | tf_op jit(solution)/shard_map/ppermute | solution.py:335
  27.7 2.0 %collective-permute-done.4.wo_ref = f32[1,128]{1,0:T(1,128)S(1)} collective-permute-done((f32[1,128]{1,0:T(1,128)S(1)}, f32[1,128]{1,0:T(1,128)S(1)}, u32[]{:S(2)}, u32[]{:S(2)}) %collective-permute-start.4) | collective-permute-done | bytes 544 | tf_op jit(solution)/shard_map/ppermute | solution.py:335
  29.8 0.5 %copy-done.8 = f32[1,128]{1,0:T(1,128)} copy-done((f32[1,128]{1,0:T(1,128)}, f32[1,128]{1,0:T(1,128)S(1)}, u32[]{:S(2)}) %copy-start.8) | copy-done | bytes 536
  30.3 0.2 copy-done.2
  30.5 10.8 %shard_map.133 = (f32[1,14]{1,0:T(1,128)}, f32[1,30]{1,0:T(1,128)}, f32[1,128]{1,0:T(1,128)}) custom-call(s32[30]{0:T(128)} %tpar_ref.1, s32[1]{0:T(128)} %bitcast.pick_ref, s32[14]{0:T(128)} %lpar_ref.1, f32[8,65,128]{2,1,0:T(8,128)} %copy-done.1, f32[8,65,128]{2,1,0:T(8,128)} %copy-done.2, f32[30,64,64]{2,1,0:T(8,128)} %get-tuple-element.58.tp_ref, ...), custom_call_target="tpu_custom_call" | custom-call | tf_op jit(solution)/shard_map/pallas_call | solution.py:274
  41.3 0.7 %copy-done.10 = f32[1,14]{1,0:T(1,128)S(1)} copy-done((f32[1,14]{1,0:T(1,128)S(1)}, f32[1,14]{1,0:T(1,128)}, u32[]{:S(2)}) %copy-start.10) | copy-done | bytes 80
  41.9 0.0 copy-done.11
  42.0 5.4 %all-reduce = (f32[14]{0:T(128)}, f32[30]{0:T(128)}) all-reduce(f32[14]{0:T(128)S(1)} %bitcast.40, f32[30]{0:T(128)S(1)} %bitcast.41), channel_id=1, replica_groups=mesh['leaf'=16,'site'=2] {'site'}, use_global_device_ids=true, to_apply=%region_0.1 | all-reduce | flops 44 | bytes 352 | tf_op jit(solution)/shard_map/psum | solution.py:366
  (25 shorter events, 0.1 us)
Async XLA Ops:
  4.1 4.1 %copy-start.4 = (f32[64]{0:T(128)S(1)}, f32[64]{0:T(128)}, u32[]{:S(2)}) copy-start(f32[64]{0:T(128)} %param.25) | copy-start | bytes 772
  4.1 4.2 %copy-start.5 = (f32[30]{0:T(128)S(1)}, f32[30]{0:T(128)}, u32[]{:S(2)}) copy-start(f32[30]{0:T(128)} %top_len_ref.1) | copy-start | bytes 364
  4.1 7.4 %collective-permute-start = (f32[1,65,128]{2,1,0:T(8,128)}, f32[1,65,128]{2,1,0:T(8,128)S(1)}, u32[]{:S(2)}, u32[]{:S(2)}) collective-permute-start(f32[1,65,128]{2,1,0:T(8,128)} %bitcast.32), channel_id=1, source_target_pairs={{0,16},{2,18},{4,20},{6,22},{8,24},{10,26},{12,28},{14,30},{16,0},... | collective-permute-start | bytes 99848 | tf_op jit(solution)/shard_map/ppermute | solution.py:304
  8.3 1.3 %copy-start.3 = (f32[65,128]{1,0:T(8,128)S(1)}, f32[65,128]{1,0:T(8,128)}, u32[]{:S(2)}) copy-start(f32[65,128]{1,0:T(8,128)} %get-tuple-element.53) | copy-start | bytes 99844
  9.1 14.6 %copy-start = (f32[30,64,64]{2,1,0:T(8,128)}, f32[30,64,64]{2,1,0:T(8,128)S(1)}, u32[]{:S(2)}) copy-start(f32[30,64,64]{2,1,0:T(8,128)S(1)} %fusion.4.jt_ref) | copy-start | bytes 1474564
  11.5 1.7 %copy-start.6 = (f32[14]{0:T(128)S(1)}, f32[14]{0:T(128)}, u32[]{:S(2)}) copy-start(f32[14]{0:T(128)} %len_ref.1) | copy-start | bytes 172
  11.6 4.4 %collective-permute-start.1 = (f32[2,65,128]{2,1,0:T(8,128)S(1)}, f32[2,65,128]{2,1,0:T(8,128)S(1)}, u32[]{:S(2)}, u32[]{:S(2)}) collective-permute-start(f32[2,65,128]{2,1,0:T(8,128)S(1)} %scatter-add.10), channel_id=1, source_target_pairs={{0,8},{2,10},{4,12},{6,14},{8,0},{10,2},{12,4},{14,6},{16,24},{18,... | collective-permute-start | bytes 199688 | tf_op jit(solution)/shard_map/ppermute | solution.py:304
  17.9 5.7 %collective-permute-start.2 = (f32[4,65,128]{2,0,1:T(4,128)S(1)}, f32[4,65,128]{2,0,1:T(4,128)S(1)}, u32[]{:S(2)}, u32[]{:S(2)}) collective-permute-start(f32[4,65,128]{2,0,1:T(4,128)S(1)} %scatter-add.11), channel_id=1, source_target_pairs={{0,4},{2,6},{4,0},{6,2},{8,12},{10,14},{12,8},{14,10},{16,20},{18,... | collective-permute-start | bytes 399368 | tf_op jit(solution)/shard_map/ppermute | solution.py:304
  25.5 0.7 %copy-start.9 = (s32[128]{0:T(128)S(1)}, s32[128]{0:T(128)}, u32[]{:S(2)}) copy-start(s32[128]{0:T(128)} %param.22) | copy-start | bytes 1540
  25.6 4.7 %copy-start.1 = (f32[8,65,128]{2,1,0:T(8,128)}, f32[8,65,128]{2,1,0:T(8,128)S(1)}, u32[]{:S(2)}) copy-start(f32[8,65,128]{2,1,0:T(8,128)S(1)} %scatter-add.14.gat0_ref) | copy-start | bytes 798724
  25.6 4.1 %collective-permute-start.3 = (f32[8,65,128]{2,1,0:T(8,128)S(1)}, f32[8,65,128]{2,1,0:T(8,128)S(1)}, u32[]{:S(2)}, u32[]{:S(2)}) collective-permute-start(f32[8,65,128]{2,1,0:T(8,128)S(1)} %scatter-add.14.gat0_ref), channel_id=1, source_target_pairs={{0,2},{2,0},{4,6},{6,4},{8,10},{10,8},{12,14},{14,12},{16,18},{18,... | collective-permute-start | bytes 798728 | tf_op jit(solution)/shard_map/ppermute | solution.py:304
  26.2 1.5 %copy-start.7 = (f32[1,128]{1,0:T(1,128)}, f32[1,128]{1,0:T(1,128)S(1)}, u32[]{:S(2)}) copy-start(f32[1,128]{1,0:T(1,128)S(1)} %convert_bitcast_fusion.w_ref) | copy-start | bytes 1540
  26.2 3.6 %collective-permute-start.4 = (f32[1,128]{1,0:T(1,128)S(1)}, f32[1,128]{1,0:T(1,128)S(1)}, u32[]{:S(2)}, u32[]{:S(2)}) collective-permute-start(f32[1,128]{1,0:T(1,128)S(1)} %convert_bitcast_fusion.w_ref), channel_id=1, source_target_pairs={{0,1},{1,0},{2,3},{3,2},{4,5},{5,4},{6,7},{7,6},{8,9},{9,8},{10,11... | collective-permute-start | bytes 1544 | tf_op jit(solution)/shard_map/ppermute | solution.py:335
  29.8 0.5 %copy-start.8 = (f32[1,128]{1,0:T(1,128)}, f32[1,128]{1,0:T(1,128)S(1)}, u32[]{:S(2)}) copy-start(f32[1,128]{1,0:T(1,128)S(1)} %collective-permute-done.4.wo_ref) | copy-start | bytes 1540
  29.8 0.7 %copy-start.2 = (f32[8,65,128]{2,1,0:T(8,128)}, f32[8,65,128]{2,1,0:T(8,128)S(1)}, u32[]{:S(2)}) copy-start(f32[8,65,128]{2,1,0:T(8,128)S(1)} %collective-permute-done.3.gat1_ref) | copy-start | bytes 798724
  41.3 0.7 %copy-start.10 = (f32[1,14]{1,0:T(1,128)S(1)}, f32[1,14]{1,0:T(1,128)}, u32[]{:S(2)}) copy-start(f32[1,14]{1,0:T(1,128)} %get-tuple-element.64) | copy-start | bytes 172
  41.3 0.7 %copy-start.11 = (f32[1,30]{1,0:T(1,128)S(1)}, f32[1,30]{1,0:T(1,128)}, u32[]{:S(2)}) copy-start(f32[1,30]{1,0:T(1,128)} %get-tuple-element.65) | copy-start | bytes 364

commit v10 on v5

--- a/solution.py
+++ b/solution.py
@@ -87,8 +87,8 @@
     )(parents, lengths, tips, vecs, inv, lam_row)
 
 
-def _matrix_kernel(top_len_ref, v_ref, vi_ref, lab_ref, lam_ref, jl_ref, xw_ref, trl_ref,
-                   mixed_ref, ptl_ref, tp_ref, tpt_ref, basis_ref, vw_ref):
+def _matrix_kernel(top_len_ref, v_ref, vi_ref, lab_ref, lam_ref, jl_ref, xw_ref,
+                   mixed_ref, tp_ref, basis_ref, vw_ref):
     local_edges, states, columns = mixed_ref.shape
     top_edges = tp_ref.shape[0]
     vecs = v_ref[...]
@@ -99,15 +99,12 @@
     vw_ref[...] = _dot(inv, xw_ref[...])
     for c in range(local_edges):
         mixed_ref[c] = _dot(basis * jl_ref[c], vw_ref[:, _cols(c, columns)])
-        ptl_ref[c] = trl_ref[c].T
     for c in range(top_edges):
-        trans = _dot(vecs * jnp.exp(lam * top_len_ref[c]), inv)
-        tp_ref[c] = trans
-        tpt_ref[c] = trans.T
-
-
-def matrices(top_lengths, vecs, inv, labeled, lam_row, j_local, xw, trl):
-    local_edges, states, _ = trl.shape
+        tp_ref[c] = _dot(vecs * jnp.exp(lam * top_len_ref[c]), inv)
+
+
+def matrices(top_lengths, vecs, inv, labeled, lam_row, j_local, xw):
+    local_edges, states, _ = j_local.shape
     columns = xw.shape[1] // local_edges
     top_edges = top_lengths.shape[0]
     sq = (states, states)
@@ -115,16 +112,14 @@
         _matrix_kernel,
         out_shape=(
             jax.ShapeDtypeStruct((local_edges, states, columns), F32),
-            jax.ShapeDtypeStruct((local_edges,) + sq, F32),
-            jax.ShapeDtypeStruct((top_edges,) + sq, F32),
             jax.ShapeDtypeStruct((top_edges,) + sq, F32),
             jax.ShapeDtypeStruct(sq, F32),
         ),
-        in_specs=[SMEM] + [VMEM] * 7,
-        out_specs=(VMEM,) * 5,
+        in_specs=[SMEM] + [VMEM] * 6,
+        out_specs=(VMEM,) * 3,
         scratch_shapes=[pltpu.VMEM((states, local_edges * columns), F32)],
         compiler_params=PARAMS,
-    )(top_lengths, vecs, inv, labeled, lam_row, j_local, xw, trl)
+    )(top_lengths, vecs, inv, labeled, lam_row, j_local, xw)
 
 
 def _lane_put(row, lane, value):
@@ -149,7 +144,8 @@
         return outside_ref[p - leaf_count] * msg_ref[s]
 
     def outward(c, arriving):
-        out = _dot(pt_ref[c], arriving)
+        out = lax.dot_general(pt_ref[c], arriving, (((0,), (0,)), ((), ())),
+                              precision=FAST, preferred_element_type=F32)
         return out / jnp.max(out, axis=0, keepdims=True)
 
     for c in range(edge_count - 1, -1, -1):
@@ -325,9 +321,10 @@
         pick = jnp.zeros((1,), jnp.int32)
     j_local = jax.vmap(lambda t: integrals(eig_values, t))(branch_lengths)
     j_top = jax.vmap(lambda t: integrals(eig_values, t))(top_lengths)
-    lmixed, lpt, tp, tpt, basis = matrices(
-        top_lengths, eig_vectors, eig_inverse, labeled_rates, lam_row, j_local, xw, trl
-    )
+    lmixed, tp, basis = matrices(
+        top_lengths, eig_vectors, eig_inverse, labeled_rates, lam_row, j_local, xw
+    )
+    lpt, tpt = trl, tp
     local_row, top_row, loglik = join(
         top_parents, pick, parents, halves, tp, tpt, basis, j_top, eig_vectors, eig_inverse,
         root_freq[None, :], w_row, w_other, msgs, lmixed, lpt, taxon_count, paired,

time: 43.8 us -> 43.4 us (level)
  Pallas kernels: 18 us -> 17.4 us
  local copies, waits for them, and re-layouts: 1.5 us -> 2.05 us
    unnamed x22, local copies, waits for them, and re-layouts: 1.4 us -> 1.96 us
    pallas_call x1, Pallas kernels: 3.77 us -> 3.24 us  [matrices(): pl.pallas_call(_matrix_kernel, out_shape=(jax.ShapeDtypeStruct((local_edg...]
  transfers between devices with their start and end apart: 5 -> 5, of which waited for: 3 -> 3; matrix products, arithmetic and copies ran while one was open for 8% -> 7% of each run, Pallas kernels for 9% -> 8%
where the time goes in v10:
time: 43.4 us; the launch traced here: 43.2 us
  Pallas kernels  17.4 us (40%)
  starting transfers between devices  9.03 us (21%)
  blocking collectives  5.41 us (12%)
  waiting for transfers between devices  5.36 us (12%)
  other arithmetic  3.13 us (7%)
  local copies, waits for them, and re-layouts  2.05 us (5%)
  between operations  0.75 us (2%)
    pallas_call x1, Pallas kernels, join(): pl.pallas_call(functools.partial(_join_kernel, taxon_count=taxon_count, p...  10.7 us
    ppermute x4, starting transfers between devices, gather_roots(): other = lax.ppermute(buf, 'leaf', [(i, i ^ step) for i in range(groups)])  7.52 us
    psum x1, blocking collectives, on_device(): local_sum, top_sum = lax.psum((local_row[0], top_row[0]), 'site')  5.41 us
    ppermute x4, waiting for transfers between devices, gather_roots(): other = lax.ppermute(buf, 'leaf', [(i, i ^ step) for i in range(groups)])  5.36 us
    pallas_call x1, Pallas kernels, climb(): pl.pallas_call(_climb_kernel, out_shape=(jax.ShapeDtypeStruct((states + 1...  3.47 us
    pallas_call x1, Pallas kernels, matrices(): pl.pallas_call(_matrix_kernel, out_shape=(jax.ShapeDtypeStruct((local_edg...  3.24 us
    mul x4, other arithmetic, integrals(): return branch * jnp.exp(eig_values[None, :] * branch) * growth  2.97 us
    unnamed x22, local copies, waits for them, and re-layouts  1.96 us
  transfers between devices with their start and end apart: 5, of which 3 were waited for; matrix products, arithmetic and copies ran while one was open for 7% of the time, Pallas kernels for 8%

profile of v10, /device:TPU:0, one launch (start us, length us, event | category | flops | bytes accessed | tf_op | source)
XLA Modules:
  0.0 43.2 jit_solution(7719620249149982163)
XLA Ops:
  0.6 0.0 copy-start.8
  0.6 0.0 copy-start.3
  0.7 3.5 %shard_map.130 = (f32[65,128]{1,0:T(8,128)}, f32[14,64,128]{2,1,0:T(8,128)}, f32[64,1792]{1,0:T(8,128)}, f32[14,64,64]{2,1,0:T(8,128)}) custom-call(s32[14]{0:T(128)} %lpar_ref.1, f32[14]{0:T(128)} %len_ref.1, f32[8,64,128]{2,1,0:T(8,128)} %leaf_ref.1, f32[64,64]{1,0:T(8,128)} %v_ref.5, f32[64,64]{1,0:T(8,128)} %vi_ref.5, f32[1,64]{1,0:T(1,128)} %bitcast.29), custom_call_target="tpu_custom_call" | custom-call | tf_op jit(solution)/shard_map/pallas_call | solution.py:75
  4.1 4.1 %collective-permute-start = (f32[1,65,128]{2,1,0:T(8,128)}, f32[1,65,128]{2,1,0:T(8,128)S(1)}, u32[]{:S(2)}, u32[]{:S(2)}) collective-permute-start(f32[1,65,128]{2,1,0:T(8,128)} %bitcast.26), channel_id=1, source_target_pairs={{0,16},{2,18},{4,20},{6,22},{8,24},{10,26},{12,28},{14,30},{16,0},... | collective-permute-start | bytes 99848 | tf_op jit(solution)/shard_map/ppermute | solution.py:278
  8.3 1.5 %collective-permute-start.4 = (f32[1,128]{1,0:T(1,128)S(1)}, f32[1,128]{1,0:T(1,128)S(1)}, u32[]{:S(2)}, u32[]{:S(2)}) collective-permute-start(f32[1,128]{1,0:T(1,128)S(1)} %convert_bitcast_fusion.w_ref), channel_id=1, source_target_pairs={{0,1},{1,0},{2,3},{3,2},{4,5},{5,4},{6,7},{7,6},{8,9},{9,8},{10,11... | collective-permute-start | bytes 1544 | tf_op jit(solution)/shard_map/ppermute | solution.py:306
  9.8 0.0 copy-done.3
  9.8 0.1 broadcast_subtract_fusion
  9.9 0.9 %collective-permute-done = f32[1,65,128]{2,1,0:T(8,128)S(1)} collective-permute-done((f32[1,65,128]{2,1,0:T(8,128)}, f32[1,65,128]{2,1,0:T(8,128)S(1)}, u32[]{:S(2)}, u32[]{:S(2)}) %collective-permute-start) | collective-permute-done | bytes 33312 | tf_op jit(solution)/shard_map/ppermute | solution.py:278
  10.8 0.0 copy-start.4
  10.8 1.6 %collective-permute-start.1 = (f32[2,65,128]{2,1,0:T(8,128)S(1)}, f32[2,65,128]{2,1,0:T(8,128)S(1)}, u32[]{:S(2)}, u32[]{:S(2)}) collective-permute-start(f32[2,65,128]{2,1,0:T(8,128)S(1)} %get-tuple-element.26), channel_id=1, source_target_pairs={{0,8},{2,10},{4,12},{6,14},{8,0},{10,2},{12,4},{14,6},{16,24},{18,... | collective-permute-start | bytes 199688 | tf_op jit(solution)/shard_map/ppermute | solution.py:278
  12.4 0.1 exponential_multiply_fusion
  12.5 2.8 %collective-permute-done.1 = f32[2,65,128]{2,1,0:T(8,128)S(1)} collective-permute-done((f32[2,65,128]{2,1,0:T(8,128)S(1)}, f32[2,65,128]{2,1,0:T(8,128)S(1)}, u32[]{:S(2)}, u32[]{:S(2)}) %collective-permute-start.1) | collective-permute-done | bytes 66592 | tf_op jit(solution)/shard_map/ppermute | solution.py:278
  15.3 0.1 copy.14
  15.3 1.7 %collective-permute-start.2 = (f32[4,65,128]{2,0,1:T(4,128)S(1)}, f32[4,65,128]{2,0,1:T(4,128)S(1)}, u32[]{:S(2)}, u32[]{:S(2)}) collective-permute-start(f32[4,65,128]{2,0,1:T(4,128)S(1)} %bitcast.22), channel_id=1, source_target_pairs={{0,4},{2,6},{4,0},{6,2},{8,12},{10,14},{12,8},{14,10},{16,20},{18,... | collective-permute-start | bytes 399368 | tf_op jit(solution)/shard_map/ppermute | solution.py:278
  17.1 1.7 %fusion.4.jt_ref = f32[30,64,64]{2,1,0:T(8,128)} fusion(f32[30]{0:T(128)S(1)} %copy-done.4, f32[64,64]{1,0:T(8,128)S(1)} %broadcast_subtract_fusion, f32[30,64]{1,0:T(8,128)S(1)} %exponential_multiply_fusion), kind=kLoop, calls=%fused_computation.14 | loop fusion | flops 1474560 | bytes 515704 | tf_op jit(solution)/shard_map/vmap()/mul | solution.py:31
  18.8 1.6 %collective-permute-done.2 = f32[4,65,128]{2,0,1:T(4,128)S(1)} collective-permute-done((f32[4,65,128]{2,0,1:T(4,128)S(1)}, f32[4,65,128]{2,0,1:T(4,128)S(1)}, u32[]{:S(2)}, u32[]{:S(2)}) %collective-permute-start.2) | collective-permute-done | bytes 133152 | tf_op jit(solution)/shard_map/ppermute | solution.py:278
  20.4 0.1 pad_maximum_fusion
  20.5 0.0 copy-start.5
  20.5 0.1 collective-permute-start.3
  20.6 0.6 %copy-done.5 = f32[14]{0:T(128)S(1)} copy-done((f32[14]{0:T(128)S(1)}, f32[14]{0:T(128)}, u32[]{:S(2)}) %copy-start.5) | copy-done | bytes 80
  21.2 0.1 exponential_multiply_fusion.1
  21.3 1.2 %fusion.11.jl_ref = f32[14,64,64]{2,1,0:T(8,128)} fusion(f32[14]{0:T(128)S(1)} %copy-done.5, f32[64,64]{1,0:T(8,128)S(1)} %broadcast_subtract_fusion, f32[14,64]{1,0:T(8,128)S(1)} %exponential_multiply_fusion.1), kind=kLoop, calls=%fused_computation.21 | loop fusion | flops 688128 | bytes 249400 | tf_op jit(solution)/shard_map/vmap()/mul | solution.py:31
  22.4 3.2 %shard_map.131 = (f32[14,64,128]{2,1,0:T(8,128)}, f32[30,64,64]{2,1,0:T(8,128)}, f32[64,64]{1,0:T(8,128)}) custom-call(f32[30]{0:T(128)} %top_len_ref.1, f32[64,64]{1,0:T(8,128)} %v_ref.5, f32[64,64]{1,0:T(8,128)} %vi_ref.5, f32[64,64]{1,0:T(8,128)} %lab_ref.1, f32[1,64]{1,0:T(1,128)} %bitcast.30, f32[14,64,64]{2,1,0:T(8,128)} %fusion.11.jl_ref, ...), custom_call_target="tpu_custom_call" | custom-call | tf_op jit(solution)/shard_map/pallas_call | solution.py:111
  25.7 0.0 collective-permute-done.4.wo_ref
  25.7 0.0 collective-permute-done.3.gat1_ref
  25.7 0.0 copy-start.1
  25.7 0.5 %copy-done.7 = f32[1,128]{1,0:T(1,128)} copy-done((f32[1,128]{1,0:T(1,128)}, f32[1,128]{1,0:T(1,128)S(1)}, u32[]{:S(2)}) %copy-start.7) | copy-done | bytes 536
  26.2 0.2 copy-done.1
  26.4 10.7 %shard_map.132 = (f32[1,14]{1,0:T(1,128)}, f32[1,30]{1,0:T(1,128)}, f32[1,128]{1,0:T(1,128)}) custom-call(s32[30]{0:T(128)} %tpar_ref.1, s32[1]{0:T(128)} %bitcast.pick_ref, s32[14]{0:T(128)} %lpar_ref.1, f32[8,65,128]{2,1,0:T(8,128)} %bitcast.21, f32[8,65,128]{2,1,0:T(8,128)} %copy-done.1, f32[30,64,64]{2,1,0:T(8,128)} %get-tuple-element.15.tp_ref.tpt_ref, ...), custom_call_target="tpu_custom_call" | custom-call | tf_op jit(solution)/shard_map/pallas_call | solution.py:248
  37.1 0.6 %copy-done.9 = f32[1,14]{1,0:T(1,128)S(1)} copy-done((f32[1,14]{1,0:T(1,128)S(1)}, f32[1,14]{1,0:T(1,128)}, u32[]{:S(2)}) %copy-start.9) | copy-done | bytes 80
  37.8 0.0 copy-done.10
  37.8 5.4 %all-reduce = (f32[14]{0:T(128)}, f32[30]{0:T(128)}) all-reduce(f32[14]{0:T(128)S(1)} %bitcast.33, f32[30]{0:T(128)S(1)} %bitcast.34), channel_id=1, replica_groups=mesh['leaf'=16,'site'=2] {'site'}, use_global_device_ids=true, to_apply=%region_0.1 | all-reduce | flops 44 | bytes 352 | tf_op jit(solution)/shard_map/psum | solution.py:332
  (15 shorter events, 0.1 us)
Async XLA Ops:
  0.6 7.6 %copy-start.8 = (s32[128]{0:T(128)S(1)}, s32[128]{0:T(128)}, u32[]{:S(2)}) copy-start(s32[128]{0:T(128)} %param.16) | copy-start | bytes 1540
  0.6 9.1 %copy-start.3 = (f32[64]{0:T(128)S(1)}, f32[64]{0:T(128)}, u32[]{:S(2)}) copy-start(f32[64]{0:T(128)} %param.19) | copy-start | bytes 772
  4.1 6.7 %copy-start.2 = (f32[65,128]{1,0:T(8,128)S(1)}, f32[65,128]{1,0:T(8,128)}, u32[]{:S(2)}) copy-start(f32[65,128]{1,0:T(8,128)} %get-tuple-element.13) | copy-start | bytes 99844
  4.1 6.7 %collective-permute-start = (f32[1,65,128]{2,1,0:T(8,128)}, f32[1,65,128]{2,1,0:T(8,128)S(1)}, u32[]{:S(2)}, u32[]{:S(2)}) collective-permute-start(f32[1,65,128]{2,1,0:T(8,128)} %bitcast.26), channel_id=1, source_target_pairs={{0,16},{2,18},{4,20},{6,22},{8,24},{10,26},{12,28},{14,30},{16,0},... | collective-permute-start | bytes 99848 | tf_op jit(solution)/shard_map/ppermute | solution.py:278
  8.3 1.6 %copy-start.6 = (f32[1,128]{1,0:T(1,128)}, f32[1,128]{1,0:T(1,128)S(1)}, u32[]{:S(2)}) copy-start(f32[1,128]{1,0:T(1,128)S(1)} %convert_bitcast_fusion.w_ref) | copy-start | bytes 1540
  8.3 17.4 %collective-permute-start.4 = (f32[1,128]{1,0:T(1,128)S(1)}, f32[1,128]{1,0:T(1,128)S(1)}, u32[]{:S(2)}, u32[]{:S(2)}) collective-permute-start(f32[1,128]{1,0:T(1,128)S(1)} %convert_bitcast_fusion.w_ref), channel_id=1, source_target_pairs={{0,1},{1,0},{2,3},{3,2},{4,5},{5,4},{6,7},{7,6},{8,9},{9,8},{10,11... | collective-permute-start | bytes 1544 | tf_op jit(solution)/shard_map/ppermute | solution.py:306
  10.8 1.6 %copy-start.4 = (f32[30]{0:T(128)S(1)}, f32[30]{0:T(128)}, u32[]{:S(2)}) copy-start(f32[30]{0:T(128)} %top_len_ref.1) | copy-start | bytes 364
  10.8 4.4 %collective-permute-start.1 = (f32[2,65,128]{2,1,0:T(8,128)S(1)}, f32[2,65,128]{2,1,0:T(8,128)S(1)}, u32[]{:S(2)}, u32[]{:S(2)}) collective-permute-start(f32[2,65,128]{2,1,0:T(8,128)S(1)} %get-tuple-element.26), channel_id=1, source_target_pairs={{0,8},{2,10},{4,12},{6,14},{8,0},{10,2},{12,4},{14,6},{16,24},{18,... | collective-permute-start | bytes 199688 | tf_op jit(solution)/shard_map/ppermute | solution.py:278
  15.3 5.1 %collective-permute-start.2 = (f32[4,65,128]{2,0,1:T(4,128)S(1)}, f32[4,65,128]{2,0,1:T(4,128)S(1)}, u32[]{:S(2)}, u32[]{:S(2)}) collective-permute-start(f32[4,65,128]{2,0,1:T(4,128)S(1)} %bitcast.22), channel_id=1, source_target_pairs={{0,4},{2,6},{4,0},{6,2},{8,12},{10,14},{12,8},{14,10},{16,20},{18,... | collective-permute-start | bytes 399368 | tf_op jit(solution)/shard_map/ppermute | solution.py:278
  20.5 5.2 %copy-start = (f32[4,2,65,128]{3,2,1,0:T(8,128)}, f32[4,2,65,128]{3,2,1,0:T(8,128)S(1)}, u32[]{:S(2)}) copy-start(f32[4,2,65,128]{3,2,1,0:T(8,128)S(1)} %copy.16) | copy-start | bytes 798724
  20.5 0.7 %copy-start.5 = (f32[14]{0:T(128)S(1)}, f32[14]{0:T(128)}, u32[]{:S(2)}) copy-start(f32[14]{0:T(128)} %len_ref.1) | copy-start | bytes 172
  20.5 5.2 %collective-permute-start.3 = (f32[8,65,128]{2,1,0:T(8,128)S(1)}, f32[8,65,128]{2,1,0:T(8,128)S(1)}, u32[]{:S(2)}, u32[]{:S(2)}) collective-permute-start(f32[8,65,128]{2,1,0:T(8,128)S(1)} %bitcast.20), channel_id=1, source_target_pairs={{0,2},{2,0},{4,6},{6,4},{8,10},{10,8},{12,14},{14,12},{16,18},{18,... | collective-permute-start | bytes 798728 | tf_op jit(solution)/shard_map/ppermute | solution.py:278
  25.7 0.5 %copy-start.7 = (f32[1,128]{1,0:T(1,128)}, f32[1,128]{1,0:T(1,128)S(1)}, u32[]{:S(2)}) copy-start(f32[1,128]{1,0:T(1,128)S(1)} %collective-permute-done.4.wo_ref) | copy-start | bytes 1540
  25.7 0.7 %copy-start.1 = (f32[8,65,128]{2,1,0:T(8,128)}, f32[8,65,128]{2,1,0:T(8,128)S(1)}, u32[]{:S(2)}) copy-start(f32[8,65,128]{2,1,0:T(8,128)S(1)} %collective-permute-done.3.gat1_ref) | copy-start | bytes 798724
  37.1 0.6 %copy-start.9 = (f32[1,14]{1,0:T(1,128)S(1)}, f32[1,14]{1,0:T(1,128)}, u32[]{:S(2)}) copy-start(f32[1,14]{1,0:T(1,128)} %get-tuple-element.20) | copy-start | bytes 172
  37.1 0.6 %copy-start.10 = (f32[1,30]{1,0:T(1,128)S(1)}, f32[1,30]{1,0:T(1,128)}, u32[]{:S(2)}) copy-start(f32[1,30]{1,0:T(1,128)} %get-tuple-element.21) | copy-start | bytes 364

commit v11 on v10

--- a/solution.py
+++ b/solution.py
@@ -87,8 +87,9 @@
     )(parents, lengths, tips, vecs, inv, lam_row)
 
 
-def _matrix_kernel(top_len_ref, v_ref, vi_ref, lab_ref, lam_ref, jl_ref, xw_ref,
-                   mixed_ref, tp_ref, basis_ref, vw_ref):
+def _matrix_kernel(top_len_ref, v_ref, vi_ref, lab_ref, lam_ref, jl_ref, xw_ref, carry_ref,
+                   mixed_ref, tp_ref, basis_ref, carried_ref, vw_ref):
+    carried_ref[...] = carry_ref[...]
     local_edges, states, columns = mixed_ref.shape
     top_edges = tp_ref.shape[0]
     vecs = v_ref[...]
@@ -103,7 +104,7 @@
         tp_ref[c] = _dot(vecs * jnp.exp(lam * top_len_ref[c]), inv)
 
 
-def matrices(top_lengths, vecs, inv, labeled, lam_row, j_local, xw):
+def matrices(top_lengths, vecs, inv, labeled, lam_row, j_local, xw, carry):
     local_edges, states, _ = j_local.shape
     columns = xw.shape[1] // local_edges
     top_edges = top_lengths.shape[0]
@@ -114,12 +115,13 @@
             jax.ShapeDtypeStruct((local_edges, states, columns), F32),
             jax.ShapeDtypeStruct((top_edges,) + sq, F32),
             jax.ShapeDtypeStruct(sq, F32),
+            jax.ShapeDtypeStruct(carry.shape, F32),
         ),
-        in_specs=[SMEM] + [VMEM] * 6,
-        out_specs=(VMEM,) * 3,
+        in_specs=[SMEM] + [VMEM] * 7,
+        out_specs=(VMEM,) * 4,
         scratch_shapes=[pltpu.VMEM((states, local_edges * columns), F32)],
         compiler_params=PARAMS,
-    )(top_lengths, vecs, inv, labeled, lam_row, j_local, xw)
+    )(top_lengths, vecs, inv, labeled, lam_row, j_local, xw, carry)
 
 
 def _lane_put(row, lane, value):
@@ -271,13 +273,15 @@
       w_other, lmsgs, lmixed, lpt)
 
 
-def gather_roots(block, groups):
+def gather_roots(block, groups, hook):
     buf = block[None]
     step = groups // 2
     while step >= 1:
         other = lax.ppermute(buf, "leaf", [(i, i ^ step) for i in range(groups)])
         if step == 1:
             return buf, other
+        if step == max(groups // 4, 1):
+            buf = hook(buf)
         buf = jnp.stack([buf, other], axis=1).reshape((-1,) + block.shape)
         step //= 2
     return buf, buf
@@ -312,18 +316,27 @@
         parents, branch_lengths, tips, eig_vectors, eig_inverse, lam_row
     )
     paired = groups & (groups - 1) == 0
+    j_local = jax.vmap(lambda t: integrals(eig_values, t))(branch_lengths)
+    j_top = jax.vmap(lambda t: integrals(eig_values, t))(top_lengths)
+    made = {}
+
+    def hook(buf):
+        made["m"] = matrices(
+            top_lengths, eig_vectors, eig_inverse, labeled_rates, lam_row, j_local, xw, buf
+        )
+        return made["m"][3]
+
     if paired:
-        halves = gather_roots(root_block, groups)
+        halves = gather_roots(root_block, groups, hook)
         pick = jnp.reshape(member_index, (1,)).astype(jnp.int32)
     else:
         gathered = lax.all_gather(root_block, "leaf", axis=0, tiled=False)
+        hook(root_block[None])
         halves = (gathered, gathered)
         pick = jnp.zeros((1,), jnp.int32)
-    j_local = jax.vmap(lambda t: integrals(eig_values, t))(branch_lengths)
-    j_top = jax.vmap(lambda t: integrals(eig_values, t))(top_lengths)
-    lmixed, tp, basis = matrices(
-        top_lengths, eig_vectors, eig_inverse, labeled_rates, lam_row, j_local, xw
-    )
+    if "m" not in made:
+        hook(root_block[None])
+    lmixed, tp, basis, _ = made["m"]
     lpt, tpt = trl, tp
     local_row, top_row, loglik = join(
         top_parents, pick, parents, halves, tp, tpt, basis, j_top, eig_vectors, eig_inverse,

time: 43.4 us -> 42.5 us (0.979)
  waiting for transfers between devices: 5.36 us -> 4.21 us
  other arithmetic: 3.13 us -> 4.01 us
  local copies, waits for them, and re-layouts: 2.05 us -> 1.47 us
    ppermute x4, waiting for transfers between devices: 5.36 us -> 4.21 us  [gather_roots(): other = lax.ppermute(buf, 'leaf', [(i, i ^ step) for i in range(groups)])]
    another operation x3 -> x2, other arithmetic: 0.09 us -> 0.96 us  [gather_roots(): buf = jnp.stack([buf, other], axis=1).reshape((-1,) + block.shape)]
    unnamed x22 -> x26, local copies, waits for them, and re-layouts: 1.96 us -> 1.38 us
  transfers between devices with their start and end apart: 5 -> 5, of which waited for: 3 -> 2; matrix products, arithmetic and copies ran while one was open for 7% -> 10% of each run, Pallas kernels for 8% -> 8%
where the time goes in v11:
time: 42.5 us; the launch traced here: 42.2 us
  Pallas kernels  17.4 us (41%)
  starting transfers between devices  8.91 us (21%)
  blocking collectives  5.41 us (13%)
  waiting for transfers between devices  4.21 us (10%)
  other arithmetic  4.01 us (9%)
  local copies, waits for them, and re-layouts  1.47 us (3%)
  between operations  0.76 us (2%)
    pallas_call x1, Pallas kernels, join(): pl.pallas_call(functools.partial(_join_kernel, taxon_count=taxon_count, p...  10.7 us
    ppermute x4, starting transfers between devices, gather_roots(): other = lax.ppermute(buf, 'leaf', [(i, i ^ step) for i in range(groups)])  7.32 us
    psum x1, blocking collectives, on_device(): local_sum, top_sum = lax.psum((local_row[0], top_row[0]), 'site')  5.41 us
    ppermute x4, waiting for transfers between devices, gather_roots(): other = lax.ppermute(buf, 'leaf', [(i, i ^ step) for i in range(groups)])  4.21 us
    pallas_call x1, Pallas kernels, climb(): pl.pallas_call(_climb_kernel, out_shape=(jax.ShapeDtypeStruct((states + 1...  3.46 us
    pallas_call x1, Pallas kernels, matrices(): pl.pallas_call(_matrix_kernel, out_shape=(jax.ShapeDtypeStruct((local_edg...  3.24 us
    mul x4, other arithmetic, integrals(): return branch * jnp.exp(eig_values[None, :] * branch) * growth  2.97 us
    ppermute x1, starting transfers between devices, on_device(): w_other = lax.ppermute(w_row, 'site', [(0, 1), (1, 0)])  1.58 us
  transfers between devices with their start and end apart: 5, of which 2 were waited for; matrix products, arithmetic and copies ran while one was open for 10% of the time, Pallas kernels for 8%

profile of v11, /device:TPU:0, one launch (start us, length us, event | category | flops | bytes accessed | tf_op | source)
XLA Modules:
  0.0 42.2 jit_solution(14237759463561608058)
XLA Ops:
  0.6 0.0 copy-start.4
  0.7 3.5 %shard_map.130 = (f32[65,128]{1,0:T(8,128)}, f32[14,64,128]{2,1,0:T(8,128)}, f32[64,1792]{1,0:T(8,128)}, f32[14,64,64]{2,1,0:T(8,128)}) custom-call(s32[14]{0:T(128)} %lpar_ref.1, f32[14]{0:T(128)} %len_ref.1, f32[8,64,128]{2,1,0:T(8,128)} %leaf_ref.1, f32[64,64]{1,0:T(8,128)} %v_ref.5, f32[64,64]{1,0:T(8,128)} %vi_ref.5, f32[1,64]{1,0:T(1,128)} %bitcast.29), custom_call_target="tpu_custom_call" | custom-call | tf_op jit(solution)/shard_map/pallas_call | solution.py:75
  4.1 4.1 %collective-permute-start = (f32[1,65,128]{2,1,0:T(8,128)}, f32[1,65,128]{2,1,0:T(8,128)S(1)}, u32[]{:S(2)}, u32[]{:S(2)}) collective-permute-start(f32[1,65,128]{2,1,0:T(8,128)} %bitcast.26), channel_id=1, source_target_pairs={{0,16},{2,18},{4,20},{6,22},{8,24},{10,26},{12,28},{14,30},{16,0},... | collective-permute-start | bytes 99848 | tf_op jit(solution)/shard_map/ppermute | solution.py:280
  8.3 1.6 %collective-permute-start.4 = (f32[1,128]{1,0:T(1,128)S(1)}, f32[1,128]{1,0:T(1,128)S(1)}, u32[]{:S(2)}, u32[]{:S(2)}) collective-permute-start(f32[1,128]{1,0:T(1,128)S(1)} %convert_bitcast_fusion.w_ref), channel_id=1, source_target_pairs={{0,1},{1,0},{2,3},{3,2},{4,5},{5,4},{6,7},{7,6},{8,9},{9,8},{10,11... | collective-permute-start | bytes 1544 | tf_op jit(solution)/shard_map/ppermute | solution.py:310
  9.8 0.1 broadcast_subtract_fusion
  9.9 0.0 copy-done.7
  9.9 0.1 exponential_multiply_fusion.1
  10.0 0.8 %collective-permute-done = f32[1,65,128]{2,1,0:T(8,128)S(1)} collective-permute-done((f32[1,65,128]{2,1,0:T(8,128)}, f32[1,65,128]{2,1,0:T(8,128)S(1)}, u32[]{:S(2)}, u32[]{:S(2)}) %collective-permute-start) | collective-permute-done | bytes 33312 | tf_op jit(solution)/shard_map/ppermute | solution.py:280
  10.8 1.6 %collective-permute-start.1 = (f32[2,65,128]{2,1,0:T(8,128)S(1)}, f32[2,65,128]{2,1,0:T(8,128)S(1)}, u32[]{:S(2)}, u32[]{:S(2)}) collective-permute-start(f32[2,65,128]{2,1,0:T(8,128)S(1)} %maximum_bitcast_fusion.carry_ref), channel_id=1, source_target_pairs={{0,8},{2,10},{4,12},{6,14},{8,0},{10,2},{12,4},{14,6},{16,24},{18,... | collective-permute-start | bytes 199688 | tf_op jit(solution)/shard_map/ppermute | solution.py:280
  12.4 1.1 %fusion.11.jl_ref = f32[14,64,64]{2,1,0:T(8,128)} fusion(f32[14]{0:T(128)S(1)} %copy-done.7, f32[64,64]{1,0:T(8,128)S(1)} %broadcast_subtract_fusion, f32[14,64]{1,0:T(8,128)S(1)} %exponential_multiply_fusion.1), kind=kLoop, calls=%fused_computation.21 | loop fusion | flops 688128 | bytes 249400 | tf_op jit(solution)/shard_map/vmap()/mul | solution.py:31
  13.5 3.2 %shard_map.131 = (f32[14,64,128]{2,1,0:T(8,128)}, f32[30,64,64]{2,1,0:T(8,128)}, f32[64,64]{1,0:T(8,128)}, f32[2,65,128]{2,1,0:T(8,128)}) custom-call(f32[30]{0:T(128)} %top_len_ref.1, f32[64,64]{1,0:T(8,128)} %v_ref.5, f32[64,64]{1,0:T(8,128)} %vi_ref.5, f32[64,64]{1,0:T(8,128)} %lab_ref.1, f32[1,64]{1,0:T(1,128)} %bitcast.30, ...), custom_call_target="tpu_custom_call" | custom-call | tf_op jit(solution)/shard_map/pallas_call | solution.py:112
  16.8 0.0 collective-permute-done.1
  16.8 0.9 %pad_maximum_fusion.1 = f32[2,2,65,128]{3,2,0,1:T(8,128)S(1)} fusion(f32[2,1,65,128]{3,2,0,1:T(8,128)S(1)} %bitcast.24, f32[2,1,65,128]{3,2,0,1:T(8,128)} %bitcast.25), kind=kLoop, calls=%fused_computation.25 | loop fusion | flops 33280 | bytes 266240 | tf_op jit(solution)/shard_map/stack | solution.py:285
  17.7 0.1 copy.14
  17.8 0.0 copy-start.5
  17.8 0.0 copy-start.6
  17.8 1.6 %collective-permute-start.2 = (f32[4,65,128]{2,0,1:T(4,128)S(1)}, f32[4,65,128]{2,0,1:T(4,128)S(1)}, u32[]{:S(2)}, u32[]{:S(2)}) collective-permute-start(f32[4,65,128]{2,0,1:T(4,128)S(1)} %bitcast.21), channel_id=1, source_target_pairs={{0,4},{2,6},{4,0},{6,2},{8,12},{10,14},{12,8},{14,10},{16,20},{18,... | collective-permute-start | bytes 399368 | tf_op jit(solution)/shard_map/ppermute | solution.py:280
  19.3 0.1 exponential_multiply_fusion
  19.4 3.4 %collective-permute-done.2 = f32[4,65,128]{2,0,1:T(4,128)S(1)} collective-permute-done((f32[4,65,128]{2,0,1:T(4,128)S(1)}, f32[4,65,128]{2,0,1:T(4,128)S(1)}, u32[]{:S(2)}, u32[]{:S(2)}) %collective-permute-start.2) | collective-permute-done | bytes 133152 | tf_op jit(solution)/shard_map/ppermute | solution.py:280
  22.8 0.1 pad_maximum_fusion
  22.9 0.0 copy-start
  22.9 0.1 collective-permute-start.3
  23.0 1.7 %fusion.4.jt_ref = f32[30,64,64]{2,1,0:T(8,128)} fusion(f32[30]{0:T(128)S(1)} %copy-done.6, f32[64,64]{1,0:T(8,128)S(1)} %broadcast_subtract_fusion, f32[30,64]{1,0:T(8,128)S(1)} %exponential_multiply_fusion), kind=kLoop, calls=%fused_computation.14 | loop fusion | flops 1474560 | bytes 515704 | tf_op jit(solution)/shard_map/vmap()/mul | solution.py:31
  24.7 0.0 collective-permute-done.4.wo_ref
  24.7 0.0 collective-permute-done.3.gat1_ref
  24.7 0.0 copy-start.1
  24.7 0.5 %copy-done.9 = f32[1,128]{1,0:T(1,128)} copy-done((f32[1,128]{1,0:T(1,128)}, f32[1,128]{1,0:T(1,128)S(1)}, u32[]{:S(2)}) %copy-start.9) | copy-done | bytes 536
  25.2 0.2 copy-done.1
  25.4 10.7 %shard_map.132 = (f32[1,14]{1,0:T(1,128)}, f32[1,30]{1,0:T(1,128)}, f32[1,128]{1,0:T(1,128)}) custom-call(s32[30]{0:T(128)} %tpar_ref.1, s32[1]{0:T(128)} %bitcast.pick_ref, s32[14]{0:T(128)} %lpar_ref.1, f32[8,65,128]{2,1,0:T(8,128)} %bitcast.20, f32[8,65,128]{2,1,0:T(8,128)} %copy-done.1, f32[30,64,64]{2,1,0:T(8,128)} %get-tuple-element.17.tp_ref.tpt_ref, ...), custom_call_target="tpu_custom_call" | custom-call | tf_op jit(solution)/shard_map/pallas_call | solution.py:250
  36.2 0.6 %copy-done.11 = f32[1,14]{1,0:T(1,128)S(1)} copy-done((f32[1,14]{1,0:T(1,128)S(1)}, f32[1,14]{1,0:T(1,128)}, u32[]{:S(2)}) %copy-start.11) | copy-done | bytes 80
  36.8 0.0 copy-done.12
  36.8 5.4 %all-reduce = (f32[14]{0:T(128)}, f32[30]{0:T(128)}) all-reduce(f32[14]{0:T(128)S(1)} %bitcast.33, f32[30]{0:T(128)S(1)} %bitcast.34), channel_id=1, replica_groups=mesh['leaf'=16,'site'=2] {'site'}, use_global_device_ids=true, to_apply=%region_0.1 | all-reduce | flops 44 | bytes 352 | tf_op jit(solution)/shard_map/psum | solution.py:345
  (19 shorter events, 0.1 us)
Async XLA Ops:
  0.6 7.6 %copy-start.10 = (s32[128]{0:T(128)S(1)}, s32[128]{0:T(128)}, u32[]{:S(2)}) copy-start(s32[128]{0:T(128)} %param.16) | copy-start | bytes 1540
  0.6 9.2 %copy-start.4 = (f32[64]{0:T(128)S(1)}, f32[64]{0:T(128)}, u32[]{:S(2)}) copy-start(f32[64]{0:T(128)} %param.19) | copy-start | bytes 772
  4.1 6.7 %copy-start.3 = (f32[65,128]{1,0:T(8,128)S(1)}, f32[65,128]{1,0:T(8,128)}, u32[]{:S(2)}) copy-start(f32[65,128]{1,0:T(8,128)} %get-tuple-element.15) | copy-start | bytes 99844
  4.1 6.7 %collective-permute-start = (f32[1,65,128]{2,1,0:T(8,128)}, f32[1,65,128]{2,1,0:T(8,128)S(1)}, u32[]{:S(2)}, u32[]{:S(2)}) collective-permute-start(f32[1,65,128]{2,1,0:T(8,128)} %bitcast.26), channel_id=1, source_target_pairs={{0,16},{2,18},{4,20},{6,22},{8,24},{10,26},{12,28},{14,30},{16,0},... | collective-permute-start | bytes 99848 | tf_op jit(solution)/shard_map/ppermute | solution.py:280
  8.2 1.7 %copy-start.8 = (f32[1,128]{1,0:T(1,128)}, f32[1,128]{1,0:T(1,128)S(1)}, u32[]{:S(2)}) copy-start(f32[1,128]{1,0:T(1,128)S(1)} %convert_bitcast_fusion.w_ref) | copy-start | bytes 1540
  8.3 1.7 %copy-start.7 = (f32[14]{0:T(128)S(1)}, f32[14]{0:T(128)}, u32[]{:S(2)}) copy-start(f32[14]{0:T(128)} %len_ref.1) | copy-start | bytes 172
  8.3 16.4 %collective-permute-start.4 = (f32[1,128]{1,0:T(1,128)S(1)}, f32[1,128]{1,0:T(1,128)S(1)}, u32[]{:S(2)}, u32[]{:S(2)}) collective-permute-start(f32[1,128]{1,0:T(1,128)S(1)} %convert_bitcast_fusion.w_ref), channel_id=1, source_target_pairs={{0,1},{1,0},{2,3},{3,2},{4,5},{5,4},{6,7},{7,6},{8,9},{9,8},{10,11... | collective-permute-start | bytes 1544 | tf_op jit(solution)/shard_map/ppermute | solution.py:310
  10.8 2.7 %copy-start.2 = (f32[2,65,128]{2,1,0:T(8,128)}, f32[2,65,128]{2,1,0:T(8,128)S(1)}, u32[]{:S(2)}) copy-start(f32[2,65,128]{2,1,0:T(8,128)S(1)} %maximum_bitcast_fusion.carry_ref) | copy-start | bytes 199684
  10.8 6.0 %collective-permute-start.1 = (f32[2,65,128]{2,1,0:T(8,128)S(1)}, f32[2,65,128]{2,1,0:T(8,128)S(1)}, u32[]{:S(2)}, u32[]{:S(2)}) collective-permute-start(f32[2,65,128]{2,1,0:T(8,128)S(1)} %maximum_bitcast_fusion.carry_ref), channel_id=1, source_target_pairs={{0,8},{2,10},{4,12},{6,14},{8,0},{10,2},{12,4},{14,6},{16,24},{18,... | collective-permute-start | bytes 199688 | tf_op jit(solution)/shard_map/ppermute | solution.py:280
  17.8 1.6 %copy-start.5 = (f32[64]{0:T(128)S(1)}, f32[64]{0:T(128)}, u32[]{:S(2)}) copy-start(f32[64]{0:T(128)} %param.19) | copy-start | bytes 772
  17.8 1.6 %copy-start.6 = (f32[30]{0:T(128)S(1)}, f32[30]{0:T(128)}, u32[]{:S(2)}) copy-start(f32[30]{0:T(128)} %top_len_ref.1) | copy-start | bytes 364
  17.8 5.1 %collective-permute-start.2 = (f32[4,65,128]{2,0,1:T(4,128)S(1)}, f32[4,65,128]{2,0,1:T(4,128)S(1)}, u32[]{:S(2)}, u32[]{:S(2)}) collective-permute-start(f32[4,65,128]{2,0,1:T(4,128)S(1)} %bitcast.21), channel_id=1, source_target_pairs={{0,4},{2,6},{4,0},{6,2},{8,12},{10,14},{12,8},{14,10},{16,20},{18,... | collective-permute-start | bytes 399368 | tf_op jit(solution)/shard_map/ppermute | solution.py:280
  22.9 1.8 %copy-start = (f32[4,2,65,128]{3,2,1,0:T(8,128)}, f32[4,2,65,128]{3,2,1,0:T(8,128)S(1)}, u32[]{:S(2)}) copy-start(f32[4,2,65,128]{3,2,1,0:T(8,128)S(1)} %copy.16) | copy-start | bytes 798724
  22.9 1.8 %collective-permute-start.3 = (f32[8,65,128]{2,1,0:T(8,128)S(1)}, f32[8,65,128]{2,1,0:T(8,128)S(1)}, u32[]{:S(2)}, u32[]{:S(2)}) collective-permute-start(f32[8,65,128]{2,1,0:T(8,128)S(1)} %bitcast.19), channel_id=1, source_target_pairs={{0,2},{2,0},{4,6},{6,4},{8,10},{10,8},{12,14},{14,12},{16,18},{18,... | collective-permute-start | bytes 798728 | tf_op jit(solution)/shard_map/ppermute | solution.py:280
  24.7 0.5 %copy-start.9 = (f32[1,128]{1,0:T(1,128)}, f32[1,128]{1,0:T(1,128)S(1)}, u32[]{:S(2)}) copy-start(f32[1,128]{1,0:T(1,128)S(1)} %collective-permute-done.4.wo_ref) | copy-start | bytes 1540
  24.7 0.7 %copy-start.1 = (f32[8,65,128]{2,1,0:T(8,128)}, f32[8,65,128]{2,1,0:T(8,128)S(1)}, u32[]{:S(2)}) copy-start(f32[8,65,128]{2,1,0:T(8,128)S(1)} %collective-permute-done.3.gat1_ref) | copy-start | bytes 798724
  36.1 0.6 %copy-start.11 = (f32[1,14]{1,0:T(1,128)S(1)}, f32[1,14]{1,0:T(1,128)}, u32[]{:S(2)}) copy-start(f32[1,14]{1,0:T(1,128)} %get-tuple-element.22) | copy-start | bytes 172
  36.2 0.6 %copy-start.12 = (f32[1,30]{1,0:T(1,128)S(1)}, f32[1,30]{1,0:T(1,128)}, u32[]{:S(2)}) copy-start(f32[1,30]{1,0:T(1,128)} %get-tuple-element.23) | copy-start | bytes 364

commit v12 on v11

--- a/solution.py
+++ b/solution.py
@@ -280,7 +280,7 @@
         other = lax.ppermute(buf, "leaf", [(i, i ^ step) for i in range(groups)])
         if step == 1:
             return buf, other
-        if step == max(groups // 4, 1):
+        if step == max(groups // 8, 1):
             buf = hook(buf)
         buf = jnp.stack([buf, other], axis=1).reshape((-1,) + block.shape)
         step //= 2

time: 42.5 us -> 41.6 us (0.979)
  waiting for transfers between devices: 4.21 us -> 2.61 us
  local copies, waits for them, and re-layouts: 1.47 us -> 1.99 us
    ppermute x4, waiting for transfers between devices: 4.21 us -> 2.61 us  [gather_roots(): other = lax.ppermute(buf, 'leaf', [(i, i ^ step) for i in range(groups)])]
    unnamed x26, local copies, waits for them, and re-layouts: 1.38 us -> 1.96 us
    another operation x2 -> x3, other arithmetic: 0.96 us -> 0.96 us  [gather_roots(): buf = jnp.stack([buf, other], axis=1).reshape((-1,) + block.shape)]
  transfers between devices with their start and end apart: 5 -> 5, of which waited for: 2 -> 3; matrix products, arithmetic and copies ran while one was open for 10% -> 10% of each run, Pallas kernels for 8% -> 8%
where the time goes in v12:
time: 41.6 us; the launch traced here: 41.3 us
  Pallas kernels  17.5 us (42%)
  starting transfers between devices  9.11 us (22%)
  blocking collectives  5.41 us (13%)
  other arithmetic  4 us (10%)
  waiting for transfers between devices  2.61 us (6%)
  local copies, waits for them, and re-layouts  1.99 us (5%)
  between operations  0.76 us (2%)
    pallas_call x1, Pallas kernels, join(): pl.pallas_call(functools.partial(_join_kernel, taxon_count=taxon_count, p...  10.7 us
    ppermute x4, starting transfers between devices, gather_roots(): other = lax.ppermute(buf, 'leaf', [(i, i ^ step) for i in range(groups)])  7.52 us
    psum x1, blocking collectives, on_device(): local_sum, top_sum = lax.psum((local_row[0], top_row[0]), 'site')  5.41 us
    pallas_call x1, Pallas kernels, climb(): pl.pallas_call(_climb_kernel, out_shape=(jax.ShapeDtypeStruct((states + 1...  3.46 us
    pallas_call x1, Pallas kernels, matrices(): pl.pallas_call(_matrix_kernel, out_shape=(jax.ShapeDtypeStruct((local_edg...  3.26 us
    mul x4, other arithmetic, integrals(): return branch * jnp.exp(eig_values[None, :] * branch) * growth  2.97 us
    ppermute x4, waiting for transfers between devices, gather_roots(): other = lax.ppermute(buf, 'leaf', [(i, i ^ step) for i in range(groups)])  2.61 us
    unnamed x26, local copies, waits for them, and re-layouts  1.96 us
  transfers between devices with their start and end apart: 5, of which 3 were waited for; matrix products, arithmetic and copies ran while one was open for 10% of the time, Pallas kernels for 8%

profile of v12, /device:TPU:0, one launch (start us, length us, event | category | flops | bytes accessed | tf_op | source)
XLA Modules:
  0.0 41.3 jit_solution(8499763891339538989)
XLA Ops:
  0.6 0.0 copy-start.10
  0.6 0.0 copy-start.4
  0.7 3.5 %shard_map.130 = (f32[65,128]{1,0:T(8,128)}, f32[14,64,128]{2,1,0:T(8,128)}, f32[64,1792]{1,0:T(8,128)}, f32[14,64,64]{2,1,0:T(8,128)}) custom-call(s32[14]{0:T(128)} %lpar_ref.1, f32[14]{0:T(128)} %len_ref.1, f32[8,64,128]{2,1,0:T(8,128)} %leaf_ref.1, f32[64,64]{1,0:T(8,128)} %v_ref.5, f32[64,64]{1,0:T(8,128)} %vi_ref.5, f32[1,64]{1,0:T(1,128)} %bitcast.30), custom_call_target="tpu_custom_call" | custom-call | tf_op jit(solution)/shard_map/pallas_call | solution.py:75
  4.1 4.1 %collective-permute-start = (f32[1,65,128]{2,1,0:T(8,128)}, f32[1,65,128]{2,1,0:T(8,128)S(1)}, u32[]{:S(2)}, u32[]{:S(2)}) collective-permute-start(f32[1,65,128]{2,1,0:T(8,128)} %bitcast.27), channel_id=1, source_target_pairs={{0,16},{2,18},{4,20},{6,22},{8,24},{10,26},{12,28},{14,30},{16,0},... | collective-permute-start | bytes 99848 | tf_op jit(solution)/shard_map/ppermute | solution.py:280
  8.2 0.0 copy-done.10
  8.3 1.6 %collective-permute-start.4 = (f32[1,128]{1,0:T(1,128)S(1)}, f32[1,128]{1,0:T(1,128)S(1)}, u32[]{:S(2)}, u32[]{:S(2)}) collective-permute-start(f32[1,128]{1,0:T(1,128)S(1)} %convert_bitcast_fusion.w_ref), channel_id=1, source_target_pairs={{0,1},{1,0},{2,3},{3,2},{4,5},{5,4},{6,7},{7,6},{8,9},{9,8},{10,11... | collective-permute-start | bytes 1544 | tf_op jit(solution)/shard_map/ppermute | solution.py:310
  9.8 0.1 broadcast_subtract_fusion
  9.9 0.0 copy-done.8
  9.9 0.1 exponential_multiply_fusion.1
  10.0 0.8 %collective-permute-done = f32[1,65,128]{2,1,0:T(8,128)S(1)} collective-permute-done((f32[1,65,128]{2,1,0:T(8,128)}, f32[1,65,128]{2,1,0:T(8,128)S(1)}, u32[]{:S(2)}, u32[]{:S(2)}) %collective-permute-start) | collective-permute-done | bytes 33312 | tf_op jit(solution)/shard_map/ppermute | solution.py:280
  10.8 1.6 %collective-permute-start.1 = (f32[2,65,128]{2,1,0:T(8,128)S(1)}, f32[2,65,128]{2,1,0:T(8,128)S(1)}, u32[]{:S(2)}, u32[]{:S(2)}) collective-permute-start(f32[2,65,128]{2,1,0:T(8,128)S(1)} %get-tuple-element.28), channel_id=1, source_target_pairs={{0,8},{2,10},{4,12},{6,14},{8,0},{10,2},{12,4},{14,6},{16,24},{18,... | collective-permute-start | bytes 199688 | tf_op jit(solution)/shard_map/ppermute | solution.py:280
  12.4 1.1 %fusion.11.jl_ref = f32[14,64,64]{2,1,0:T(8,128)} fusion(f32[14]{0:T(128)S(1)} %copy-done.7, f32[64,64]{1,0:T(8,128)S(1)} %broadcast_subtract_fusion, f32[14,64]{1,0:T(8,128)S(1)} %exponential_multiply_fusion.1), kind=kLoop, calls=%fused_computation.21 | loop fusion | flops 688128 | bytes 249400 | tf_op jit(solution)/shard_map/vmap()/mul | solution.py:31
  13.5 1.7 %collective-permute-done.1 = f32[2,65,128]{2,1,0:T(8,128)S(1)} collective-permute-done((f32[2,65,128]{2,1,0:T(8,128)S(1)}, f32[2,65,128]{2,1,0:T(8,128)S(1)}, u32[]{:S(2)}, u32[]{:S(2)}) %collective-permute-start.1) | collective-permute-done | bytes 66592 | tf_op jit(solution)/shard_map/ppermute | solution.py:280
  15.3 0.0 copy-start.1
  15.3 0.0 copy-start.5
  15.3 1.8 %collective-permute-start.2 = (f32[4,65,128]{2,1,0:T(8,128)S(1)}, f32[4,65,128]{2,1,0:T(8,128)S(1)}, u32[]{:S(2)}, u32[]{:S(2)}) collective-permute-start(f32[4,65,128]{2,1,0:T(8,128)S(1)} %bitcast.22), channel_id=1, source_target_pairs={{0,4},{2,6},{4,0},{6,2},{8,12},{10,14},{12,8},{14,10},{16,20},{18,... | collective-permute-start | bytes 399368 | tf_op jit(solution)/shard_map/ppermute | solution.py:280
  17.0 0.1 exponential_multiply_fusion
  17.1 3.3 %shard_map.131 = (f32[14,64,128]{2,1,0:T(8,128)}, f32[30,64,64]{2,1,0:T(8,128)}, f32[64,64]{1,0:T(8,128)}, f32[4,65,128]{2,1,0:T(8,128)}) custom-call(f32[30]{0:T(128)} %top_len_ref.1, f32[64,64]{1,0:T(8,128)} %v_ref.5, f32[64,64]{1,0:T(8,128)} %vi_ref.5, f32[64,64]{1,0:T(8,128)} %lab_ref.1, f32[1,64]{1,0:T(1,128)} %bitcast.31, ...), custom_call_target="tpu_custom_call" | custom-call | tf_op jit(solution)/shard_map/pallas_call | solution.py:112
  20.4 0.1 collective-permute-done.2
  20.5 0.9 %pad_maximum_fusion = f32[4,2,65,128]{3,2,0,1:T(8,128)S(1)} fusion(f32[4,1,65,128]{3,2,0,1:T(8,128)S(1)} %bitcast.24, f32[4,1,65,128]{3,2,0,1:T(8,128)} %bitcast.25), kind=kLoop, calls=%fused_computation.24 | loop fusion | flops 66560 | bytes 532480 | tf_op jit(solution)/shard_map/stack | solution.py:285
  21.5 0.0 copy-start
  21.5 0.0 copy-start.6
  21.5 0.1 collective-permute-start.3
  21.6 0.6 %copy-done.6 = f32[30]{0:T(128)S(1)} copy-done((f32[30]{0:T(128)S(1)}, f32[30]{0:T(128)}, u32[]{:S(2)}) %copy-start.6) | copy-done | bytes 144
  22.2 1.7 %fusion.4.jt_ref = f32[30,64,64]{2,1,0:T(8,128)} fusion(f32[30]{0:T(128)S(1)} %copy-done.6, f32[64,64]{1,0:T(8,128)S(1)} %broadcast_subtract_fusion, f32[30,64]{1,0:T(8,128)S(1)} %exponential_multiply_fusion), kind=kLoop, calls=%fused_computation.14 | loop fusion | flops 1474560 | bytes 515704 | tf_op jit(solution)/shard_map/vmap()/mul | solution.py:31
  23.8 0.0 collective-permute-done.4.wo_ref
  23.8 0.0 collective-permute-done.3.gat1_ref
  23.9 0.5 %copy-done.9 = f32[1,128]{1,0:T(1,128)} copy-done((f32[1,128]{1,0:T(1,128)}, f32[1,128]{1,0:T(1,128)S(1)}, u32[]{:S(2)}) %copy-start.9) | copy-done | bytes 536
  24.4 0.2 copy-done.2
  24.6 10.7 %shard_map.132 = (f32[1,14]{1,0:T(1,128)}, f32[1,30]{1,0:T(1,128)}, f32[1,128]{1,0:T(1,128)}) custom-call(s32[30]{0:T(128)} %tpar_ref.1, s32[1]{0:T(128)} %bitcast.pick_ref, s32[14]{0:T(128)} %lpar_ref.1, f32[8,65,128]{2,1,0:T(8,128)} %bitcast.21, f32[8,65,128]{2,1,0:T(8,128)} %copy-done.2, f32[30,64,64]{2,1,0:T(8,128)} %get-tuple-element.17.tp_ref.tpt_ref, ...), custom_call_target="tpu_custom_call" | custom-call | tf_op jit(solution)/shard_map/pallas_call | solution.py:250
  35.3 0.6 %copy-done.11 = f32[1,14]{1,0:T(1,128)S(1)} copy-done((f32[1,14]{1,0:T(1,128)S(1)}, f32[1,14]{1,0:T(1,128)}, u32[]{:S(2)}) %copy-start.11) | copy-done | bytes 80
  35.9 5.4 %all-reduce = (f32[14]{0:T(128)}, f32[30]{0:T(128)}) all-reduce(f32[14]{0:T(128)S(1)} %bitcast.34, f32[30]{0:T(128)S(1)} %bitcast.35), channel_id=1, replica_groups=mesh['leaf'=16,'site'=2] {'site'}, use_global_device_ids=true, to_apply=%region_0.1 | all-reduce | flops 44 | bytes 352 | tf_op jit(solution)/shard_map/psum | solution.py:345
  (19 shorter events, 0.1 us)
Async XLA Ops:
  0.6 7.6 %copy-start.10 = (s32[128]{0:T(128)S(1)}, s32[128]{0:T(128)}, u32[]{:S(2)}) copy-start(s32[128]{0:T(128)} %param.16) | copy-start | bytes 1540
  0.6 9.2 %copy-start.4 = (f32[64]{0:T(128)S(1)}, f32[64]{0:T(128)}, u32[]{:S(2)}) copy-start(f32[64]{0:T(128)} %param.19) | copy-start | bytes 772
  4.1 6.7 %copy-start.3 = (f32[65,128]{1,0:T(8,128)S(1)}, f32[65,128]{1,0:T(8,128)}, u32[]{:S(2)}) copy-start(f32[65,128]{1,0:T(8,128)} %get-tuple-element.15) | copy-start | bytes 99844
  4.1 6.7 %collective-permute-start = (f32[1,65,128]{2,1,0:T(8,128)}, f32[1,65,128]{2,1,0:T(8,128)S(1)}, u32[]{:S(2)}, u32[]{:S(2)}) collective-permute-start(f32[1,65,128]{2,1,0:T(8,128)} %bitcast.27), channel_id=1, source_target_pairs={{0,16},{2,18},{4,20},{6,22},{8,24},{10,26},{12,28},{14,30},{16,0},... | collective-permute-start | bytes 99848 | tf_op jit(solution)/shard_map/ppermute | solution.py:280
  8.2 1.7 %copy-start.8 = (f32[1,128]{1,0:T(1,128)}, f32[1,128]{1,0:T(1,128)S(1)}, u32[]{:S(2)}) copy-start(f32[1,128]{1,0:T(1,128)S(1)} %convert_bitcast_fusion.w_ref) | copy-start | bytes 1540
  8.3 1.7 %copy-start.7 = (f32[14]{0:T(128)S(1)}, f32[14]{0:T(128)}, u32[]{:S(2)}) copy-start(f32[14]{0:T(128)} %len_ref.1) | copy-start | bytes 172
  8.3 15.6 %collective-permute-start.4 = (f32[1,128]{1,0:T(1,128)S(1)}, f32[1,128]{1,0:T(1,128)S(1)}, u32[]{:S(2)}, u32[]{:S(2)}) collective-permute-start(f32[1,128]{1,0:T(1,128)S(1)} %convert_bitcast_fusion.w_ref), channel_id=1, source_target_pairs={{0,1},{1,0},{2,3},{3,2},{4,5},{5,4},{6,7},{7,6},{8,9},{9,8},{10,11... | collective-permute-start | bytes 1544 | tf_op jit(solution)/shard_map/ppermute | solution.py:310
  10.8 4.4 %collective-permute-start.1 = (f32[2,65,128]{2,1,0:T(8,128)S(1)}, f32[2,65,128]{2,1,0:T(8,128)S(1)}, u32[]{:S(2)}, u32[]{:S(2)}) collective-permute-start(f32[2,65,128]{2,1,0:T(8,128)S(1)} %get-tuple-element.28), channel_id=1, source_target_pairs={{0,8},{2,10},{4,12},{6,14},{8,0},{10,2},{12,4},{14,6},{16,24},{18,... | collective-permute-start | bytes 199688 | tf_op jit(solution)/shard_map/ppermute | solution.py:280
  15.3 1.9 %copy-start.1 = (f32[2,2,65,128]{3,2,1,0:T(8,128)}, f32[2,2,65,128]{3,2,1,0:T(8,128)S(1)}, u32[]{:S(2)}) copy-start(f32[2,2,65,128]{3,2,1,0:T(8,128)S(1)} %copy.14) | copy-start | bytes 399364
  15.3 1.8 %copy-start.5 = (f32[30]{0:T(128)S(1)}, f32[30]{0:T(128)}, u32[]{:S(2)}) copy-start(f32[30]{0:T(128)} %top_len_ref.1) | copy-start | bytes 364
  15.3 5.2 %collective-permute-start.2 = (f32[4,65,128]{2,1,0:T(8,128)S(1)}, f32[4,65,128]{2,1,0:T(8,128)S(1)}, u32[]{:S(2)}, u32[]{:S(2)}) collective-permute-start(f32[4,65,128]{2,1,0:T(8,128)S(1)} %bitcast.22), channel_id=1, source_target_pairs={{0,4},{2,6},{4,0},{6,2},{8,12},{10,14},{12,8},{14,10},{16,20},{18,... | collective-permute-start | bytes 399368 | tf_op jit(solution)/shard_map/ppermute | solution.py:280
  21.5 2.4 %copy-start = (f32[4,2,65,128]{3,2,1,0:T(8,128)}, f32[4,2,65,128]{3,2,1,0:T(8,128)S(1)}, u32[]{:S(2)}) copy-start(f32[4,2,65,128]{3,2,1,0:T(8,128)S(1)} %copy.15) | copy-start | bytes 798724
  21.5 0.7 %copy-start.6 = (f32[30]{0:T(128)S(1)}, f32[30]{0:T(128)}, u32[]{:S(2)}) copy-start(f32[30]{0:T(128)} %top_len_ref.1) | copy-start | bytes 364
  21.5 2.4 %collective-permute-start.3 = (f32[8,65,128]{2,1,0:T(8,128)S(1)}, f32[8,65,128]{2,1,0:T(8,128)S(1)}, u32[]{:S(2)}, u32[]{:S(2)}) collective-permute-start(f32[8,65,128]{2,1,0:T(8,128)S(1)} %bitcast.20), channel_id=1, source_target_pairs={{0,2},{2,0},{4,6},{6,4},{8,10},{10,8},{12,14},{14,12},{16,18},{18,... | collective-permute-start | bytes 798728 | tf_op jit(solution)/shard_map/ppermute | solution.py:280
  23.8 0.5 %copy-start.9 = (f32[1,128]{1,0:T(1,128)}, f32[1,128]{1,0:T(1,128)S(1)}, u32[]{:S(2)}) copy-start(f32[1,128]{1,0:T(1,128)S(1)} %collective-permute-done.4.wo_ref) | copy-start | bytes 1540
  23.8 0.7 %copy-start.2 = (f32[8,65,128]{2,1,0:T(8,128)}, f32[8,65,128]{2,1,0:T(8,128)S(1)}, u32[]{:S(2)}) copy-start(f32[8,65,128]{2,1,0:T(8,128)S(1)} %collective-permute-done.3.gat1_ref) | copy-start | bytes 798724
  35.3 0.6 %copy-start.11 = (f32[1,14]{1,0:T(1,128)S(1)}, f32[1,14]{1,0:T(1,128)}, u32[]{:S(2)}) copy-start(f32[1,14]{1,0:T(1,128)} %get-tuple-element.22) | copy-start | bytes 172
  35.3 0.6 %copy-start.12 = (f32[1,30]{1,0:T(1,128)S(1)}, f32[1,30]{1,0:T(1,128)}, u32[]{:S(2)}) copy-start(f32[1,30]{1,0:T(1,128)} %get-tuple-element.23) | copy-start | bytes 364

commit v13 on v12

--- a/solution.py
+++ b/solution.py
@@ -104,8 +104,9 @@
         tp_ref[c] = _dot(vecs * jnp.exp(lam * top_len_ref[c]), inv)
 
 
-def matrices(top_lengths, vecs, inv, labeled, lam_row, j_local, xw, carry):
-    local_edges, states, _ = j_local.shape
+def matrices(top_lengths, vecs, inv, labeled, lam_row, j_all, xw, carry):
+    local_edges = j_all.shape[0] - top_lengths.shape[0]
+    states = j_all.shape[1]
     columns = xw.shape[1] // local_edges
     top_edges = top_lengths.shape[0]
     sq = (states, states)
@@ -121,7 +122,7 @@
         out_specs=(VMEM,) * 4,
         scratch_shapes=[pltpu.VMEM((states, local_edges * columns), F32)],
         compiler_params=PARAMS,
-    )(top_lengths, vecs, inv, labeled, lam_row, j_local, xw, carry)
+    )(top_lengths, vecs, inv, labeled, lam_row, j_all, xw, carry)
 
 
 def _lane_put(row, lane, value):
@@ -231,7 +232,7 @@
     row = jnp.zeros((1, lanes), F32)
     row = _counts(
         row, 0, w, vt, tarr_ref, tmsg_ref,
-        lambda c: _dot(basis * jt_ref[c], tvw_ref[:, _cols(c, columns)]),
+        lambda c: _dot(basis * jt_ref[local_edges + c], tvw_ref[:, _cols(c, columns)]),
     )
     top_ref[...] = row[:, 0:top_edges] / weight_total
     row = jnp.zeros((1, lanes), F32)
@@ -316,13 +317,14 @@
         parents, branch_lengths, tips, eig_vectors, eig_inverse, lam_row
     )
     paired = groups & (groups - 1) == 0
-    j_local = jax.vmap(lambda t: integrals(eig_values, t))(branch_lengths)
-    j_top = jax.vmap(lambda t: integrals(eig_values, t))(top_lengths)
+    j_all = jax.vmap(lambda t: integrals(eig_values, t))(
+        jnp.concatenate([branch_lengths, top_lengths])
+    )
     made = {}
 
     def hook(buf):
         made["m"] = matrices(
-            top_lengths, eig_vectors, eig_inverse, labeled_rates, lam_row, j_local, xw, buf
+            top_lengths, eig_vectors, eig_inverse, labeled_rates, lam_row, j_all, xw, buf
         )
         return made["m"][3]
 
@@ -339,7 +341,7 @@
     lmixed, tp, basis, _ = made["m"]
     lpt, tpt = trl, tp
     local_row, top_row, loglik = join(
-        top_parents, pick, parents, halves, tp, tpt, basis, j_top, eig_vectors, eig_inverse,
+        top_parents, pick, parents, halves, tp, tpt, basis, j_all, eig_vectors, eig_inverse,
         root_freq[None, :], w_row, w_other, msgs, lmixed, lpt, taxon_count, paired,
     )
     local_sum, top_sum = lax.psum((local_row[0], top_row[0]), "site")

time: 41.6 us -> 45.5 us (1.094)
  waiting for transfers between devices: 2.61 us -> 5.15 us
  other arithmetic: 4 us -> 6.13 us
  local copies, waits for them, and re-layouts: 1.99 us -> 0.74 us
    ppermute x1, waiting for transfers between devices: 0.01 us -> 2.05 us  [on_device(): w_other = lax.ppermute(w_row, 'site', [(0, 1), (1, 0)])]
    unnamed x26 -> x12, local copies, waits for them, and re-layouts: 1.96 us -> 0.71 us
    another operation x3, other arithmetic: 0.96 us -> 1.72 us  [gather_roots(): buf = jnp.stack([buf, other], axis=1).reshape((-1,) + block.shape)]
    concatenate x0 -> x1, other arithmetic: none -> 0.75 us  [on_device(): jnp.concatenate([branch_lengths, top_lengths])]
    sub x1, other arithmetic: 0.07 us -> 0.8 us  [integrals(): spread = (eig_values[:, None] - eig_values[None, :]) * branch]
    ppermute x4, waiting for transfers between devices: 2.61 us -> 3.1 us  [gather_roots(): other = lax.ppermute(buf, 'leaf', [(i, i ^ step) for i in range(groups)])]
    mul x4 -> x2, other arithmetic: 2.97 us -> 2.85 us  [integrals(): return branch * jnp.exp(eig_values[None, :] * branch) * growth]
where the time goes in v13:
time: 45.5 us; the launch traced here: 45.2 us
  Pallas kernels  17.9 us (39%)
  starting transfers between devices  9.07 us (20%)
  other arithmetic  6.13 us (13%)
  blocking collectives  5.43 us (12%)
  waiting for transfers between devices  5.15 us (11%)
  local copies, waits for them, and re-layouts  0.74 us (2%)
  between operations  0.73 us (2%)
    pallas_call x1, Pallas kernels, join(): pl.pallas_call(functools.partial(_join_kernel, taxon_count=taxon_count, p...  10.9 us
    ppermute x4, starting transfers between devices, gather_roots(): other = lax.ppermute(buf, 'leaf', [(i, i ^ step) for i in range(groups)])  7.48 us
    psum x1, blocking collectives, on_device(): local_sum, top_sum = lax.psum((local_row[0], top_row[0]), 'site')  5.43 us
    pallas_call x1, Pallas kernels, matrices(): pl.pallas_call(_matrix_kernel, out_shape=(jax.ShapeDtypeStruct((local_edg...  3.58 us
    pallas_call x1, Pallas kernels, climb(): pl.pallas_call(_climb_kernel, out_shape=(jax.ShapeDtypeStruct((states + 1...  3.42 us
    ppermute x4, waiting for transfers between devices, gather_roots(): other = lax.ppermute(buf, 'leaf', [(i, i ^ step) for i in range(groups)])  3.1 us
    mul x2, other arithmetic, integrals(): return branch * jnp.exp(eig_values[None, :] * branch) * growth  2.85 us
    ppermute x1, waiting for transfers between devices, on_device(): w_other = lax.ppermute(w_row, 'site', [(0, 1), (1, 0)])  2.05 us
  transfers between devices with their start and end apart: 5, of which 3 were waited for; matrix products, arithmetic and copies ran while one was open for 10% of the time, Pallas kernels for 8%

profile of v13, /device:TPU:0, one launch (start us, length us, event | category | flops | bytes accessed | tf_op | source)
XLA Modules:
  0.0 45.2 jit_solution(10236736174409109595)
XLA Ops:
  0.6 3.4 %shard_map.130 = (f32[65,128]{1,0:T(8,128)}, f32[14,64,128]{2,1,0:T(8,128)}, f32[64,1792]{1,0:T(8,128)}, f32[14,64,64]{2,1,0:T(8,128)}) custom-call(s32[14]{0:T(128)} %lpar_ref.1, f32[14]{0:T(128)} %len_ref.1, f32[8,64,128]{2,1,0:T(8,128)} %leaf_ref.1, f32[64,64]{1,0:T(8,128)} %v_ref.5, f32[64,64]{1,0:T(8,128)} %vi_ref.5, f32[1,64]{1,0:T(1,128)} %bitcast.30), custom_call_target="tpu_custom_call" | custom-call | tf_op jit(solution)/shard_map/pallas_call | solution.py:75
  4.0 4.1 %collective-permute-start = (f32[1,65,128]{2,1,0:T(8,128)}, f32[1,65,128]{2,1,0:T(8,128)S(1)}, u32[]{:S(2)}, u32[]{:S(2)}) collective-permute-start(f32[1,65,128]{2,1,0:T(8,128)} %bitcast.27), channel_id=1, source_target_pairs={{0,16},{2,18},{4,20},{6,22},{8,24},{10,26},{12,28},{14,30},{16,0},... | collective-permute-start | bytes 99848 | tf_op jit(solution)/shard_map/ppermute | solution.py:281
  8.1 0.8 %broadcast_subtract_fusion = f32[64,64]{1,0:T(8,128)S(1)} fusion(f32[64]{0:T(128)} %param.19), kind=kLoop, calls=%fused_computation.18 | loop fusion | flops 4096 | bytes 16640 | tf_op jit(solution)/shard_map/vmap()/sub | solution.py:25
  8.9 0.8 %pad_maximum_fusion.3 = f32[44]{0:T(128)S(1)} fusion(f32[30]{0:T(128)} %top_len_ref.1, f32[14]{0:T(128)} %len_ref.1), kind=kLoop, calls=%fused_computation.19 | loop fusion | flops 44 | bytes 352 | tf_op jit(solution)/shard_map/concatenate | solution.py:321
  9.7 1.0 %collective-permute-done = f32[1,65,128]{2,1,0:T(8,128)S(1)} collective-permute-done((f32[1,65,128]{2,1,0:T(8,128)}, f32[1,65,128]{2,1,0:T(8,128)S(1)}, u32[]{:S(2)}, u32[]{:S(2)}) %collective-permute-start) | collective-permute-done | bytes 33312 | tf_op jit(solution)/shard_map/ppermute | solution.py:281
  10.7 0.8 %fusion.8 = (f32[2,1,65,128]{3,2,0,1:T(8,128)S(1)}, f32[2,65,128]{2,1,0:T(8,128)S(1)}) fusion(f32[1,1,65,128]{3,2,1,0:T(8,128)S(1)} %bitcast.29, f32[1,1,65,128]{3,2,1,0:T(8,128)} %bitcast.28), kind=kLoop, calls=%fused_computation.16 | loop fusion | flops 16640 | bytes 199680 | tf_op jit(solution)/shard_map/stack;reshape | solution.py:286
  11.4 1.6 %collective-permute-start.1 = (f32[2,65,128]{2,1,0:T(8,128)S(1)}, f32[2,65,128]{2,1,0:T(8,128)S(1)}, u32[]{:S(2)}, u32[]{:S(2)}) collective-permute-start(f32[2,65,128]{2,1,0:T(8,128)S(1)} %get-tuple-element.28), channel_id=1, source_target_pairs={{0,8},{2,10},{4,12},{6,14},{8,0},{10,2},{12,4},{14,6},{16,24},{18,... | collective-permute-start | bytes 199688 | tf_op jit(solution)/shard_map/ppermute | solution.py:281
  13.0 0.7 %exponential_multiply_fusion = f32[44,64]{1,0:T(8,128)S(1)} fusion(f32[64]{0:T(128)} %param.19, f32[44]{0:T(128)S(1)} %pad_maximum_fusion.3), kind=kLoop, calls=%fused_computation.17 | loop fusion | flops 5632 | bytes 11696 | tf_op jit(solution)/shard_map/vmap()/mul | solution.py:31
  13.8 2.1 %collective-permute-done.1 = f32[2,65,128]{2,1,0:T(8,128)S(1)} collective-permute-done((f32[2,65,128]{2,1,0:T(8,128)S(1)}, f32[2,65,128]{2,1,0:T(8,128)S(1)}, u32[]{:S(2)}, u32[]{:S(2)}) %collective-permute-start.1) | collective-permute-done | bytes 66592 | tf_op jit(solution)/shard_map/ppermute | solution.py:281
  15.9 0.0 copy-start.1
  15.9 1.8 %collective-permute-start.2 = (f32[4,65,128]{2,1,0:T(8,128)S(1)}, f32[4,65,128]{2,1,0:T(8,128)S(1)}, u32[]{:S(2)}, u32[]{:S(2)}) collective-permute-start(f32[4,65,128]{2,1,0:T(8,128)S(1)} %bitcast.22), channel_id=1, source_target_pairs={{0,4},{2,6},{4,0},{6,2},{8,12},{10,14},{12,8},{14,10},{16,20},{18,... | collective-permute-start | bytes 399368 | tf_op jit(solution)/shard_map/ppermute | solution.py:281
  17.7 2.1 %fusion.4.jl_ref.jt_ref = f32[44,64,64]{2,1,0:T(8,128)} fusion(f32[44]{0:T(128)S(1)} %pad_maximum_fusion.3, f32[64,64]{1,0:T(8,128)S(1)} %broadcast_subtract_fusion, f32[44,64]{1,0:T(8,128)S(1)} %exponential_multiply_fusion), kind=kLoop, calls=%fused_computation.9 | loop fusion | flops 2162688 | bytes 748720 | tf_op jit(solution)/shard_map/vmap()/mul | solution.py:31
  19.8 0.0 copy-done.1
  19.8 0.0 copy-start.5
  19.8 3.6 %shard_map.131 = (f32[14,64,128]{2,1,0:T(8,128)}, f32[30,64,64]{2,1,0:T(8,128)}, f32[64,64]{1,0:T(8,128)}, f32[4,65,128]{2,1,0:T(8,128)}) custom-call(f32[30]{0:T(128)} %top_len_ref.1, f32[64,64]{1,0:T(8,128)} %v_ref.5, f32[64,64]{1,0:T(8,128)} %vi_ref.5, f32[64,64]{1,0:T(8,128)} %lab_ref.1, f32[1,64]{1,0:T(1,128)} %bitcast.31, ...), custom_call_target="tpu_custom_call" | custom-call | tf_op jit(solution)/shard_map/pallas_call | solution.py:113
  23.4 0.0 collective-permute-done.2
  23.4 0.9 %pad_maximum_fusion = f32[4,2,65,128]{3,2,0,1:T(8,128)S(1)} fusion(f32[4,1,65,128]{3,2,0,1:T(8,128)S(1)} %bitcast.24, f32[4,1,65,128]{3,2,0,1:T(8,128)} %bitcast.25), kind=kLoop, calls=%fused_computation.12 | loop fusion | flops 66560 | bytes 532480 | tf_op jit(solution)/shard_map/stack | solution.py:286
  24.3 0.0 copy-start
  24.4 0.1 collective-permute-start.3
  24.4 0.0 copy-done.5
  24.5 0.0 copy-start.3
  24.5 1.6 %collective-permute-start.4 = (f32[1,128]{1,0:T(1,128)S(1)}, f32[1,128]{1,0:T(1,128)S(1)}, u32[]{:S(2)}, u32[]{:S(2)}) collective-permute-start(f32[1,128]{1,0:T(1,128)S(1)} %convert_bitcast_fusion.w_ref), channel_id=1, source_target_pairs={{0,1},{1,0},{2,3},{3,2},{4,5},{5,4},{6,7},{7,6},{8,9},{9,8},{10,11... | collective-permute-start | bytes 1544 | tf_op jit(solution)/shard_map/ppermute | solution.py:311
  26.1 2.0 %collective-permute-done.4.wo_ref = f32[1,128]{1,0:T(1,128)S(1)} collective-permute-done((f32[1,128]{1,0:T(1,128)S(1)}, f32[1,128]{1,0:T(1,128)S(1)}, u32[]{:S(2)}, u32[]{:S(2)}) %collective-permute-start.4) | collective-permute-done | bytes 544 | tf_op jit(solution)/shard_map/ppermute | solution.py:311
  28.1 0.0 copy-start.4
  28.1 0.0 collective-permute-done.3.gat1_ref
  28.1 0.0 copy-start.2
  28.1 0.0 copy-done
  28.1 0.0 copy-done.3
  28.1 0.5 %copy-done.4 = f32[1,128]{1,0:T(1,128)} copy-done((f32[1,128]{1,0:T(1,128)}, f32[1,128]{1,0:T(1,128)S(1)}, u32[]{:S(2)}) %copy-start.4) | copy-done | bytes 536
  28.6 0.2 copy-done.2
  28.8 10.9 %shard_map.132 = (f32[1,14]{1,0:T(1,128)}, f32[1,30]{1,0:T(1,128)}, f32[1,128]{1,0:T(1,128)}) custom-call(s32[30]{0:T(128)} %tpar_ref.1, s32[1]{0:T(128)} %bitcast.pick_ref, s32[14]{0:T(128)} %lpar_ref.1, f32[8,65,128]{2,1,0:T(8,128)} %bitcast.21, f32[8,65,128]{2,1,0:T(8,128)} %copy-done.2, f32[30,64,64]{2,1,0:T(8,128)} %get-tuple-element.17.tp_ref.tpt_ref, ...), custom_call_target="tpu_custom_call" | custom-call | tf_op jit(solution)/shard_map/pallas_call | solution.py:251
  39.7 5.4 %all-reduce = (f32[14]{0:T(128)}, f32[30]{0:T(128)}) all-reduce(f32[14]{0:T(128)} %bitcast.34, f32[30]{0:T(128)} %bitcast.35), channel_id=1, replica_groups=mesh['leaf'=16,'site'=2] {'site'}, use_global_device_ids=true, to_apply=%region_0.1 | all-reduce | flops 44 | bytes 352 | tf_op jit(solution)/shard_map/psum | solution.py:347
  (4 shorter events, 0.0 us)
Async XLA Ops:
  4.0 6.6 %collective-permute-start = (f32[1,65,128]{2,1,0:T(8,128)}, f32[1,65,128]{2,1,0:T(8,128)S(1)}, u32[]{:S(2)}, u32[]{:S(2)}) collective-permute-start(f32[1,65,128]{2,1,0:T(8,128)} %bitcast.27), channel_id=1, source_target_pairs={{0,16},{2,18},{4,20},{6,22},{8,24},{10,26},{12,28},{14,30},{16,0},... | collective-permute-start | bytes 99848 | tf_op jit(solution)/shard_map/ppermute | solution.py:281
  11.4 4.4 %collective-permute-start.1 = (f32[2,65,128]{2,1,0:T(8,128)S(1)}, f32[2,65,128]{2,1,0:T(8,128)S(1)}, u32[]{:S(2)}, u32[]{:S(2)}) collective-permute-start(f32[2,65,128]{2,1,0:T(8,128)S(1)} %get-tuple-element.28), channel_id=1, source_target_pairs={{0,8},{2,10},{4,12},{6,14},{8,0},{10,2},{12,4},{14,6},{16,24},{18,... | collective-permute-start | bytes 199688 | tf_op jit(solution)/shard_map/ppermute | solution.py:281
  15.9 3.9 %copy-start.1 = (f32[2,2,65,128]{3,2,1,0:T(8,128)}, f32[2,2,65,128]{3,2,1,0:T(8,128)S(1)}, u32[]{:S(2)}) copy-start(f32[2,2,65,128]{3,2,1,0:T(8,128)S(1)} %copy.14) | copy-start | bytes 399364
  15.9 7.5 %collective-permute-start.2 = (f32[4,65,128]{2,1,0:T(8,128)S(1)}, f32[4,65,128]{2,1,0:T(8,128)S(1)}, u32[]{:S(2)}, u32[]{:S(2)}) collective-permute-start(f32[4,65,128]{2,1,0:T(8,128)S(1)} %bitcast.22), channel_id=1, source_target_pairs={{0,4},{2,6},{4,0},{6,2},{8,12},{10,14},{12,8},{14,10},{16,20},{18,... | collective-permute-start | bytes 399368 | tf_op jit(solution)/shard_map/ppermute | solution.py:281
  19.8 4.6 %copy-start.5 = (s32[128]{0:T(128)S(1)}, s32[128]{0:T(128)}, u32[]{:S(2)}) copy-start(s32[128]{0:T(128)} %param.16) | copy-start | bytes 1540
  24.3 3.8 %copy-start = (f32[4,2,65,128]{3,2,1,0:T(8,128)}, f32[4,2,65,128]{3,2,1,0:T(8,128)S(1)}, u32[]{:S(2)}) copy-start(f32[4,2,65,128]{3,2,1,0:T(8,128)S(1)} %copy.15) | copy-start | bytes 798724
  24.4 3.8 %collective-permute-start.3 = (f32[8,65,128]{2,1,0:T(8,128)S(1)}, f32[8,65,128]{2,1,0:T(8,128)S(1)}, u32[]{:S(2)}, u32[]{:S(2)}) collective-permute-start(f32[8,65,128]{2,1,0:T(8,128)S(1)} %bitcast.20), channel_id=1, source_target_pairs={{0,2},{2,0},{4,6},{6,4},{8,10},{10,8},{12,14},{14,12},{16,18},{18,... | collective-permute-start | bytes 798728 | tf_op jit(solution)/shard_map/ppermute | solution.py:281
  24.5 3.7 %copy-start.3 = (f32[1,128]{1,0:T(1,128)}, f32[1,128]{1,0:T(1,128)S(1)}, u32[]{:S(2)}) copy-start(f32[1,128]{1,0:T(1,128)S(1)} %convert_bitcast_fusion.w_ref) | copy-start | bytes 1540
  24.5 3.6 %collective-permute-start.4 = (f32[1,128]{1,0:T(1,128)S(1)}, f32[1,128]{1,0:T(1,128)S(1)}, u32[]{:S(2)}, u32[]{:S(2)}) collective-permute-start(f32[1,128]{1,0:T(1,128)S(1)} %convert_bitcast_fusion.w_ref), channel_id=1, source_target_pairs={{0,1},{1,0},{2,3},{3,2},{4,5},{5,4},{6,7},{7,6},{8,9},{9,8},{10,11... | collective-permute-start | bytes 1544 | tf_op jit(solution)/shard_map/ppermute | solution.py:311
  28.1 0.5 %copy-start.4 = (f32[1,128]{1,0:T(1,128)}, f32[1,128]{1,0:T(1,128)S(1)}, u32[]{:S(2)}) copy-start(f32[1,128]{1,0:T(1,128)S(1)} %collective-permute-done.4.wo_ref) | copy-start | bytes 1540
  28.1 0.7 %copy-start.2 = (f32[8,65,128]{2,1,0:T(8,128)}, f32[8,65,128]{2,1,0:T(8,128)S(1)}, u32[]{:S(2)}) copy-start(f32[8,65,128]{2,1,0:T(8,128)S(1)} %collective-permute-done.3.gat1_ref) | copy-start | bytes 798724

commit v14 on v12

--- a/solution.py
+++ b/solution.py
@@ -122,6 +122,21 @@
         scratch_shapes=[pltpu.VMEM((states, local_edges * columns), F32)],
         compiler_params=PARAMS,
     )(top_lengths, vecs, inv, labeled, lam_row, j_local, xw, carry)
+
+
+def _relay_kernel(a_ref, b_ref, a_out_ref, b_out_ref):
+    a_out_ref[...] = a_ref[...]
+    b_out_ref[...] = b_ref[...]
+
+
+def relay(a, b):
+    return pl.pallas_call(
+        _relay_kernel,
+        out_shape=(jax.ShapeDtypeStruct(a.shape, F32), jax.ShapeDtypeStruct(b.shape, F32)),
+        in_specs=[VMEM, VMEM],
+        out_specs=(VMEM, VMEM),
+        compiler_params=PARAMS,
+    )(a, b)
 
 
 def _lane_put(row, lane, value):
@@ -273,7 +288,7 @@
       w_other, lmsgs, lmixed, lpt)
 
 
-def gather_roots(block, groups, hook):
+def gather_roots(block, groups, hook, early_hook):
     buf = block[None]
     step = groups // 2
     while step >= 1:
@@ -282,6 +297,8 @@
             return buf, other
         if step == max(groups // 8, 1):
             buf = hook(buf)
+        elif step == groups // 4:
+            buf = early_hook(buf)
         buf = jnp.stack([buf, other], axis=1).reshape((-1,) + block.shape)
         step //= 2
     return buf, buf
@@ -326,8 +343,12 @@
         )
         return made["m"][3]
 
+    def early_hook(buf):
+        buf, made["j"] = relay(buf, j_top)
+        return buf
+
     if paired:
-        halves = gather_roots(root_block, groups, hook)
+        halves = gather_roots(root_block, groups, hook, early_hook)
         pick = jnp.reshape(member_index, (1,)).astype(jnp.int32)
     else:
         gathered = lax.all_gather(root_block, "leaf", axis=0, tiled=False)
@@ -337,6 +358,7 @@
     if "m" not in made:
         hook(root_block[None])
     lmixed, tp, basis, _ = made["m"]
+    j_top = made.get("j", j_top)
     lpt, tpt = trl, tp
     local_row, top_row, loglik = join(
         top_parents, pick, parents, halves, tp, tpt, basis, j_top, eig_vectors, eig_inverse,

time: 41.6 us -> 45.3 us (1.089)
  Pallas kernels: 17.5 us -> 19.7 us
  other arithmetic: 4 us -> 4.88 us
  waiting for transfers between devices: 2.61 us -> 3.23 us
    pallas_call x0 -> x1, Pallas kernels: none -> 2.27 us  [relay(): pl.pallas_call(_relay_kernel, out_shape=(jax.ShapeDtypeStruct(a.shape, F3...]
    ppermute x1, waiting for transfers between devices: 0.01 us -> 2.05 us  [on_device(): w_other = lax.ppermute(w_row, 'site', [(0, 1), (1, 0)])]
    ppermute x4, waiting for transfers between devices: 2.61 us -> 1.18 us  [gather_roots(): other = lax.ppermute(buf, 'leaf', [(i, i ^ step) for i in range(groups)])]
    another operation x3 -> x2, other arithmetic: 0.96 us -> 1.83 us  [gather_roots(): buf = jnp.stack([buf, other], axis=1).reshape((-1,) + block.shape)]
  transfers between devices with their start and end apart: 5 -> 5, of which waited for: 3 -> 3; matrix products, arithmetic and copies ran while one was open for 10% -> 7% of each run, Pallas kernels for 8% -> 12%
where the time goes in v14:
time: 45.3 us; the launch traced here: 45 us
  Pallas kernels  19.7 us (43%)
  starting transfers between devices  9.07 us (20%)
  blocking collectives  5.41 us (12%)
  other arithmetic  4.88 us (11%)
  waiting for transfers between devices  3.23 us (7%)
  local copies, waits for them, and re-layouts  1.94 us (4%)
  between operations  0.74 us (2%)
    pallas_call x1, Pallas kernels, join(): pl.pallas_call(functools.partial(_join_kernel, taxon_count=taxon_count, p...  10.7 us
    ppermute x4, starting transfers between devices, gather_roots(): other = lax.ppermute(buf, 'leaf', [(i, i ^ step) for i in range(groups)])  7.55 us
    psum x1, blocking collectives, on_device(): local_sum, top_sum = lax.psum((local_row[0], top_row[0]), 'site')  5.41 us
    pallas_call x1, Pallas kernels, climb(): pl.pallas_call(_climb_kernel, out_shape=(jax.ShapeDtypeStruct((states + 1...  3.44 us
    pallas_call x1, Pallas kernels, matrices(): pl.pallas_call(_matrix_kernel, out_shape=(jax.ShapeDtypeStruct((local_edg...  3.27 us
    mul x4, other arithmetic, integrals(): return branch * jnp.exp(eig_values[None, :] * branch) * growth  2.97 us
    pallas_call x1, Pallas kernels, relay(): pl.pallas_call(_relay_kernel, out_shape=(jax.ShapeDtypeStruct(a.shape, F3...  2.27 us
    ppermute x1, waiting for transfers between devices, on_device(): w_other = lax.ppermute(w_row, 'site', [(0, 1), (1, 0)])  2.05 us
  transfers between devices with their start and end apart: 5, of which 3 were waited for; matrix products, arithmetic and copies ran while one was open for 7% of the time, Pallas kernels for 12%

profile of v14, /device:TPU:0, one launch (start us, length us, event | category | flops | bytes accessed | tf_op | source)
XLA Modules:
  0.0 45.0 jit_solution(17214807650649066852)
XLA Ops:
  0.6 3.4 %shard_map.130 = (f32[65,128]{1,0:T(8,128)}, f32[14,64,128]{2,1,0:T(8,128)}, f32[64,1792]{1,0:T(8,128)}, f32[14,64,64]{2,1,0:T(8,128)}) custom-call(s32[14]{0:T(128)} %lpar_ref.1, f32[14]{0:T(128)} %len_ref.1, f32[8,64,128]{2,1,0:T(8,128)} %leaf_ref.1, f32[64,64]{1,0:T(8,128)} %v_ref.5, f32[64,64]{1,0:T(8,128)} %vi_ref.5, f32[1,64]{1,0:T(1,128)} %bitcast.30), custom_call_target="tpu_custom_call" | custom-call | tf_op jit(solution)/shard_map/pallas_call | solution.py:75
  4.1 4.1 %collective-permute-start = (f32[1,65,128]{2,1,0:T(8,128)}, f32[1,65,128]{2,1,0:T(8,128)S(1)}, u32[]{:S(2)}, u32[]{:S(2)}) collective-permute-start(f32[1,65,128]{2,1,0:T(8,128)} %bitcast.27), channel_id=1, source_target_pairs={{0,16},{2,18},{4,20},{6,22},{8,24},{10,26},{12,28},{14,30},{16,0},... | collective-permute-start | bytes 99848 | tf_op jit(solution)/shard_map/ppermute | solution.py:295
  8.2 0.1 broadcast_subtract_fusion
  8.3 0.0 copy-done.6
  8.3 0.1 exponential_multiply_fusion
  8.4 0.0 copy-start.4
  8.4 1.7 %fusion.4.b_ref = f32[30,64,64]{2,1,0:T(8,128)} fusion(f32[30]{0:T(128)S(1)} %copy-done.6, f32[64,64]{1,0:T(8,128)S(1)} %broadcast_subtract_fusion, f32[30,64]{1,0:T(8,128)S(1)} %exponential_multiply_fusion), kind=kLoop, calls=%fused_computation.14 | loop fusion | flops 1474560 | bytes 515704 | tf_op jit(solution)/shard_map/vmap()/mul | solution.py:31
  10.0 0.7 %collective-permute-done = f32[1,65,128]{2,1,0:T(8,128)S(1)} collective-permute-done((f32[1,65,128]{2,1,0:T(8,128)}, f32[1,65,128]{2,1,0:T(8,128)S(1)}, u32[]{:S(2)}, u32[]{:S(2)}) %collective-permute-start) | collective-permute-done | bytes 33312 | tf_op jit(solution)/shard_map/ppermute | solution.py:295
  10.7 0.0 copy-done.4
  10.8 1.6 %collective-permute-start.1 = (f32[2,65,128]{2,1,0:T(8,128)S(1)}, f32[2,65,128]{2,1,0:T(8,128)S(1)}, u32[]{:S(2)}, u32[]{:S(2)}) collective-permute-start(f32[2,65,128]{2,1,0:T(8,128)S(1)} %maximum_bitcast_fusion.a_ref), channel_id=1, source_target_pairs={{0,8},{2,10},{4,12},{6,14},{8,0},{10,2},{12,4},{14,6},{16,24},{18,... | collective-permute-start | bytes 199688 | tf_op jit(solution)/shard_map/ppermute | solution.py:295
  12.4 0.1 exponential_multiply_fusion.1
  12.4 2.3 %shard_map.131 = (f32[2,65,128]{2,1,0:T(8,128)}, f32[30,64,64]{2,1,0:T(8,128)}) custom-call(f32[2,65,128]{2,1,0:T(8,128)} %copy-done.3, f32[30,64,64]{2,1,0:T(8,128)} %fusion.4.b_ref), custom_call_target="tpu_custom_call" | custom-call | tf_op jit(solution)/shard_map/pallas_call | solution.py:133
  14.7 0.5 %collective-permute-done.1 = f32[2,65,128]{2,1,0:T(8,128)S(1)} collective-permute-done((f32[2,65,128]{2,1,0:T(8,128)S(1)}, f32[2,65,128]{2,1,0:T(8,128)S(1)}, u32[]{:S(2)}, u32[]{:S(2)}) %collective-permute-start.1) | collective-permute-done | bytes 66592 | tf_op jit(solution)/shard_map/ppermute | solution.py:295
  15.2 0.9 %pad_maximum_fusion.1 = f32[2,2,65,128]{3,2,0,1:T(8,128)S(1)} fusion(f32[2,1,65,128]{3,2,0,1:T(8,128)S(1)} %bitcast.25, f32[2,1,65,128]{3,2,0,1:T(8,128)} %bitcast.26), kind=kLoop, calls=%fused_computation.25 | loop fusion | flops 33280 | bytes 266240 | tf_op jit(solution)/shard_map/stack | solution.py:302
  16.1 1.8 %collective-permute-start.2 = (f32[4,65,128]{2,1,0:T(8,128)S(1)}, f32[4,65,128]{2,1,0:T(8,128)S(1)}, u32[]{:S(2)}, u32[]{:S(2)}) collective-permute-start(f32[4,65,128]{2,1,0:T(8,128)S(1)} %bitcast.21), channel_id=1, source_target_pairs={{0,4},{2,6},{4,0},{6,2},{8,12},{10,14},{12,8},{14,10},{16,20},{18,... | collective-permute-start | bytes 399368 | tf_op jit(solution)/shard_map/ppermute | solution.py:295
  17.9 1.1 %fusion.11.jl_ref = f32[14,64,64]{2,1,0:T(8,128)} fusion(f32[14]{0:T(128)S(1)} %copy-done.7, f32[64,64]{1,0:T(8,128)S(1)} %broadcast_subtract_fusion, f32[14,64]{1,0:T(8,128)S(1)} %exponential_multiply_fusion.1), kind=kLoop, calls=%fused_computation.21 | loop fusion | flops 688128 | bytes 249400 | tf_op jit(solution)/shard_map/vmap()/mul | solution.py:31
  19.0 3.3 %shard_map.132 = (f32[14,64,128]{2,1,0:T(8,128)}, f32[30,64,64]{2,1,0:T(8,128)}, f32[64,64]{1,0:T(8,128)}, f32[4,65,128]{2,1,0:T(8,128)}) custom-call(f32[30]{0:T(128)} %top_len_ref.1, f32[64,64]{1,0:T(8,128)} %v_ref.5, f32[64,64]{1,0:T(8,128)} %vi_ref.5, f32[64,64]{1,0:T(8,128)} %lab_ref.1, f32[1,64]{1,0:T(1,128)} %bitcast.31, ...), custom_call_target="tpu_custom_call" | custom-call | tf_op jit(solution)/shard_map/pallas_call | solution.py:112
  22.3 0.0 collective-permute-done.2
  22.3 0.9 %pad_maximum_fusion = f32[4,2,65,128]{3,2,0,1:T(8,128)S(1)} fusion(f32[4,1,65,128]{3,2,0,1:T(8,128)S(1)} %bitcast.23, f32[4,1,65,128]{3,2,0,1:T(8,128)} %bitcast.24), kind=kLoop, calls=%fused_computation.24 | loop fusion | flops 66560 | bytes 532480 | tf_op jit(solution)/shard_map/stack | solution.py:302
  23.3 0.0 copy-start.10
  23.3 0.1 collective-permute-start.3
  23.4 0.6 %copy-done.10 = s32[128]{0:T(128)S(1)} copy-done((s32[128]{0:T(128)S(1)}, s32[128]{0:T(128)}, u32[]{:S(2)}) %copy-start.10) | copy-done | bytes 536
  24.0 1.5 %collective-permute-start.4 = (f32[1,128]{1,0:T(1,128)S(1)}, f32[1,128]{1,0:T(1,128)S(1)}, u32[]{:S(2)}, u32[]{:S(2)}) collective-permute-start(f32[1,128]{1,0:T(1,128)S(1)} %convert_bitcast_fusion.w_ref), channel_id=1, source_target_pairs={{0,1},{1,0},{2,3},{3,2},{4,5},{5,4},{6,7},{7,6},{8,9},{9,8},{10,11... | collective-permute-start | bytes 1544 | tf_op jit(solution)/shard_map/ppermute | solution.py:327
  25.5 2.0 %collective-permute-done.4.wo_ref = f32[1,128]{1,0:T(1,128)S(1)} collective-permute-done((f32[1,128]{1,0:T(1,128)S(1)}, f32[1,128]{1,0:T(1,128)S(1)}, u32[]{:S(2)}, u32[]{:S(2)}) %collective-permute-start.4) | collective-permute-done | bytes 544 | tf_op jit(solution)/shard_map/ppermute | solution.py:327
  27.5 0.0 collective-permute-done.3.gat1_ref
  27.5 0.5 %copy-done.9 = f32[1,128]{1,0:T(1,128)} copy-done((f32[1,128]{1,0:T(1,128)}, f32[1,128]{1,0:T(1,128)S(1)}, u32[]{:S(2)}) %copy-start.9) | copy-done | bytes 536
  28.1 0.0 copy-done
  28.1 0.2 copy-done.2
  28.2 10.7 %shard_map.133 = (f32[1,14]{1,0:T(1,128)}, f32[1,30]{1,0:T(1,128)}, f32[1,128]{1,0:T(1,128)}) custom-call(s32[30]{0:T(128)} %tpar_ref.1, s32[1]{0:T(128)} %bitcast.pick_ref, s32[14]{0:T(128)} %lpar_ref.1, f32[8,65,128]{2,1,0:T(8,128)} %bitcast.20, f32[8,65,128]{2,1,0:T(8,128)} %copy-done.2, f32[30,64,64]{2,1,0:T(8,128)} %get-tuple-element.20.tp_ref.tpt_ref, ...), custom_call_target="tpu_custom_call" | custom-call | tf_op jit(solution)/shard_map/pallas_call | solution.py:265
  39.0 0.0 copy-start.12
  39.0 0.6 %copy-done.11 = f32[1,14]{1,0:T(1,128)S(1)} copy-done((f32[1,14]{1,0:T(1,128)S(1)}, f32[1,14]{1,0:T(1,128)}, u32[]{:S(2)}) %copy-start.11) | copy-done | bytes 80
  39.5 5.4 %all-reduce = (f32[14]{0:T(128)}, f32[30]{0:T(128)}) all-reduce(f32[14]{0:T(128)S(1)} %bitcast.34, f32[30]{0:T(128)S(1)} %bitcast.35), channel_id=1, replica_groups=mesh['leaf'=16,'site'=2] {'site'}, use_global_device_ids=true, to_apply=%region_0.1 | all-reduce | flops 44 | bytes 352 | tf_op jit(solution)/shard_map/psum | solution.py:367
  (20 shorter events, 0.1 us)
Async XLA Ops:
  4.1 4.1 %copy-start.5 = (f32[64]{0:T(128)S(1)}, f32[64]{0:T(128)}, u32[]{:S(2)}) copy-start(f32[64]{0:T(128)} %param.19) | copy-start | bytes 772
  4.1 4.2 %copy-start.6 = (f32[30]{0:T(128)S(1)}, f32[30]{0:T(128)}, u32[]{:S(2)}) copy-start(f32[30]{0:T(128)} %top_len_ref.1) | copy-start | bytes 364
  4.1 6.7 %collective-permute-start = (f32[1,65,128]{2,1,0:T(8,128)}, f32[1,65,128]{2,1,0:T(8,128)S(1)}, u32[]{:S(2)}, u32[]{:S(2)}) collective-permute-start(f32[1,65,128]{2,1,0:T(8,128)} %bitcast.27), channel_id=1, source_target_pairs={{0,16},{2,18},{4,20},{6,22},{8,24},{10,26},{12,28},{14,30},{16,0},... | collective-permute-start | bytes 99848 | tf_op jit(solution)/shard_map/ppermute | solution.py:295
  8.4 2.4 %copy-start.4 = (f32[65,128]{1,0:T(8,128)S(1)}, f32[65,128]{1,0:T(8,128)}, u32[]{:S(2)}) copy-start(f32[65,128]{1,0:T(8,128)} %get-tuple-element.17) | copy-start | bytes 99844
  10.7 1.6 %copy-start.7 = (f32[14]{0:T(128)S(1)}, f32[14]{0:T(128)}, u32[]{:S(2)}) copy-start(f32[14]{0:T(128)} %len_ref.1) | copy-start | bytes 172
  10.8 1.7 %copy-start.3 = (f32[2,65,128]{2,1,0:T(8,128)}, f32[2,65,128]{2,1,0:T(8,128)S(1)}, u32[]{:S(2)}) copy-start(f32[2,65,128]{2,1,0:T(8,128)S(1)} %maximum_bitcast_fusion.a_ref) | copy-start | bytes 199684
  10.8 4.4 %collective-permute-start.1 = (f32[2,65,128]{2,1,0:T(8,128)S(1)}, f32[2,65,128]{2,1,0:T(8,128)S(1)}, u32[]{:S(2)}, u32[]{:S(2)}) collective-permute-start(f32[2,65,128]{2,1,0:T(8,128)S(1)} %maximum_bitcast_fusion.a_ref), channel_id=1, source_target_pairs={{0,8},{2,10},{4,12},{6,14},{8,0},{10,2},{12,4},{14,6},{16,24},{18,... | collective-permute-start | bytes 199688 | tf_op jit(solution)/shard_map/ppermute | solution.py:295
  16.1 2.9 %copy-start.1 = (f32[2,2,65,128]{3,2,1,0:T(8,128)}, f32[2,2,65,128]{3,2,1,0:T(8,128)S(1)}, u32[]{:S(2)}) copy-start(f32[2,2,65,128]{3,2,1,0:T(8,128)S(1)} %copy.14) | copy-start | bytes 399364
  16.1 6.2 %collective-permute-start.2 = (f32[4,65,128]{2,1,0:T(8,128)S(1)}, f32[4,65,128]{2,1,0:T(8,128)S(1)}, u32[]{:S(2)}, u32[]{:S(2)}) collective-permute-start(f32[4,65,128]{2,1,0:T(8,128)S(1)} %bitcast.21), channel_id=1, source_target_pairs={{0,4},{2,6},{4,0},{6,2},{8,12},{10,14},{12,8},{14,10},{16,20},{18,... | collective-permute-start | bytes 399368 | tf_op jit(solution)/shard_map/ppermute | solution.py:295
  23.3 4.8 %copy-start = (f32[4,2,65,128]{3,2,1,0:T(8,128)}, f32[4,2,65,128]{3,2,1,0:T(8,128)S(1)}, u32[]{:S(2)}) copy-start(f32[4,2,65,128]{3,2,1,0:T(8,128)S(1)} %copy.15) | copy-start | bytes 798724
  23.3 0.7 %copy-start.10 = (s32[128]{0:T(128)S(1)}, s32[128]{0:T(128)}, u32[]{:S(2)}) copy-start(s32[128]{0:T(128)} %param.16) | copy-start | bytes 1540
  23.3 4.2 %collective-permute-start.3 = (f32[8,65,128]{2,1,0:T(8,128)S(1)}, f32[8,65,128]{2,1,0:T(8,128)S(1)}, u32[]{:S(2)}, u32[]{:S(2)}) collective-permute-start(f32[8,65,128]{2,1,0:T(8,128)S(1)} %bitcast.19), channel_id=1, source_target_pairs={{0,2},{2,0},{4,6},{6,4},{8,10},{10,8},{12,14},{14,12},{16,18},{18,... | collective-permute-start | bytes 798728 | tf_op jit(solution)/shard_map/ppermute | solution.py:295
  24.0 1.5 %copy-start.8 = (f32[1,128]{1,0:T(1,128)}, f32[1,128]{1,0:T(1,128)S(1)}, u32[]{:S(2)}) copy-start(f32[1,128]{1,0:T(1,128)S(1)} %convert_bitcast_fusion.w_ref) | copy-start | bytes 1540
  24.0 3.6 %collective-permute-start.4 = (f32[1,128]{1,0:T(1,128)S(1)}, f32[1,128]{1,0:T(1,128)S(1)}, u32[]{:S(2)}, u32[]{:S(2)}) collective-permute-start(f32[1,128]{1,0:T(1,128)S(1)} %convert_bitcast_fusion.w_ref), channel_id=1, source_target_pairs={{0,1},{1,0},{2,3},{3,2},{4,5},{5,4},{6,7},{7,6},{8,9},{9,8},{10,11... | collective-permute-start | bytes 1544 | tf_op jit(solution)/shard_map/ppermute | solution.py:327
  27.5 0.5 %copy-start.9 = (f32[1,128]{1,0:T(1,128)}, f32[1,128]{1,0:T(1,128)S(1)}, u32[]{:S(2)}) copy-start(f32[1,128]{1,0:T(1,128)S(1)} %collective-permute-done.4.wo_ref) | copy-start | bytes 1540
  27.5 0.7 %copy-start.2 = (f32[8,65,128]{2,1,0:T(8,128)}, f32[8,65,128]{2,1,0:T(8,128)S(1)}, u32[]{:S(2)}) copy-start(f32[8,65,128]{2,1,0:T(8,128)S(1)} %collective-permute-done.3.gat1_ref) | copy-start | bytes 798724
  39.0 0.6 %copy-start.11 = (f32[1,14]{1,0:T(1,128)S(1)}, f32[1,14]{1,0:T(1,128)}, u32[]{:S(2)}) copy-start(f32[1,14]{1,0:T(1,128)} %get-tuple-element.26) | copy-start | bytes 172
  39.0 0.6 %copy-start.12 = (f32[1,30]{1,0:T(1,128)S(1)}, f32[1,30]{1,0:T(1,128)}, u32[]{:S(2)}) copy-start(f32[1,30]{1,0:T(1,128)} %get-tuple-element.27) | copy-start | bytes 364
